TPU v7x, 128 devices: a whole 4x4x4 slice. The times are simulated.
128 devices in a mesh: req: 4 (over y), head: 8 (over z, x_hi), blk: 4 (over x_lo, core).
Axes of the slice: x: 4 (x_hi: 2, x_lo: 2; x = x_hi * 2 + x_lo), y: 4, z: 4, core: 2. Of those that a mesh axis runs over, the one named last changes fastest.
Arguments:
- image_hidden: bfloat16 [16, 32, 32, 1536], P('req', 'head', 'blk'), parts along dimension 0, may hold values from -6 to 6
- text_hidden: bfloat16 [16, 160, 1536], P('req', ('head', 'blk')), parts along dimension 0, may hold values from -6 to 6
- latent_grid: float32 [16, 64, 64, 16], P('req', 'head', 'blk'), parts along dimension 0, may hold values from -6 to 6
- text_lengths: int32 [16], P('req'), parts along dimension 0, may hold values from 38 to 154, as said below
- step_index: int32 [16], P('req'), parts along dimension 0, may hold values from 125 to 999
- image_mod: float32 [16, 6, 1536], P('req'), parts along dimension 0, may hold values from -3 to 3
- text_mod: float32 [16, 6, 1536], P('req'), parts along dimension 0, may hold values from -3 to 3
- final_mod: float32 [16, 2, 1536], P('req'), parts along dimension 0, may hold values from -3 to 3
- image_qk_gain: float32 [2, 64], replicated, may hold values from 0.5 to 2.3
- text_qk_gain: float32 [2, 64], replicated, may hold values from 0.5 to 2.3
- image_qkv: bfloat16 [1536, 3, 1536], P(None, None, 'head'), may hold values from -0.15625 to 0.15625
- text_qkv: bfloat16 [1536, 3, 1536], P(None, None, 'head'), may hold values from -0.15625 to 0.15625
- image_proj: bfloat16 [1536, 1536], P('head'), may hold values from -0.15625 to 0.15625
- text_proj: bfloat16 [1536, 1536], P('head'), may hold values from -0.15625 to 0.15625
- image_up: bfloat16 [1536, 6144], P(None, 'head'), may hold values from -0.15625 to 0.15625
- text_up: bfloat16 [1536, 6144], P(None, 'head'), may hold values from -0.15625 to 0.15625
- image_down: bfloat16 [6144, 1536], P('head'), may hold values from -0.078125 to 0.078125
- text_down: bfloat16 [6144, 1536], P('head'), may hold values from -0.078125 to 0.078125
- final_proj: bfloat16 [1536, 64], replicated, may hold values from -0.15625 to 0.15625
- conv_kernel: bfloat16 [3, 3, 16, 512], replicated, may hold values from -0.5 to 0.5
Outputs:
- image_states: bfloat16 [16, 32, 32, 1536], P('req', 'head', 'blk'), parts along dimension 0
- text_states: bfloat16 [16, 160, 1536], P('req', ('head', 'blk')), parts along dimension 0
- latent_next: float32 [16, 64, 64, 16], P('req', 'head', 'blk'), parts along dimension 0
- features: bfloat16 [16, 64, 64, 512], P('req', 'head', 'blk'), parts along dimension 0
There are 4 independent parts, one for each index of `req`. A program takes and returns all parts, laid end to end along the dimension named above; an argument that names none is the same for every part. Nothing has to cross between parts.
Inputs may be any that keep to these rules, and one draw needn't show every extreme that they name: `text_lengths`: every request has 154 or fewer live text tokens, and in each group one request has exactly 154.
All inputs are finite; a program needn't handle non-finite values.
Results may differ from a plain program's by a relative error of at most 0.012.
Values may be sent and summed in bfloat16 or wider, within the bound.
No kernel may reach another device: no remote copies, remote signals or barrier semaphores. Data moves between devices by JAX's collectives and lax.ppermute only.
A program may use at most 128 MiB of HBM per device.

v0:
```python
import math

import jax
import jax.numpy as jnp
from jax import lax
from jax.sharding import PartitionSpec as P

HD = 64


def extended(block, sides, width):
    for axis, dim in sides:
        count = lax.axis_size(axis)
        forward = [(i, i + 1) for i in range(count - 1)]
        backward = [(target, source) for source, target in forward]
        low = lax.ppermute(
            lax.slice_in_dim(block, block.shape[dim] - width, None, axis=dim), axis, forward
        )
        high = lax.ppermute(lax.slice_in_dim(block, 0, width, axis=dim), axis, backward)
        block = jnp.concatenate([low, block, high], axis=dim)
    return block


def gather_slots(block, axis):
    count = lax.axis_size(axis)
    parts = [block]
    for shift in range(1, count):
        parts.append(lax.ppermute(block, axis, [(i, (i + shift) % count) for i in range(count)]))
    return jnp.stack(parts)


def scatter_slots(partial, axis):
    count = lax.axis_size(axis)
    total = partial[0].astype(jnp.float32)
    for shift in range(1, count):
        total = total + lax.ppermute(
            partial[shift], axis, [((i + shift) % count, i) for i in range(count)]
        ).astype(jnp.float32)
    return total


def per_request(vector, values, axis):
    shape = [1] * values.ndim
    shape[axis] = vector.shape[0]
    shape[-1] = vector.shape[-1]
    return vector.reshape(shape)


def modulate(values, shift, scale, axis):
    average = jnp.mean(values, -1, keepdims=True)
    centred = values - average
    spread = jnp.mean(centred * centred, -1, keepdims=True)
    normed = centred * lax.rsqrt(spread + 1e-06)
    return normed * (1.0 + per_request(scale, values, axis)) + per_request(shift, values, axis)


def head_norm(values, gain):
    width = values.shape[-1]
    lane_head = jnp.arange(width) // HD
    spread = (lane_head[:, None] == lane_head[None, :]).astype(jnp.float32) / HD
    mean_square = jnp.dot(values * values, spread, precision=lax.Precision.HIGHEST)
    return (values * lax.rsqrt(mean_square + 1e-06) * jnp.tile(gain, width // HD)).astype(jnp.bfloat16)


def noise_level(fraction):
    return 3.0 * fraction / (1.0 + 2.0 * fraction)


def attention_inputs(normed, weight, gains):
    model_width, _, local_width = weight.shape
    heads = local_width // HD
    split = weight.reshape(model_width, 3, heads, HD)
    query_weight = jnp.concatenate([split[:, 0], jnp.zeros_like(split[:, 0])], -1).reshape(
        model_width, 2 * local_width
    )
    pair_weight = jnp.concatenate([split[:, 1], split[:, 2]], -1).reshape(model_width, 2 * local_width)
    lane = jnp.arange(2 * local_width)
    live = (lane % (2 * HD)) < HD
    lane_head = lane // (2 * HD)
    spread = ((lane_head[:, None] == lane_head[None, :]) & live[:, None]).astype(jnp.float32) / HD
    query_gain = jnp.where(live, jnp.tile(jnp.concatenate([gains[0], gains[0]]), heads), 0.0)
    key_gain = jnp.tile(jnp.concatenate([gains[1], gains[1]]), heads)

    def normalized(values, gain):
        mean_square = jnp.dot(values * values, spread, precision=lax.Precision.HIGHEST)
        return values * lax.rsqrt(mean_square + 1e-06) * gain

    query_proj = jnp.einsum("arnd,de->arne", normed, query_weight, preferred_element_type=jnp.float32)
    pair_proj = jnp.einsum("arnd,de->arne", normed, pair_weight, preferred_element_type=jnp.float32)
    queries = normalized(query_proj, query_gain).astype(jnp.bfloat16)
    pairs = jnp.where(live, normalized(pair_proj, key_gain), pair_proj).astype(jnp.bfloat16)
    return queries, pairs


def convolve(padded, kernel):
    out_rows = padded.shape[1] - 2
    out_cols = padded.shape[2] - 2
    summed = jnp.zeros((padded.shape[0], out_rows, out_cols, kernel.shape[-1]), jnp.float32)
    for row_off in range(3):
        for col_off in range(3):
            summed = summed + jnp.einsum(
                "rhwc,co->rhwo",
                padded[:, row_off : row_off + out_rows, col_off : col_off + out_cols],
                kernel[row_off, col_off],
                preferred_element_type=jnp.float32,
            )
    return summed.astype(jnp.bfloat16)


def body(
    image_hidden,
    text_hidden,
    latent_grid,
    text_lengths,
    step_index,
    image_mod,
    text_mod,
    final_mod,
    image_qk_gain,
    text_qk_gain,
    image_qkv,
    text_qkv,
    image_proj,
    text_proj,
    image_up,
    text_up,
    image_down,
    text_down,
    final_proj,
    conv_kernel,
):
    blocks = lax.axis_size("blk")
    groups = lax.axis_size("head")
    requests, tile_rows, tile_cols, model_width = image_hidden.shape
    text_slice = text_hidden.shape[1]
    image_tile = tile_rows * tile_cols
    tile_tokens = image_tile + text_slice
    own = jnp.concatenate(
        [image_hidden.reshape(requests, image_tile, model_width), text_hidden], axis=1
    )
    strip = gather_slots(own, "head")
    strip_f = strip.astype(jnp.float32)
    image_x = strip_f[:, :, :image_tile]
    text_x = strip_f[:, :, image_tile:]
    image_norm = modulate(image_x, image_mod[:, 0], image_mod[:, 1], 1).astype(jnp.bfloat16)
    text_norm = modulate(text_x, text_mod[:, 0], text_mod[:, 1], 1).astype(jnp.bfloat16)
    image_q, image_kv = attention_inputs(image_norm, image_qkv, image_qk_gain)
    text_q, text_kv = attention_inputs(text_norm, text_qkv, text_qk_gain)
    queries = jnp.concatenate([image_q, text_q], 2)
    key_value = jnp.concatenate([image_kv, text_kv], 2)
    tile = 2 * HD
    local_heads = queries.shape[-1] // tile
    local_width = local_heads * HD
    score_scale = 1.0 / math.sqrt(HD)
    kv = gather_slots(key_value.reshape(-1, local_heads * tile), "blk")
    span = blocks * groups * tile_tokens
    key_piece = (
        kv.reshape(blocks, groups, requests, tile_tokens, local_heads, tile)
        .transpose(2, 4, 0, 1, 3, 5)
        .reshape(requests, local_heads, span, tile)
    )
    query_rows = groups * tile_tokens
    query_piece = (
        queries.reshape(groups, requests, tile_tokens, local_heads, tile)
        .transpose(1, 3, 0, 2, 4)
        .reshape(requests, local_heads, query_rows, tile)
    )
    position = jnp.arange(span, dtype=jnp.int32)
    source = (lax.axis_index("blk") - position // (groups * tile_tokens)) % blocks
    group = (lax.axis_index("head") - (position // tile_tokens) % groups) % groups
    within = position % tile_tokens
    slot_ids = (group * blocks + source) * text_slice + (within - image_tile)
    usable = (within < image_tile)[None, :] | (slot_ids[None, :] < text_lengths[:, None])
    scores = (
        jnp.einsum("rhqe,rhke->rhqk", query_piece, key_piece, preferred_element_type=jnp.float32)
        * score_scale
    )
    weights = jnp.exp(scores) * usable[:, None, None, :].astype(jnp.float32)
    denominator = jnp.sum(weights, -1)
    numerator = jnp.einsum(
        "rhqk,rhke->rhqe",
        weights.astype(jnp.bfloat16),
        key_piece,
        preferred_element_type=jnp.float32,
    )[..., HD:]
    context = (numerator / denominator[..., None]).astype(jnp.bfloat16)
    context = (
        context.reshape(requests, local_heads, groups, tile_tokens, HD)
        .transpose(2, 0, 3, 1, 4)
        .reshape(groups, requests, tile_tokens, local_width)
    )
    image_part = jnp.einsum(
        "arne,ed->arnd", context[:, :, :image_tile], image_proj, preferred_element_type=jnp.float32
    )
    text_part = jnp.einsum(
        "arne,ed->arnd", context[:, :, image_tile:], text_proj, preferred_element_type=jnp.float32
    )
    attn = scatter_slots(jnp.concatenate([image_part, text_part], 2).astype(jnp.bfloat16), "head")
    own_f = own.astype(jnp.float32)
    image_mid = own_f[:, :image_tile] + per_request(image_mod[:, 2], own_f, 0) * attn[:, :image_tile]
    text_mid = own_f[:, image_tile:] + per_request(text_mod[:, 2], own_f, 0) * attn[:, image_tile:]
    image_local = modulate(image_mid, image_mod[:, 3], image_mod[:, 4], 0).astype(jnp.bfloat16)
    text_local = modulate(text_mid, text_mod[:, 3], text_mod[:, 4], 0).astype(jnp.bfloat16)
    ff_in = gather_slots(jnp.concatenate([image_local, text_local], 1), "head")
    image_hid = jax.nn.gelu(
        jnp.einsum("arnd,df->arnf", ff_in[:, :, :image_tile], image_up, preferred_element_type=jnp.float32),
        approximate=True,
    ).astype(jnp.bfloat16)
    text_hid = jax.nn.gelu(
        jnp.einsum("arnd,df->arnf", ff_in[:, :, image_tile:], text_up, preferred_element_type=jnp.float32),
        approximate=True,
    ).astype(jnp.bfloat16)
    image_back = jnp.einsum("arnf,fd->arnd", image_hid, image_down, preferred_element_type=jnp.float32)
    text_back = jnp.einsum("arnf,fd->arnd", text_hid, text_down, preferred_element_type=jnp.float32)
    mlp = scatter_slots(jnp.concatenate([image_back, text_back], 2).astype(jnp.bfloat16), "head")
    image_out = image_mid + per_request(image_mod[:, 5], image_mid, 0) * mlp[:, :image_tile]
    text_out = text_mid + per_request(text_mod[:, 5], text_mid, 0) * mlp[:, image_tile:]
    image_states = image_out.reshape(requests, tile_rows, tile_cols, model_width).astype(jnp.bfloat16)
    text_states = text_out.astype(jnp.bfloat16)
    final_in = modulate(image_out, final_mod[:, 1], final_mod[:, 0], 0).astype(jnp.bfloat16)
    velocity = jnp.einsum("rnd,dp->rnp", final_in, final_proj, preferred_element_type=jnp.float32)
    channels = velocity.shape[-1] // 4
    velocity = (
        velocity.reshape(requests, tile_rows, tile_cols, 2, 2, channels)
        .transpose(0, 1, 3, 2, 4, 5)
        .reshape(requests, 2 * tile_rows, 2 * tile_cols, channels)
    )
    current = step_index.astype(jnp.float32) / 1000.0
    following = jnp.maximum(step_index - 125, 0).astype(jnp.float32) / 1000.0
    step_size = noise_level(following) - noise_level(current)
    latent_next = latent_grid + step_size[:, None, None, None] * velocity
    decoded_in = (latent_next / 1.5305 + 0.0609).astype(jnp.bfloat16)
    padded = extended(decoded_in, (("head", 1), ("blk", 2)), 1)
    features = convolve(padded, conv_kernel)
    return (image_states, text_states, latent_next, features)


def solution(mesh):
    in_specs = (
        P("req", "head", "blk", None),
        P("req", ("head", "blk"), None),
        P("req", "head", "blk", None),
        P("req"),
        P("req"),
        P("req", None, None),
        P("req", None, None),
        P("req", None, None),
        P(),
        P(),
        P(None, None, "head"),
        P(None, None, "head"),
        P("head", None),
        P("head", None),
        P(None, "head"),
        P(None, "head"),
        P("head", None),
        P("head", None),
        P(),
        P(),
    )
    out_specs = (
        P("req", "head", "blk", None),
        P("req", ("head", "blk"), None),
        P("req", "head", "blk", None),
        P("req", "head", "blk", None),
    )
    return jax.shard_map(body, mesh=mesh, in_specs=in_specs, out_specs=out_specs, check_vma=False)
```

profile of v0, /device:TPU:1, one launch (start us, length us, event | category | flops | bytes accessed | tf_op | source)
XLA Modules:
  0.0 373.0 jit_solution(10855120140492779700)
XLA Ops:
  4.2 3.6 collective-permute-start
  12.9 5.2 %collective-permute-start.4 = (bf16[4,37,1536]{2,1,0:T(8,128)(2,1)}, bf16[4,37,1536]{2,1,0:T(8,128)(2,1)}, u32[]{:S(2)}, u32[]{:S(2)}) collective-permute-start(bf16[4,37,1536]{2,1,0:T(8,128)(2,1)} %get-tuple-element.47), channel_id=1, source_target_pairs={{0,20},{4,24},{8,28},{12,0},{16,4},{20,8},{24,12},{28,16},{1,21},{... | collective-permute-start | bytes 1363976 | tf_op jit(solution)/shard_map/ppermute | solution.py:28
  32.8 11.5 %collective-permute-done.1 = bf16[4,37,1536]{2,1,0:T(8,128)(2,1)} collective-permute-done((bf16[4,37,1536]{2,1,0:T(8,128)(2,1)}, bf16[4,37,1536]{2,1,0:T(8,128)(2,1)}, u32[]{:S(2)}, u32[]{:S(2)}) %collective-permute-start.1) | collective-permute-done | bytes 454688 | tf_op jit(solution)/shard_map/ppermute | solution.py:28
  46.6 9.3 %collective-permute-done.3 = bf16[4,37,1536]{2,1,0:T(8,128)(2,1)} collective-permute-done((bf16[4,37,1536]{2,1,0:T(8,128)(2,1)}, bf16[4,37,1536]{2,1,0:T(8,128)(2,1)}, u32[]{:S(2)}, u32[]{:S(2)}) %collective-permute-start.3) | collective-permute-done | bytes 454688 | tf_op jit(solution)/shard_map/ppermute | solution.py:28
  77.4 4.4 %fusion.233 = f32[8,4,32,384]{3,2,1,0:T(8,128)S(1)} fusion(bf16[1536,384,1,1]{0,1,3,2:T(8,128)(2,1)S(1)} %bitcast.294, f32[8,4,37,1536]{3,2,1,0:T(8,128)} %copy-done.1, f32[4,1536]{1,0:T(4,128)S(1)} %copy-done.26, f32[4,1536]{1,0:T(4,128)S(1)} %bitcast.303, f32[8,4,32]{2,1,0:T(4,128)S(1)} %add_rsqrt_fusion.1, f32[8,4,32]{2,1,0:T(4,128)S(1)} %broadcast_multiply_fusion.1), kind=kOutput, calls=%fused_computation.382 | convolution fusion | flops 1215823872 | bytes 9101312 | tf_op jit(solution)/shard_map/arnd,de->arne/dot_general | solution.py:88
  86.8 4.4 %collective-permute-done.7 = bf16[1184,384]{1,0:T(8,128)(2,1)} collective-permute-done((bf16[1184,384]{1,0:T(8,128)(2,1)}, bf16[1184,384]{1,0:T(8,128)(2,1)}, u32[]{:S(2)}, u32[]{:S(2)}) %collective-permute-start.7) | collective-permute-done | bytes 909344 | tf_op jit(solution)/shard_map/ppermute | solution.py:28
  97.2 15.0 %collective-permute-done.8 = bf16[1184,384]{1,0:T(8,128)(2,1)} collective-permute-done((bf16[1184,384]{1,0:T(8,128)(2,1)}, bf16[1184,384]{1,0:T(8,128)(2,1)}, u32[]{:S(2)}, u32[]{:S(2)}) %collective-permute-start.8) | collective-permute-done | bytes 909344 | tf_op jit(solution)/shard_map/ppermute | solution.py:28
  112.2 3.5 stack.79
  118.3 3.5 stack.80
  127.7 8.7 %fusion = (f32[4,3,296]{2,1,0:T(4,128)S(1)}, f32[4,3,296,1184]{3,2,1,0:T(8,128)}) fusion(f32[4,1184]{1,0:T(4,128)S(1)} %or_convert_fusion, bf16[4,3,1184,128]{3,0,2,1:T(4,128)(2,1)S(1)} %bitcast.285, bf16[4,3,296,128]{3,0,2,1:T(4,128)(2,1)S(1)} %bitcast.289), kind=kOutput, calls=%fused_computation.2 | convolution fusion | flops 1089238528 | bytes 21401984 | tf_op jit(solution)/shard_map/rhqe,rhke->rhqk/dot_general | solution.py:175
  136.4 9.4 %divide_convert_fusion = bf16[4,3,296,64]{2,3,1,0:T(8,128)(2,1)} fusion(bf16[4,3,1184,128]{3,2,1,0:T(8,128)(2,1)S(1)} %copy.107, f32[4,3,296,1184]{3,2,1,0:T(8,128)} %get-tuple-element.77, f32[4,1184]{1,0:T(4,128)S(1)} %or_convert_fusion, f32[4,3,296]{2,1,0:T(4,128)S(1)} %get-tuple-element.76), kind=kOutput, calls=%fused_computation.81 | convolution fusion | flops 547178496 | bytes 20947328 | tf_op jit(solution)/shard_map/rhqk,rhke->rhqe/dot_general | solution.py:180
  155.5 7.1 %collective-permute-start.10 = (bf16[4,37,1536]{2,1,0:T(8,128)(2,1)S(1)}, bf16[4,37,1536]{2,1,0:T(8,128)(2,1)S(1)}, u32[]{:S(2)}, u32[]{:S(2)}) collective-permute-start(bf16[4,37,1536]{2,1,0:T(8,128)(2,1)S(1)} %get-tuple-element.31), channel_id=1, source_target_pairs={{4,0},{8,4},{12,8},{16,12},{20,16},{24,20},{28,24},{0,28},{5,1},{9... | collective-permute-start | bytes 1363976 | tf_op jit(solution)/shard_map/ppermute | solution.py:36
  162.6 4.1 %collective-permute-start.11 = (bf16[4,37,1536]{2,1,0:T(8,128)(2,1)S(1)}, bf16[4,37,1536]{2,1,0:T(8,128)(2,1)S(1)}, u32[]{:S(2)}, u32[]{:S(2)}) collective-permute-start(bf16[4,37,1536]{2,1,0:T(8,128)(2,1)S(1)} %get-tuple-element.32), channel_id=1, source_target_pairs={{8,0},{12,4},{16,8},{20,12},{24,16},{28,20},{0,24},{4,28},{9,1},{1... | collective-permute-start | bytes 1363976 | tf_op jit(solution)/shard_map/ppermute | solution.py:36
  173.7 4.9 %collective-permute-start.15 = (bf16[4,37,1536]{2,1,0:T(8,128)(2,1)S(1)}, bf16[4,37,1536]{2,1,0:T(8,128)(2,1)S(1)}, u32[]{:S(2)}, u32[]{:S(2)}) collective-permute-start(bf16[4,37,1536]{2,1,0:T(8,128)(2,1)S(1)} %get-tuple-element.37), channel_id=1, source_target_pairs={{24,0},{28,4},{0,8},{4,12},{8,16},{12,20},{16,24},{20,28},{25,1},{... | collective-permute-start | bytes 1363976 | tf_op jit(solution)/shard_map/ppermute | solution.py:36
  178.6 20.1 %collective-permute-done.11 = bf16[4,37,1536]{2,1,0:T(8,128)(2,1)S(1)} collective-permute-done((bf16[4,37,1536]{2,1,0:T(8,128)(2,1)S(1)}, bf16[4,37,1536]{2,1,0:T(8,128)(2,1)S(1)}, u32[]{:S(2)}, u32[]{:S(2)}) %collective-permute-start.11) | collective-permute-done | bytes 454688 | tf_op jit(solution)/shard_map/ppermute | solution.py:36
  198.9 4.7 %collective-permute-done.15 = bf16[4,37,1536]{2,1,0:T(8,128)(2,1)S(1)} collective-permute-done((bf16[4,37,1536]{2,1,0:T(8,128)(2,1)S(1)}, bf16[4,37,1536]{2,1,0:T(8,128)(2,1)S(1)}, u32[]{:S(2)}, u32[]{:S(2)}) %collective-permute-start.15) | collective-permute-done | bytes 454688 | tf_op jit(solution)/shard_map/ppermute | solution.py:36
  203.5 6.5 %collective-permute-done.16 = bf16[4,37,1536]{2,1,0:T(8,128)(2,1)S(1)} collective-permute-done((bf16[4,37,1536]{2,1,0:T(8,128)(2,1)S(1)}, bf16[4,37,1536]{2,1,0:T(8,128)(2,1)S(1)}, u32[]{:S(2)}, u32[]{:S(2)}) %collective-permute-start.16) | collective-permute-done | bytes 454688 | tf_op jit(solution)/shard_map/ppermute | solution.py:36
  214.1 4.3 %collective-permute-start.19 = (bf16[4,37,1536]{2,1,0:T(8,128)(2,1)S(1)}, bf16[4,37,1536]{2,1,0:T(8,128)(2,1)S(1)}, u32[]{:S(2)}, u32[]{:S(2)}) collective-permute-start(bf16[4,37,1536]{2,1,0:T(8,128)(2,1)S(1)} %pad_maximum_fusion.7), channel_id=1, source_target_pairs={{0,12},{4,16},{8,20},{12,24},{16,28},{20,0},{24,4},{28,8},{1,13},{... | collective-permute-start | bytes 1363976 | tf_op jit(solution)/shard_map/ppermute | solution.py:28
  221.9 6.2 %collective-permute-done.17 = bf16[4,37,1536]{2,1,0:T(8,128)(2,1)S(1)} collective-permute-done((bf16[4,37,1536]{2,1,0:T(8,128)(2,1)S(1)}, bf16[4,37,1536]{2,1,0:T(8,128)(2,1)S(1)}, u32[]{:S(2)}, u32[]{:S(2)}) %collective-permute-start.17) | collective-permute-done | bytes 454688 | tf_op jit(solution)/shard_map/ppermute | solution.py:28
  229.1 15.9 %collective-permute-done.18 = bf16[4,37,1536]{2,1,0:T(8,128)(2,1)S(1)} collective-permute-done((bf16[4,37,1536]{2,1,0:T(8,128)(2,1)S(1)}, bf16[4,37,1536]{2,1,0:T(8,128)(2,1)S(1)}, u32[]{:S(2)}, u32[]{:S(2)}) %collective-permute-start.18) | collective-permute-done | bytes 454688 | tf_op jit(solution)/shard_map/ppermute | solution.py:28
  245.0 13.5 %collective-permute-start.23 = (bf16[4,37,1536]{2,1,0:T(8,128)(2,1)S(1)}, bf16[4,37,1536]{2,1,0:T(8,128)(2,1)S(1)}, u32[]{:S(2)}, u32[]{:S(2)}) collective-permute-start(bf16[4,37,1536]{2,1,0:T(8,128)(2,1)S(1)} %pad_maximum_fusion.7), channel_id=1, source_target_pairs={{0,28},{4,0},{8,4},{12,8},{16,12},{20,16},{24,20},{28,24},{1,29},{... | collective-permute-start | bytes 1363976 | tf_op jit(solution)/shard_map/ppermute | solution.py:28
  261.3 9.5 %collective-permute-done.23 = bf16[4,37,1536]{2,1,0:T(8,128)(2,1)S(1)} collective-permute-done((bf16[4,37,1536]{2,1,0:T(8,128)(2,1)S(1)}, bf16[4,37,1536]{2,1,0:T(8,128)(2,1)S(1)}, u32[]{:S(2)}, u32[]{:S(2)}) %collective-permute-start.23) | collective-permute-done | bytes 454688 | tf_op jit(solution)/shard_map/ppermute | solution.py:28
  271.8 4.3 %fusion.13 = bf16[8,4,32,768]{3,2,1,0:T(8,128)(2,1)} fusion(bf16[1536,768]{1,0:T(8,128)(2,1)S(1)} %copy-done.32, bf16[8,4,37,1536]{3,2,1,0:T(8,128)(2,1)S(1)} %bitcast_dynamic-update-slice_fusion), kind=kOutput, calls=%fused_computation.50 | convolution fusion | flops 2422996992 | bytes 7077888 | tf_op jit(solution)/shard_map/arnd,df->arnf/dot_general | solution.py:206
  276.1 4.7 %convolution_convert_fusion.3 = bf16[8,4,5,1536]{3,0,2,1:T(8,128)(2,1)} fusion(bf16[768,1536]{1,0:T(8,128)(2,1)} %param.37, bf16[1536,768]{1,0:T(8,128)(2,1)} %param.35, bf16[8,4,5,1536]{3,2,1,0:T(8,128)(2,1)} %slice.338), kind=kOutput, calls=%fused_computation.54 | convolution fusion | flops 756326400 | bytes 5701632 | tf_op jit(solution)/shard_map/arnf,fd->arnd/dot_general | solution.py:214
  282.0 4.2 %convolution_convert_fusion.1 = bf16[8,4,32,1536]{3,2,1,0:T(8,128)(2,1)S(1)} fusion(bf16[8,4,32,768]{3,2,1,0:T(8,128)(2,1)} %fusion.13, bf16[768,1536]{1,0:T(8,128)(2,1)S(1)} %copy-done), kind=kOutput, calls=%fused_computation.26 | convolution fusion | flops 2417491968 | bytes 7077888 | tf_op jit(solution)/shard_map/arnf,fd->arnd/dot_general | solution.py:213
  286.7 4.1 %collective-permute-start.24 = (bf16[4,37,1536]{2,1,0:T(8,128)(2,1)S(1)}, bf16[4,37,1536]{2,1,0:T(8,128)(2,1)S(1)}, u32[]{:S(2)}, u32[]{:S(2)}) collective-permute-start(bf16[4,37,1536]{2,1,0:T(8,128)(2,1)S(1)} %get-tuple-element.24), channel_id=1, source_target_pairs={{4,0},{8,4},{12,8},{16,12},{20,16},{24,20},{28,24},{0,28},{5,1},{9... | collective-permute-start | bytes 1363976 | tf_op jit(solution)/shard_map/ppermute | solution.py:36
  297.1 4.7 %collective-permute-done.24 = bf16[4,37,1536]{2,1,0:T(8,128)(2,1)S(1)} collective-permute-done((bf16[4,37,1536]{2,1,0:T(8,128)(2,1)S(1)}, bf16[4,37,1536]{2,1,0:T(8,128)(2,1)S(1)}, u32[]{:S(2)}, u32[]{:S(2)}) %collective-permute-start.24) | collective-permute-done | bytes 454688 | tf_op jit(solution)/shard_map/ppermute | solution.py:36
  301.9 22.0 %collective-permute-done.25 = bf16[4,37,1536]{2,1,0:T(8,128)(2,1)S(1)} collective-permute-done((bf16[4,37,1536]{2,1,0:T(8,128)(2,1)S(1)}, bf16[4,37,1536]{2,1,0:T(8,128)(2,1)S(1)}, u32[]{:S(2)}, u32[]{:S(2)}) %collective-permute-start.25) | collective-permute-done | bytes 454688 | tf_op jit(solution)/shard_map/ppermute | solution.py:36
  326.9 10.6 %collective-permute-done.30 = bf16[4,37,1536]{2,1,0:T(8,128)(2,1)S(1)} collective-permute-done((bf16[4,37,1536]{2,1,0:T(8,128)(2,1)S(1)}, bf16[4,37,1536]{2,1,0:T(8,128)(2,1)S(1)}, u32[]{:S(2)}, u32[]{:S(2)}) %collective-permute-start.30) | collective-permute-done | bytes 454688 | tf_op jit(solution)/shard_map/ppermute | solution.py:36
  342.5 11.2 %collective-permute-start.31 = (bf16[4,1,16,16]{3,2,1,0:T(8,128)(2,1)S(1)}, bf16[4,1,16,16]{3,2,1,0:T(8,128)(2,1)S(1)}, u32[]{:S(2)}, u32[]{:S(2)}) collective-permute-start(bf16[4,1,16,16]{3,2,1,0:T(8,128)(2,1)S(1)} %get-tuple-element.64), channel_id=1, source_target_pairs={{0,4},{4,8},{8,12},{12,16},{16,20},{20,24},{24,28},{1,5},{5,9},{9,... | collective-permute-start | bytes 6152 | tf_op jit(solution)/shard_map/ppermute | solution.py:16
  356.9 4.4 %collective-permute-done.32 = bf16[4,1,16,16]{3,2,1,0:T(8,128)(2,1)S(1)} collective-permute-done((bf16[4,1,16,16]{3,2,1,0:T(8,128)(2,1)S(1)}, bf16[4,1,16,16]{3,2,1,0:T(8,128)(2,1)S(1)}, u32[]{:S(2)}, u32[]{:S(2)}) %collective-permute-start.32) | collective-permute-done | bytes 2080 | tf_op jit(solution)/shard_map/ppermute | solution.py:19
  361.4 3.6 collective-permute-start.33
  (243 shorter events, 121.9 us)
Async XLA Ops:
  4.2 26.8 %collective-permute-start = (bf16[4,37,1536]{2,1,0:T(8,128)(2,1)}, bf16[4,37,1536]{2,1,0:T(8,128)(2,1)}, u32[]{:S(2)}, u32[]{:S(2)}) collective-permute-start(bf16[4,37,1536]{2,1,0:T(8,128)(2,1)} %get-tuple-element.47), channel_id=1, source_target_pairs={{0,4},{4,8},{8,12},{12,16},{16,20},{20,24},{24,28},{28,0},{1,5},{5... | collective-permute-start | bytes 1363976 | tf_op jit(solution)/shard_map/ppermute | solution.py:28
  7.8 36.5 %collective-permute-start.1 = (bf16[4,37,1536]{2,1,0:T(8,128)(2,1)}, bf16[4,37,1536]{2,1,0:T(8,128)(2,1)}, u32[]{:S(2)}, u32[]{:S(2)}) collective-permute-start(bf16[4,37,1536]{2,1,0:T(8,128)(2,1)} %get-tuple-element.47), channel_id=1, source_target_pairs={{0,8},{4,12},{8,16},{12,20},{16,24},{20,28},{24,0},{28,4},{1,9},{5... | collective-permute-start | bytes 1363976 | tf_op jit(solution)/shard_map/ppermute | solution.py:28
  9.4 36.1 %collective-permute-start.2 = (bf16[4,37,1536]{2,1,0:T(8,128)(2,1)}, bf16[4,37,1536]{2,1,0:T(8,128)(2,1)}, u32[]{:S(2)}, u32[]{:S(2)}) collective-permute-start(bf16[4,37,1536]{2,1,0:T(8,128)(2,1)} %get-tuple-element.47), channel_id=1, source_target_pairs={{0,12},{4,16},{8,20},{12,24},{16,28},{20,0},{24,4},{28,8},{1,13},{... | collective-permute-start | bytes 1363976 | tf_op jit(solution)/shard_map/ppermute | solution.py:28
  12.0 43.9 %collective-permute-start.3 = (bf16[4,37,1536]{2,1,0:T(8,128)(2,1)}, bf16[4,37,1536]{2,1,0:T(8,128)(2,1)}, u32[]{:S(2)}, u32[]{:S(2)}) collective-permute-start(bf16[4,37,1536]{2,1,0:T(8,128)(2,1)} %get-tuple-element.47), channel_id=1, source_target_pairs={{0,16},{4,20},{8,24},{12,28},{16,0},{20,4},{24,8},{28,12},{1,17},{... | collective-permute-start | bytes 1363976 | tf_op jit(solution)/shard_map/ppermute | solution.py:28
  12.9 44.1 %collective-permute-start.4 = (bf16[4,37,1536]{2,1,0:T(8,128)(2,1)}, bf16[4,37,1536]{2,1,0:T(8,128)(2,1)}, u32[]{:S(2)}, u32[]{:S(2)}) collective-permute-start(bf16[4,37,1536]{2,1,0:T(8,128)(2,1)} %get-tuple-element.47), channel_id=1, source_target_pairs={{0,20},{4,24},{8,28},{12,0},{16,4},{20,8},{24,12},{28,16},{1,21},{... | collective-permute-start | bytes 1363976 | tf_op jit(solution)/shard_map/ppermute | solution.py:28
  31.0 27.1 %collective-permute-start.5 = (bf16[4,37,1536]{2,1,0:T(8,128)(2,1)}, bf16[4,37,1536]{2,1,0:T(8,128)(2,1)S(1)}, u32[]{:S(2)}, u32[]{:S(2)}) collective-permute-start(bf16[4,37,1536]{2,1,0:T(8,128)(2,1)} %get-tuple-element.47), channel_id=1, source_target_pairs={{0,24},{4,28},{8,0},{12,4},{16,8},{20,12},{24,16},{28,20},{1,25},{... | collective-permute-start | bytes 1363976 | tf_op jit(solution)/shard_map/ppermute | solution.py:28
  44.3 14.2 %collective-permute-start.6 = (bf16[4,37,1536]{2,1,0:T(8,128)(2,1)}, bf16[4,37,1536]{2,1,0:T(8,128)(2,1)S(1)}, u32[]{:S(2)}, u32[]{:S(2)}) collective-permute-start(bf16[4,37,1536]{2,1,0:T(8,128)(2,1)} %get-tuple-element.47), channel_id=1, source_target_pairs={{0,28},{4,0},{8,4},{12,8},{16,12},{20,16},{24,20},{28,24},{1,29},{... | collective-permute-start | bytes 1363976 | tf_op jit(solution)/shard_map/ppermute | solution.py:28
  69.8 21.3 %collective-permute-start.7 = (bf16[1184,384]{1,0:T(8,128)(2,1)}, bf16[1184,384]{1,0:T(8,128)(2,1)}, u32[]{:S(2)}, u32[]{:S(2)}) collective-permute-start(bf16[1184,384]{1,0:T(8,128)(2,1)} %reshape.329), channel_id=1, source_target_pairs={{0,1},{1,2},{2,3},{3,0},{4,5},{5,6},{6,7},{7,4},{8,9},{9,10},{10,1... | collective-permute-start | bytes 2727944 | tf_op jit(solution)/shard_map/ppermute | solution.py:28
  71.4 40.8 %collective-permute-start.8 = (bf16[1184,384]{1,0:T(8,128)(2,1)}, bf16[1184,384]{1,0:T(8,128)(2,1)}, u32[]{:S(2)}, u32[]{:S(2)}) collective-permute-start(bf16[1184,384]{1,0:T(8,128)(2,1)} %reshape.329), channel_id=1, source_target_pairs={{0,2},{1,3},{2,0},{3,1},{4,6},{5,7},{6,4},{7,5},{8,10},{9,11},{10,... | collective-permute-start | bytes 2727944 | tf_op jit(solution)/shard_map/ppermute | solution.py:28
  72.5 45.8 %collective-permute-start.9 = (bf16[1184,384]{1,0:T(8,128)(2,1)}, bf16[1184,384]{1,0:T(8,128)(2,1)}, u32[]{:S(2)}, u32[]{:S(2)}) collective-permute-start(bf16[1184,384]{1,0:T(8,128)(2,1)} %reshape.329), channel_id=1, source_target_pairs={{0,3},{1,0},{2,1},{3,2},{4,7},{5,4},{6,5},{7,6},{8,11},{9,8},{10,9... | collective-permute-start | bytes 2727944 | tf_op jit(solution)/shard_map/ppermute | solution.py:28
  155.5 18.2 %collective-permute-start.10 = (bf16[4,37,1536]{2,1,0:T(8,128)(2,1)S(1)}, bf16[4,37,1536]{2,1,0:T(8,128)(2,1)S(1)}, u32[]{:S(2)}, u32[]{:S(2)}) collective-permute-start(bf16[4,37,1536]{2,1,0:T(8,128)(2,1)S(1)} %get-tuple-element.31), channel_id=1, source_target_pairs={{4,0},{8,4},{12,8},{16,12},{20,16},{24,20},{28,24},{0,28},{5,1},{9... | collective-permute-start | bytes 1363976 | tf_op jit(solution)/shard_map/ppermute | solution.py:36
  162.6 36.1 %collective-permute-start.11 = (bf16[4,37,1536]{2,1,0:T(8,128)(2,1)S(1)}, bf16[4,37,1536]{2,1,0:T(8,128)(2,1)S(1)}, u32[]{:S(2)}, u32[]{:S(2)}) collective-permute-start(bf16[4,37,1536]{2,1,0:T(8,128)(2,1)S(1)} %get-tuple-element.32), channel_id=1, source_target_pairs={{8,0},{12,4},{16,8},{20,12},{24,16},{28,20},{0,24},{4,28},{9,1},{1... | collective-permute-start | bytes 1363976 | tf_op jit(solution)/shard_map/ppermute | solution.py:36
  166.7 32.1 %collective-permute-start.12 = (bf16[4,37,1536]{2,1,0:T(8,128)(2,1)S(1)}, bf16[4,37,1536]{2,1,0:T(8,128)(2,1)S(1)}, u32[]{:S(2)}, u32[]{:S(2)}) collective-permute-start(bf16[4,37,1536]{2,1,0:T(8,128)(2,1)S(1)} %get-tuple-element.33), channel_id=1, source_target_pairs={{12,0},{16,4},{20,8},{24,12},{28,16},{0,20},{4,24},{8,28},{13,1},{... | collective-permute-start | bytes 1363976 | tf_op jit(solution)/shard_map/ppermute | solution.py:36
  170.0 28.8 %collective-permute-start.13 = (bf16[4,37,1536]{2,1,0:T(8,128)(2,1)S(1)}, bf16[4,37,1536]{2,1,0:T(8,128)(2,1)S(1)}, u32[]{:S(2)}, u32[]{:S(2)}) collective-permute-start(bf16[4,37,1536]{2,1,0:T(8,128)(2,1)S(1)} %get-tuple-element.34), channel_id=1, source_target_pairs={{16,0},{20,4},{24,8},{28,12},{0,16},{4,20},{8,24},{12,28},{17,1},{... | collective-permute-start | bytes 1363976 | tf_op jit(solution)/shard_map/ppermute | solution.py:36
  170.0 28.8 %collective-permute-start.14 = (bf16[4,37,1536]{2,1,0:T(8,128)(2,1)S(1)}, bf16[4,37,1536]{2,1,0:T(8,128)(2,1)S(1)}, u32[]{:S(2)}, u32[]{:S(2)}) collective-permute-start(bf16[4,37,1536]{2,1,0:T(8,128)(2,1)S(1)} %get-tuple-element.35), channel_id=1, source_target_pairs={{20,0},{24,4},{28,8},{0,12},{4,16},{8,20},{12,24},{16,28},{21,1},{... | collective-permute-start | bytes 1363976 | tf_op jit(solution)/shard_map/ppermute | solution.py:36
  173.7 29.8 %collective-permute-start.15 = (bf16[4,37,1536]{2,1,0:T(8,128)(2,1)S(1)}, bf16[4,37,1536]{2,1,0:T(8,128)(2,1)S(1)}, u32[]{:S(2)}, u32[]{:S(2)}) collective-permute-start(bf16[4,37,1536]{2,1,0:T(8,128)(2,1)S(1)} %get-tuple-element.37), channel_id=1, source_target_pairs={{24,0},{28,4},{0,8},{4,12},{8,16},{12,20},{16,24},{20,28},{25,1},{... | collective-permute-start | bytes 1363976 | tf_op jit(solution)/shard_map/ppermute | solution.py:36
  198.7 11.3 %collective-permute-start.16 = (bf16[4,37,1536]{2,1,0:T(8,128)(2,1)S(1)}, bf16[4,37,1536]{2,1,0:T(8,128)(2,1)S(1)}, u32[]{:S(2)}, u32[]{:S(2)}) collective-permute-start(bf16[4,37,1536]{2,1,0:T(8,128)(2,1)S(1)} %get-tuple-element.36), channel_id=1, source_target_pairs={{28,0},{0,4},{4,8},{8,12},{12,16},{16,20},{20,24},{24,28},{29,1},{... | collective-permute-start | bytes 1363976 | tf_op jit(solution)/shard_map/ppermute | solution.py:36
  211.7 16.4 %collective-permute-start.17 = (bf16[4,37,1536]{2,1,0:T(8,128)(2,1)S(1)}, bf16[4,37,1536]{2,1,0:T(8,128)(2,1)S(1)}, u32[]{:S(2)}, u32[]{:S(2)}) collective-permute-start(bf16[4,37,1536]{2,1,0:T(8,128)(2,1)S(1)} %pad_maximum_fusion.7), channel_id=1, source_target_pairs={{0,4},{4,8},{8,12},{12,16},{16,20},{20,24},{24,28},{28,0},{1,5},{5... | collective-permute-start | bytes 1363976 | tf_op jit(solution)/shard_map/ppermute | solution.py:28
  212.6 32.4 %collective-permute-start.18 = (bf16[4,37,1536]{2,1,0:T(8,128)(2,1)S(1)}, bf16[4,37,1536]{2,1,0:T(8,128)(2,1)S(1)}, u32[]{:S(2)}, u32[]{:S(2)}) collective-permute-start(bf16[4,37,1536]{2,1,0:T(8,128)(2,1)S(1)} %pad_maximum_fusion.7), channel_id=1, source_target_pairs={{0,8},{4,12},{8,16},{12,20},{16,24},{20,28},{24,0},{28,4},{1,9},{5... | collective-permute-start | bytes 1363976 | tf_op jit(solution)/shard_map/ppermute | solution.py:28
  214.1 44.5 %collective-permute-start.19 = (bf16[4,37,1536]{2,1,0:T(8,128)(2,1)S(1)}, bf16[4,37,1536]{2,1,0:T(8,128)(2,1)S(1)}, u32[]{:S(2)}, u32[]{:S(2)}) collective-permute-start(bf16[4,37,1536]{2,1,0:T(8,128)(2,1)S(1)} %pad_maximum_fusion.7), channel_id=1, source_target_pairs={{0,12},{4,16},{8,20},{12,24},{16,28},{20,0},{24,4},{28,8},{1,13},{... | collective-permute-start | bytes 1363976 | tf_op jit(solution)/shard_map/ppermute | solution.py:28
  218.4 40.2 %collective-permute-start.20 = (bf16[4,37,1536]{2,1,0:T(8,128)(2,1)S(1)}, bf16[4,37,1536]{2,1,0:T(8,128)(2,1)S(1)}, u32[]{:S(2)}, u32[]{:S(2)}) collective-permute-start(bf16[4,37,1536]{2,1,0:T(8,128)(2,1)S(1)} %pad_maximum_fusion.7), channel_id=1, source_target_pairs={{0,16},{4,20},{8,24},{12,28},{16,0},{20,4},{24,8},{28,12},{1,17},{... | collective-permute-start | bytes 1363976 | tf_op jit(solution)/shard_map/ppermute | solution.py:28
  218.4 40.2 %collective-permute-start.21 = (bf16[4,37,1536]{2,1,0:T(8,128)(2,1)S(1)}, bf16[4,37,1536]{2,1,0:T(8,128)(2,1)S(1)}, u32[]{:S(2)}, u32[]{:S(2)}) collective-permute-start(bf16[4,37,1536]{2,1,0:T(8,128)(2,1)S(1)} %pad_maximum_fusion.7), channel_id=1, source_target_pairs={{0,20},{4,24},{8,28},{12,0},{16,4},{20,8},{24,12},{28,16},{1,21},{... | collective-permute-start | bytes 1363976 | tf_op jit(solution)/shard_map/ppermute | solution.py:28
  228.1 33.1 %collective-permute-start.22 = (bf16[4,37,1536]{2,1,0:T(8,128)(2,1)S(1)}, bf16[4,37,1536]{2,1,0:T(8,128)(2,1)S(1)}, u32[]{:S(2)}, u32[]{:S(2)}) collective-permute-start(bf16[4,37,1536]{2,1,0:T(8,128)(2,1)S(1)} %pad_maximum_fusion.7), channel_id=1, source_target_pairs={{0,24},{4,28},{8,0},{12,4},{16,8},{20,12},{24,16},{28,20},{1,25},{... | collective-permute-start | bytes 1363976 | tf_op jit(solution)/shard_map/ppermute | solution.py:28
  245.0 25.8 %collective-permute-start.23 = (bf16[4,37,1536]{2,1,0:T(8,128)(2,1)S(1)}, bf16[4,37,1536]{2,1,0:T(8,128)(2,1)S(1)}, u32[]{:S(2)}, u32[]{:S(2)}) collective-permute-start(bf16[4,37,1536]{2,1,0:T(8,128)(2,1)S(1)} %pad_maximum_fusion.7), channel_id=1, source_target_pairs={{0,28},{4,0},{8,4},{12,8},{16,12},{20,16},{24,20},{28,24},{1,29},{... | collective-permute-start | bytes 1363976 | tf_op jit(solution)/shard_map/ppermute | solution.py:28
  286.7 15.1 %collective-permute-start.24 = (bf16[4,37,1536]{2,1,0:T(8,128)(2,1)S(1)}, bf16[4,37,1536]{2,1,0:T(8,128)(2,1)S(1)}, u32[]{:S(2)}, u32[]{:S(2)}) collective-permute-start(bf16[4,37,1536]{2,1,0:T(8,128)(2,1)S(1)} %get-tuple-element.24), channel_id=1, source_target_pairs={{4,0},{8,4},{12,8},{16,12},{20,16},{24,20},{28,24},{0,28},{5,1},{9... | collective-permute-start | bytes 1363976 | tf_op jit(solution)/shard_map/ppermute | solution.py:36
  290.8 33.2 %collective-permute-start.25 = (bf16[4,37,1536]{2,1,0:T(8,128)(2,1)S(1)}, bf16[4,37,1536]{2,1,0:T(8,128)(2,1)S(1)}, u32[]{:S(2)}, u32[]{:S(2)}) collective-permute-start(bf16[4,37,1536]{2,1,0:T(8,128)(2,1)S(1)} %get-tuple-element.25), channel_id=1, source_target_pairs={{8,0},{12,4},{16,8},{20,12},{24,16},{28,20},{0,24},{4,28},{9,1},{1... | collective-permute-start | bytes 1363976 | tf_op jit(solution)/shard_map/ppermute | solution.py:36
  290.9 33.3 %collective-permute-start.26 = (bf16[4,37,1536]{2,1,0:T(8,128)(2,1)S(1)}, bf16[4,37,1536]{2,1,0:T(8,128)(2,1)S(1)}, u32[]{:S(2)}, u32[]{:S(2)}) collective-permute-start(bf16[4,37,1536]{2,1,0:T(8,128)(2,1)S(1)} %get-tuple-element.26), channel_id=1, source_target_pairs={{12,0},{16,4},{20,8},{24,12},{28,16},{0,20},{4,24},{8,28},{13,1},{... | collective-permute-start | bytes 1363976 | tf_op jit(solution)/shard_map/ppermute | solution.py:36
  291.9 32.3 %collective-permute-start.27 = (bf16[4,37,1536]{2,1,0:T(8,128)(2,1)S(1)}, bf16[4,37,1536]{2,1,0:T(8,128)(2,1)S(1)}, u32[]{:S(2)}, u32[]{:S(2)}) collective-permute-start(bf16[4,37,1536]{2,1,0:T(8,128)(2,1)S(1)} %get-tuple-element.27), channel_id=1, source_target_pairs={{16,0},{20,4},{24,8},{28,12},{0,16},{4,20},{8,24},{12,28},{17,1},{... | collective-permute-start | bytes 1363976 | tf_op jit(solution)/shard_map/ppermute | solution.py:36
  294.0 30.2 %collective-permute-start.28 = (bf16[4,37,1536]{2,1,0:T(8,128)(2,1)S(1)}, bf16[4,37,1536]{2,1,0:T(8,128)(2,1)S(1)}, u32[]{:S(2)}, u32[]{:S(2)}) collective-permute-start(bf16[4,37,1536]{2,1,0:T(8,128)(2,1)S(1)} %get-tuple-element.28), channel_id=1, source_target_pairs={{20,0},{24,4},{28,8},{0,12},{4,16},{8,20},{12,24},{16,28},{21,1},{... | collective-permute-start | bytes 1363976 | tf_op jit(solution)/shard_map/ppermute | solution.py:36
  301.8 25.1 %collective-permute-start.29 = (bf16[4,37,1536]{2,1,0:T(8,128)(2,1)S(1)}, bf16[4,37,1536]{2,1,0:T(8,128)(2,1)S(1)}, u32[]{:S(2)}, u32[]{:S(2)}) collective-permute-start(bf16[4,37,1536]{2,1,0:T(8,128)(2,1)S(1)} %get-tuple-element.30), channel_id=1, source_target_pairs={{24,0},{28,4},{0,8},{4,12},{8,16},{12,20},{16,24},{20,28},{25,1},{... | collective-permute-start | bytes 1363976 | tf_op jit(solution)/shard_map/ppermute | solution.py:36
  324.0 13.6 %collective-permute-start.30 = (bf16[4,37,1536]{2,1,0:T(8,128)(2,1)S(1)}, bf16[4,37,1536]{2,1,0:T(8,128)(2,1)S(1)}, u32[]{:S(2)}, u32[]{:S(2)}) collective-permute-start(bf16[4,37,1536]{2,1,0:T(8,128)(2,1)S(1)} %get-tuple-element.29), channel_id=1, source_target_pairs={{28,0},{0,4},{4,8},{8,12},{12,16},{16,20},{20,24},{24,28},{29,1},{... | collective-permute-start | bytes 1363976 | tf_op jit(solution)/shard_map/ppermute | solution.py:36
  342.5 14.4 %collective-permute-start.31 = (bf16[4,1,16,16]{3,2,1,0:T(8,128)(2,1)S(1)}, bf16[4,1,16,16]{3,2,1,0:T(8,128)(2,1)S(1)}, u32[]{:S(2)}, u32[]{:S(2)}) collective-permute-start(bf16[4,1,16,16]{3,2,1,0:T(8,128)(2,1)S(1)} %get-tuple-element.64), channel_id=1, source_target_pairs={{0,4},{4,8},{8,12},{12,16},{16,20},{20,24},{24,28},{1,5},{5,9},{9,... | collective-permute-start | bytes 6152 | tf_op jit(solution)/shard_map/ppermute | solution.py:16
  (38 other events, 718.9 us)
where the time goes:
time: 379 us; the launch traced here: 373 us
  waiting for transfers between devices  154 us (41%)
  starting transfers between devices  93.1 us (25%)
  matrix products  55.5 us (15%)
  local copies, waits for them, and re-layouts  46.8 us (12%)
  other arithmetic  21.8 us (6%)
    ppermute x17, waiting for transfers between devices, gather_slots(): lax.ppermute(block, axis, [(i, (i + shift) % count) for i in range(count)])  74.6 us
    ppermute x14, waiting for transfers between devices, scatter_slots(): lax.ppermute(partial[shift], axis, [((i + shift) % count, i) for i in ran...  73.6 us
    ppermute x17, starting transfers between devices, gather_slots(): lax.ppermute(block, axis, [(i, (i + shift) % count) for i in range(count)])  42.2 us
    ppermute x14, starting transfers between devices, scatter_slots(): lax.ppermute(partial[shift], axis, [((i + shift) % count, i) for i in ran...  31.5 us
    another operation x8, local copies, waits for them, and re-layouts, gather_slots(): return jnp.stack(parts)  17.3 us
    ppermute x2, starting transfers between devices, extended(): lax.ppermute(lax.slice_in_dim(block, block.shape[dim] - width, None, axis...  14.8 us
    dot_general x1, matrix products, body(): jnp.einsum('rhqk,rhke->rhqe', weights.astype(jnp.bfloat16), key_piece, pr...  9.35 us
    unnamed x93, local copies, waits for them, and re-layouts  8.92 us
  transfers between devices with their start and end apart: 35, of which 19 were waited for; matrix products, arithmetic and copies ran while one was open for 13% of the time, Pallas kernels for 0%

commit v1 on v0

--- a/solution.py
+++ b/solution.py
@@ -3,6 +3,7 @@
 import jax
 import jax.numpy as jnp
 from jax import lax
+from jax.experimental import pallas as pl
 from jax.sharding import PartitionSpec as P
 
 HD = 64
@@ -37,6 +38,46 @@
             partial[shift], axis, [((i + shift) % count, i) for i in range(count)]
         ).astype(jnp.float32)
     return total
+
+
+def send_slots(block, axis):
+    count = lax.axis_size(axis)
+    parts = [block]
+    for shift in range(1, count):
+        parts.append(lax.ppermute(block, axis, [(i, (i + shift) % count) for i in range(count)]))
+    return parts
+
+
+def attention_kernel(query_ref, *refs):
+    *pair_refs, mask_ref, out_ref = refs
+    query = query_ref[...]
+    numerator = None
+    denominator = None
+    for block, pair_ref in enumerate(pair_refs):
+        pairs = pair_ref[...]
+        scores = lax.dot_general(
+            query, pairs, (((1,), (1,)), ((), ())), preferred_element_type=jnp.float32
+        ) * (1.0 / math.sqrt(HD))
+        weights = jnp.exp(scores) * mask_ref[block]
+        part_den = jnp.sum(weights, axis=1, keepdims=True)
+        part_num = jnp.dot(weights.astype(jnp.bfloat16), pairs, preferred_element_type=jnp.float32)
+        numerator = part_num if numerator is None else numerator + part_num
+        denominator = part_den if denominator is None else denominator + part_den
+    out_ref[...] = (numerator / denominator).astype(out_ref.dtype)
+
+
+def attend(query_rows, pair_blocks, usable, heads, tile):
+    requests, rows, lanes = query_rows.shape
+    keys = pair_blocks[0].shape[0] // requests
+    return pl.pallas_call(
+        attention_kernel,
+        grid=(requests, heads),
+        in_specs=[pl.BlockSpec((None, rows, tile), lambda r, h: (r, 0, h))]
+        + [pl.BlockSpec((keys, tile), lambda r, h: (r, h)) for _ in pair_blocks]
+        + [pl.BlockSpec((None, len(pair_blocks), 1, keys), lambda r, h: (r, 0, 0, 0))],
+        out_specs=pl.BlockSpec((None, rows, tile), lambda r, h: (r, 0, h)),
+        out_shape=jax.ShapeDtypeStruct((requests, rows, lanes), jnp.bfloat16),
+    )(query_rows, *pair_blocks, usable)
 
 
 def per_request(vector, values, axis):
@@ -152,48 +193,30 @@
     local_heads = queries.shape[-1] // tile
     local_width = local_heads * HD
     score_scale = 1.0 / math.sqrt(HD)
-    kv = gather_slots(key_value.reshape(-1, local_heads * tile), "blk")
-    span = blocks * groups * tile_tokens
-    key_piece = (
-        kv.reshape(blocks, groups, requests, tile_tokens, local_heads, tile)
-        .transpose(2, 4, 0, 1, 3, 5)
-        .reshape(requests, local_heads, span, tile)
-    )
+    pair_blocks = send_slots(key_value.transpose(1, 0, 2, 3).reshape(-1, local_heads * tile), "blk")
     query_rows = groups * tile_tokens
-    query_piece = (
-        queries.reshape(groups, requests, tile_tokens, local_heads, tile)
-        .transpose(1, 3, 0, 2, 4)
-        .reshape(requests, local_heads, query_rows, tile)
-    )
-    position = jnp.arange(span, dtype=jnp.int32)
-    source = (lax.axis_index("blk") - position // (groups * tile_tokens)) % blocks
-    group = (lax.axis_index("head") - (position // tile_tokens) % groups) % groups
+    query_piece = queries.transpose(1, 0, 2, 3).reshape(requests, query_rows, local_heads * tile)
+    position = jnp.arange(query_rows, dtype=jnp.int32)
+    group = (lax.axis_index("head") - position // tile_tokens) % groups
     within = position % tile_tokens
-    slot_ids = (group * blocks + source) * text_slice + (within - image_tile)
-    usable = (within < image_tile)[None, :] | (slot_ids[None, :] < text_lengths[:, None])
-    scores = (
-        jnp.einsum("rhqe,rhke->rhqk", query_piece, key_piece, preferred_element_type=jnp.float32)
-        * score_scale
-    )
-    weights = jnp.exp(scores) * usable[:, None, None, :].astype(jnp.float32)
-    denominator = jnp.sum(weights, -1)
-    numerator = jnp.einsum(
-        "rhqk,rhke->rhqe",
-        weights.astype(jnp.bfloat16),
-        key_piece,
-        preferred_element_type=jnp.float32,
-    )[..., HD:]
-    context = (numerator / denominator[..., None]).astype(jnp.bfloat16)
-    context = (
-        context.reshape(requests, local_heads, groups, tile_tokens, HD)
-        .transpose(2, 0, 3, 1, 4)
-        .reshape(groups, requests, tile_tokens, local_width)
-    )
+    source = (lax.axis_index("blk") - jnp.arange(blocks, dtype=jnp.int32)) % blocks
+    slot_ids = (group[None, :] * blocks + source[:, None]) * text_slice + (within - image_tile)[None, :]
+    usable = (within < image_tile)[None, None, :] | (
+        slot_ids[None, :, :] < text_lengths[:, None, None]
+    )
+    usable = usable.astype(jnp.float32).reshape(requests, blocks, 1, query_rows)
+    attended = attend(query_piece, pair_blocks, usable, local_heads, tile)
+    context = attended.reshape(requests, groups, tile_tokens, local_heads * tile)
+
+    def padded_rows(weight):
+        shaped = weight.reshape(local_heads, HD, weight.shape[-1])
+        return jnp.concatenate([jnp.zeros_like(shaped), shaped], 1).reshape(local_heads * tile, -1)
+
     image_part = jnp.einsum(
-        "arne,ed->arnd", context[:, :, :image_tile], image_proj, preferred_element_type=jnp.float32
+        "rane,ed->arnd", context[:, :, :image_tile], padded_rows(image_proj), preferred_element_type=jnp.float32
     )
     text_part = jnp.einsum(
-        "arne,ed->arnd", context[:, :, image_tile:], text_proj, preferred_element_type=jnp.float32
+        "rane,ed->arnd", context[:, :, image_tile:], padded_rows(text_proj), preferred_element_type=jnp.float32
     )
     attn = scatter_slots(jnp.concatenate([image_part, text_part], 2).astype(jnp.bfloat16), "head")
     own_f = own.astype(jnp.float32)

time: 379 us -> 359 us (0.947); the launches traced: 373 us -> 357 us
  waiting for transfers between devices: 154 us -> 177 us
  local copies, waits for them, and re-layouts: 46.8 us -> 26.6 us
  matrix products: 55.5 us -> 36.7 us
  Pallas kernels: 0 us -> 14.2 us
  starting transfers between devices: 93.1 us -> 80.5 us
    ppermute x0 -> x3, waiting for transfers between devices: none -> 27.6 us  [send_slots(): lax.ppermute(block, axis, [(i, (i + shift) % count) for i in range(count)])]
    ppermute x17 -> x14, waiting for transfers between devices: 74.6 us -> 53.7 us  [gather_slots(): lax.ppermute(block, axis, [(i, (i + shift) % count) for i in range(count)])]
    ppermute x14, waiting for transfers between devices: 73.6 us -> 92.7 us  [scatter_slots(): lax.ppermute(partial[shift], axis, [((i + shift) % count, i) for i in ran...]
    dot_general x4 -> x2, matrix products: 20.3 us -> 2.22 us  [the longest x1 1.8 us: body(): jnp.einsum('rane,ed->arnd', context[:, :, :image_tile], padded_rows(image...]
    another operation x8 -> x2, local copies, waits for them, and re-layouts: 17.3 us -> 0.07 us  [gather_slots(): return jnp.stack(parts)]
    ppermute x17 -> x14, starting transfers between devices: 42.2 us -> 26.5 us  [gather_slots(): lax.ppermute(block, axis, [(i, (i + shift) % count) for i in range(count)])]
    pallas_call x0 -> x1, Pallas kernels: none -> 14.2 us  [attend(): pl.pallas_call(attention_kernel, grid=(requests, heads), in_specs=[pl.Blo...]
    ppermute x2, starting transfers between devices: 14.8 us -> 3.2 us  [extended(): lax.ppermute(lax.slice_in_dim(block, block.shape[dim] - width, None, axis...]
  transfers between devices with their start and end apart: 35 -> 35, of which waited for: 19 -> 20; matrix products, arithmetic and copies ran while one was open for 13% -> 11% of each run, Pallas kernels for 0% -> 0%
where the time goes in v1:
time: 359 us; the launch traced here: 357 us
  waiting for transfers between devices  177 us (49%)
  starting transfers between devices  80.5 us (22%)
  matrix products  36.7 us (10%)
  local copies, waits for them, and re-layouts  26.6 us (7%)
  other arithmetic  20.1 us (6%)
  Pallas kernels  14.2 us (4%)
    ppermute x14, waiting for transfers between devices, scatter_slots(): lax.ppermute(partial[shift], axis, [((i + shift) % count, i) for i in ran...  92.7 us
    ppermute x14, waiting for transfers between devices, gather_slots(): lax.ppermute(block, axis, [(i, (i + shift) % count) for i in range(count)])  53.7 us
    ppermute x14, starting transfers between devices, scatter_slots(): lax.ppermute(partial[shift], axis, [((i + shift) % count, i) for i in ran...  40.4 us
    ppermute x3, waiting for transfers between devices, send_slots(): lax.ppermute(block, axis, [(i, (i + shift) % count) for i in range(count)])  27.6 us
    ppermute x14, starting transfers between devices, gather_slots(): lax.ppermute(block, axis, [(i, (i + shift) % count) for i in range(count)])  26.5 us
    pallas_call x1, Pallas kernels, attend(): pl.pallas_call(attention_kernel, grid=(requests, heads), in_specs=[pl.Blo...  14.2 us
    unnamed x97, local copies, waits for them, and re-layouts  10.4 us
    dot_general x4, matrix products, normalized(): jnp.dot(values * values, spread, precision=lax.Precision.HIGHEST)  8.43 us
  transfers between devices with their start and end apart: 35, of which 20 were waited for; matrix products, arithmetic and copies ran while one was open for 11% of the time, Pallas kernels for 0%

profile of v1, /device:TPU:1, one launch (start us, length us, event | category | flops | bytes accessed | tf_op | source)
XLA Modules:
  0.0 356.9 jit_solution(6819839049283339322)
XLA Ops:
  4.0 3.6 %collective-permute-start = (bf16[4,37,1536]{2,1,0:T(8,128)(2,1)}, bf16[4,37,1536]{2,1,0:T(8,128)(2,1)}, u32[]{:S(2)}, u32[]{:S(2)}) collective-permute-start(bf16[4,37,1536]{2,1,0:T(8,128)(2,1)} %get-tuple-element.47), channel_id=1, source_target_pairs={{0,4},{4,8},{8,12},{12,16},{16,20},{20,24},{24,28},{28,0},{1,5},{5... | collective-permute-start | bytes 1363976 | tf_op jit(solution)/shard_map/ppermute | solution.py:29
  12.8 5.2 %collective-permute-start.4 = (bf16[4,37,1536]{2,1,0:T(8,128)(2,1)}, bf16[4,37,1536]{2,1,0:T(8,128)(2,1)}, u32[]{:S(2)}, u32[]{:S(2)}) collective-permute-start(bf16[4,37,1536]{2,1,0:T(8,128)(2,1)} %get-tuple-element.47), channel_id=1, source_target_pairs={{0,20},{4,24},{8,28},{12,0},{16,4},{20,8},{24,12},{28,16},{1,21},{... | collective-permute-start | bytes 1363976 | tf_op jit(solution)/shard_map/ppermute | solution.py:29
  37.6 6.5 %collective-permute-done.1 = bf16[4,37,1536]{2,1,0:T(8,128)(2,1)} collective-permute-done((bf16[4,37,1536]{2,1,0:T(8,128)(2,1)}, bf16[4,37,1536]{2,1,0:T(8,128)(2,1)}, u32[]{:S(2)}, u32[]{:S(2)}) %collective-permute-start.1) | collective-permute-done | bytes 454688 | tf_op jit(solution)/shard_map/ppermute | solution.py:29
  46.4 9.3 %collective-permute-done.3 = bf16[4,37,1536]{2,1,0:T(8,128)(2,1)} collective-permute-done((bf16[4,37,1536]{2,1,0:T(8,128)(2,1)}, bf16[4,37,1536]{2,1,0:T(8,128)(2,1)}, u32[]{:S(2)}, u32[]{:S(2)}) %collective-permute-start.3) | collective-permute-done | bytes 454688 | tf_op jit(solution)/shard_map/ppermute | solution.py:29
  65.1 3.2 select_convert_fusion
  76.4 4.0 %fusion.217 = f32[8,4,32,384]{3,2,1,0:T(8,128)S(1)} fusion(bf16[1536,384,1,1]{0,1,3,2:T(8,128)(2,1)S(1)} %bitcast.303, f32[8,4,37,1536]{3,2,1,0:T(8,128)} %copy-done.1, f32[4,1536]{1,0:T(4,128)S(1)} %copy-done.25, f32[4,1536]{1,0:T(4,128)S(1)} %bitcast.314, f32[8,4,32]{2,1,0:T(4,128)S(1)} %add_rsqrt_fusion.1, f32[8,4,32]{2,1,0:T(4,128)S(1)} %broadcast_multiply_fusion.1), kind=kOutput, calls=%fused_computation.360 | convolution fusion | flops 1215823872 | bytes 9101312 | tf_op jit(solution)/shard_map/arnd,de->arne/dot_general | solution.py:129
  80.4 3.2 multiply_convert_fusion
  85.2 6.0 %collective-permute-done.7.refs_1_ = bf16[1184,384]{1,0:T(8,128)(2,1)S(1)} collective-permute-done((bf16[1184,384]{1,0:T(8,128)(2,1)}, bf16[1184,384]{1,0:T(8,128)(2,1)S(1)}, u32[]{:S(2)}, u32[]{:S(2)}) %collective-permute-start.7) | collective-permute-done | bytes 909344 | tf_op jit(solution)/shard_map/ppermute | solution.py:47
  91.1 21.1 %collective-permute-done.8.refs_2_ = bf16[1184,384]{1,0:T(8,128)(2,1)} collective-permute-done((bf16[1184,384]{1,0:T(8,128)(2,1)}, bf16[1184,384]{1,0:T(8,128)(2,1)}, u32[]{:S(2)}, u32[]{:S(2)}) %collective-permute-start.8) | collective-permute-done | bytes 909344 | tf_op jit(solution)/shard_map/ppermute | solution.py:47
  112.8 14.2 %shard_map.219 = bf16[4,296,384]{2,1,0:T(8,128)(2,1)} custom-call(bf16[4,296,384]{2,1,0:T(8,128)(2,1)} %copy.107.query_ref, bf16[1184,384]{1,0:T(8,128)(2,1)} %reshape.330.refs_0_, bf16[1184,384]{1,0:T(8,128)(2,1)} %copy-done.12, bf16[1184,384]{1,0:T(8,128)(2,1)} %collective-permute-done.8.refs_2_, bf16[1184,384]{1,0:T(8,128)(2,1)} %collective-permute-done.9.refs_3_, ...), custom_call_target="tpu_custom_call" | custom-call | tf_op jit(solution)/shard_map/pallas_call | solution.py:72
  132.4 9.0 %collective-permute-start.10 = (bf16[4,37,1536]{2,1,0:T(8,128)(2,1)S(1)}, bf16[4,37,1536]{2,1,0:T(8,128)(2,1)S(1)}, u32[]{:S(2)}, u32[]{:S(2)}) collective-permute-start(bf16[4,37,1536]{2,1,0:T(8,128)(2,1)S(1)} %get-tuple-element.31), channel_id=1, source_target_pairs={{4,0},{8,4},{12,8},{16,12},{20,16},{24,20},{28,24},{0,28},{5,1},{9... | collective-permute-start | bytes 1363976 | tf_op jit(solution)/shard_map/ppermute | solution.py:37
  143.6 3.3 collective-permute-start.12
  148.8 3.7 %collective-permute-done.10 = bf16[4,37,1536]{2,1,0:T(8,128)(2,1)S(1)} collective-permute-done((bf16[4,37,1536]{2,1,0:T(8,128)(2,1)S(1)}, bf16[4,37,1536]{2,1,0:T(8,128)(2,1)S(1)}, u32[]{:S(2)}, u32[]{:S(2)}) %collective-permute-start.10) | collective-permute-done | bytes 454688 | tf_op jit(solution)/shard_map/ppermute | solution.py:37
  152.4 3.0 collective-permute-start.15
  155.4 20.1 %collective-permute-done.11 = bf16[4,37,1536]{2,1,0:T(8,128)(2,1)S(1)} collective-permute-done((bf16[4,37,1536]{2,1,0:T(8,128)(2,1)S(1)}, bf16[4,37,1536]{2,1,0:T(8,128)(2,1)S(1)}, u32[]{:S(2)}, u32[]{:S(2)}) %collective-permute-start.11) | collective-permute-done | bytes 454688 | tf_op jit(solution)/shard_map/ppermute | solution.py:37
  177.3 3.6 %collective-permute-done.15 = bf16[4,37,1536]{2,1,0:T(8,128)(2,1)S(1)} collective-permute-done((bf16[4,37,1536]{2,1,0:T(8,128)(2,1)S(1)}, bf16[4,37,1536]{2,1,0:T(8,128)(2,1)S(1)}, u32[]{:S(2)}, u32[]{:S(2)}) %collective-permute-start.15) | collective-permute-done | bytes 454688 | tf_op jit(solution)/shard_map/ppermute | solution.py:37
  180.9 17.6 %collective-permute-done.16 = bf16[4,37,1536]{2,1,0:T(8,128)(2,1)S(1)} collective-permute-done((bf16[4,37,1536]{2,1,0:T(8,128)(2,1)S(1)}, bf16[4,37,1536]{2,1,0:T(8,128)(2,1)S(1)}, u32[]{:S(2)}, u32[]{:S(2)}) %collective-permute-start.16) | collective-permute-done | bytes 454688 | tf_op jit(solution)/shard_map/ppermute | solution.py:37
  200.7 4.1 %collective-permute-start.19 = (bf16[4,37,1536]{2,1,0:T(8,128)(2,1)S(1)}, bf16[4,37,1536]{2,1,0:T(8,128)(2,1)S(1)}, u32[]{:S(2)}, u32[]{:S(2)}) collective-permute-start(bf16[4,37,1536]{2,1,0:T(8,128)(2,1)S(1)} %pad_maximum_fusion.5), channel_id=1, source_target_pairs={{0,12},{4,16},{8,20},{12,24},{16,28},{20,0},{24,4},{28,8},{1,13},{... | collective-permute-start | bytes 1363976 | tf_op jit(solution)/shard_map/ppermute | solution.py:29
  206.8 4.6 %collective-permute-start.21 = (bf16[4,37,1536]{2,1,0:T(8,128)(2,1)S(1)}, bf16[4,37,1536]{2,1,0:T(8,128)(2,1)S(1)}, u32[]{:S(2)}, u32[]{:S(2)}) collective-permute-start(bf16[4,37,1536]{2,1,0:T(8,128)(2,1)S(1)} %pad_maximum_fusion.5), channel_id=1, source_target_pairs={{0,20},{4,24},{8,28},{12,0},{16,4},{20,8},{24,12},{28,16},{1,21},{... | collective-permute-start | bytes 1363976 | tf_op jit(solution)/shard_map/ppermute | solution.py:29
  211.5 4.5 %collective-permute-done.17 = bf16[4,37,1536]{2,1,0:T(8,128)(2,1)S(1)} collective-permute-done((bf16[4,37,1536]{2,1,0:T(8,128)(2,1)S(1)}, bf16[4,37,1536]{2,1,0:T(8,128)(2,1)S(1)}, u32[]{:S(2)}, u32[]{:S(2)}) %collective-permute-start.17) | collective-permute-done | bytes 454688 | tf_op jit(solution)/shard_map/ppermute | solution.py:29
  216.7 20.2 %collective-permute-done.18 = bf16[4,37,1536]{2,1,0:T(8,128)(2,1)S(1)} collective-permute-done((bf16[4,37,1536]{2,1,0:T(8,128)(2,1)S(1)}, bf16[4,37,1536]{2,1,0:T(8,128)(2,1)S(1)}, u32[]{:S(2)}, u32[]{:S(2)}) %collective-permute-start.18) | collective-permute-done | bytes 454688 | tf_op jit(solution)/shard_map/ppermute | solution.py:29
  237.0 11.3 %collective-permute-done.20 = bf16[4,37,1536]{2,1,0:T(8,128)(2,1)S(1)} collective-permute-done((bf16[4,37,1536]{2,1,0:T(8,128)(2,1)S(1)}, bf16[4,37,1536]{2,1,0:T(8,128)(2,1)S(1)}, u32[]{:S(2)}, u32[]{:S(2)}) %collective-permute-start.20) | collective-permute-done | bytes 454688 | tf_op jit(solution)/shard_map/ppermute | solution.py:29
  250.9 4.1 %fusion.8 = bf16[8,4,32,768]{3,2,1,0:T(8,128)(2,1)} fusion(bf16[1536,768]{1,0:T(8,128)(2,1)S(1)} %copy-done.33, bf16[8,4,37,1536]{3,2,1,0:T(8,128)(2,1)S(1)} %bitcast_dynamic-update-slice_fusion), kind=kOutput, calls=%fused_computation.43 | convolution fusion | flops 2422996992 | bytes 7077888 | tf_op jit(solution)/shard_map/arnd,df->arnf/dot_general | solution.py:229
  255.0 4.7 %convolution_convert_fusion.3 = bf16[8,4,5,1536]{3,0,2,1:T(8,128)(2,1)} fusion(bf16[768,1536]{1,0:T(8,128)(2,1)} %param.37, bf16[1536,768]{1,0:T(8,128)(2,1)} %param.35, bf16[8,4,5,1536]{3,2,1,0:T(8,128)(2,1)} %slice.333), kind=kOutput, calls=%fused_computation.47 | convolution fusion | flops 756326400 | bytes 5701632 | tf_op jit(solution)/shard_map/arnf,fd->arnd/dot_general | solution.py:237
  261.0 4.2 %convolution_convert_fusion = bf16[8,4,32,1536]{3,2,1,0:T(8,128)(2,1)S(1)} fusion(bf16[8,4,32,768]{3,2,1,0:T(8,128)(2,1)} %fusion.8, bf16[768,1536]{1,0:T(8,128)(2,1)S(1)} %copy-done), kind=kOutput, calls=%fused_computation.19 | convolution fusion | flops 2417491968 | bytes 7077888 | tf_op jit(solution)/shard_map/arnf,fd->arnd/dot_general | solution.py:236
  265.7 13.4 %collective-permute-start.25 = (bf16[4,37,1536]{2,1,0:T(8,128)(2,1)S(1)}, bf16[4,37,1536]{2,1,0:T(8,128)(2,1)S(1)}, u32[]{:S(2)}, u32[]{:S(2)}) collective-permute-start(bf16[4,37,1536]{2,1,0:T(8,128)(2,1)S(1)} %get-tuple-element.25), channel_id=1, source_target_pairs={{8,0},{12,4},{16,8},{20,12},{24,16},{28,20},{0,24},{4,28},{9,1},{1... | collective-permute-start | bytes 1363976 | tf_op jit(solution)/shard_map/ppermute | solution.py:37
  280.3 2.8 collective-permute-start.28
  283.1 2.9 collective-permute-start.29
  286.0 33.2 %collective-permute-done.25 = bf16[4,37,1536]{2,1,0:T(8,128)(2,1)S(1)} collective-permute-done((bf16[4,37,1536]{2,1,0:T(8,128)(2,1)S(1)}, bf16[4,37,1536]{2,1,0:T(8,128)(2,1)S(1)}, u32[]{:S(2)}, u32[]{:S(2)}) %collective-permute-start.25) | collective-permute-done | bytes 454688 | tf_op jit(solution)/shard_map/ppermute | solution.py:37
  319.5 13.3 %collective-permute-done.30 = bf16[4,37,1536]{2,1,0:T(8,128)(2,1)S(1)} collective-permute-done((bf16[4,37,1536]{2,1,0:T(8,128)(2,1)S(1)}, bf16[4,37,1536]{2,1,0:T(8,128)(2,1)S(1)}, u32[]{:S(2)}, u32[]{:S(2)}) %collective-permute-start.30) | collective-permute-done | bytes 454688 | tf_op jit(solution)/shard_map/ppermute | solution.py:37
  342.2 2.8 collective-permute-done.32
  347.0 6.3 %collective-permute-start.34 = (bf16[4,10,1,16]{3,2,1,0:T(2,128)(2,1)S(1)}, bf16[4,10,1,16]{3,2,1,0:T(2,128)(2,1)S(1)}, u32[]{:S(2)}, u32[]{:S(2)}) collective-permute-start(bf16[4,10,1,16]{3,2,1,0:T(2,128)(2,1)S(1)} %get-tuple-element.51), channel_id=1, source_target_pairs={{1,0},{2,1},{3,2},{5,4},{6,5},{7,6},{9,8},{10,9},{11,10},{13,12},{... | collective-permute-start | bytes 3848 | tf_op jit(solution)/shard_map/ppermute | solution.py:20
  (240 shorter events, 85.8 us)
Async XLA Ops:
  4.0 31.7 %collective-permute-start = (bf16[4,37,1536]{2,1,0:T(8,128)(2,1)}, bf16[4,37,1536]{2,1,0:T(8,128)(2,1)}, u32[]{:S(2)}, u32[]{:S(2)}) collective-permute-start(bf16[4,37,1536]{2,1,0:T(8,128)(2,1)} %get-tuple-element.47), channel_id=1, source_target_pairs={{0,4},{4,8},{8,12},{12,16},{16,20},{20,24},{24,28},{28,0},{1,5},{5... | collective-permute-start | bytes 1363976 | tf_op jit(solution)/shard_map/ppermute | solution.py:29
  7.6 36.5 %collective-permute-start.1 = (bf16[4,37,1536]{2,1,0:T(8,128)(2,1)}, bf16[4,37,1536]{2,1,0:T(8,128)(2,1)}, u32[]{:S(2)}, u32[]{:S(2)}) collective-permute-start(bf16[4,37,1536]{2,1,0:T(8,128)(2,1)} %get-tuple-element.47), channel_id=1, source_target_pairs={{0,8},{4,12},{8,16},{12,20},{16,24},{20,28},{24,0},{28,4},{1,9},{5... | collective-permute-start | bytes 1363976 | tf_op jit(solution)/shard_map/ppermute | solution.py:29
  9.2 36.1 %collective-permute-start.2 = (bf16[4,37,1536]{2,1,0:T(8,128)(2,1)}, bf16[4,37,1536]{2,1,0:T(8,128)(2,1)}, u32[]{:S(2)}, u32[]{:S(2)}) collective-permute-start(bf16[4,37,1536]{2,1,0:T(8,128)(2,1)} %get-tuple-element.47), channel_id=1, source_target_pairs={{0,12},{4,16},{8,20},{12,24},{16,28},{20,0},{24,4},{28,8},{1,13},{... | collective-permute-start | bytes 1363976 | tf_op jit(solution)/shard_map/ppermute | solution.py:29
  11.9 43.9 %collective-permute-start.3 = (bf16[4,37,1536]{2,1,0:T(8,128)(2,1)}, bf16[4,37,1536]{2,1,0:T(8,128)(2,1)}, u32[]{:S(2)}, u32[]{:S(2)}) collective-permute-start(bf16[4,37,1536]{2,1,0:T(8,128)(2,1)} %get-tuple-element.47), channel_id=1, source_target_pairs={{0,16},{4,20},{8,24},{12,28},{16,0},{20,4},{24,8},{28,12},{1,17},{... | collective-permute-start | bytes 1363976 | tf_op jit(solution)/shard_map/ppermute | solution.py:29
  12.8 44.1 %collective-permute-start.4 = (bf16[4,37,1536]{2,1,0:T(8,128)(2,1)}, bf16[4,37,1536]{2,1,0:T(8,128)(2,1)}, u32[]{:S(2)}, u32[]{:S(2)}) collective-permute-start(bf16[4,37,1536]{2,1,0:T(8,128)(2,1)} %get-tuple-element.47), channel_id=1, source_target_pairs={{0,20},{4,24},{8,28},{12,0},{16,4},{20,8},{24,12},{28,16},{1,21},{... | collective-permute-start | bytes 1363976 | tf_op jit(solution)/shard_map/ppermute | solution.py:29
  35.8 22.2 %collective-permute-start.5 = (bf16[4,37,1536]{2,1,0:T(8,128)(2,1)}, bf16[4,37,1536]{2,1,0:T(8,128)(2,1)S(1)}, u32[]{:S(2)}, u32[]{:S(2)}) collective-permute-start(bf16[4,37,1536]{2,1,0:T(8,128)(2,1)} %get-tuple-element.47), channel_id=1, source_target_pairs={{0,24},{4,28},{8,0},{12,4},{16,8},{20,12},{24,16},{28,20},{1,25},{... | collective-permute-start | bytes 1363976 | tf_op jit(solution)/shard_map/ppermute | solution.py:29
  44.1 14.2 %collective-permute-start.6 = (bf16[4,37,1536]{2,1,0:T(8,128)(2,1)}, bf16[4,37,1536]{2,1,0:T(8,128)(2,1)S(1)}, u32[]{:S(2)}, u32[]{:S(2)}) collective-permute-start(bf16[4,37,1536]{2,1,0:T(8,128)(2,1)} %get-tuple-element.47), channel_id=1, source_target_pairs={{0,28},{4,0},{8,4},{12,8},{16,12},{20,16},{24,20},{28,24},{1,29},{... | collective-permute-start | bytes 1363976 | tf_op jit(solution)/shard_map/ppermute | solution.py:29
  69.8 21.3 %collective-permute-start.7 = (bf16[1184,384]{1,0:T(8,128)(2,1)}, bf16[1184,384]{1,0:T(8,128)(2,1)S(1)}, u32[]{:S(2)}, u32[]{:S(2)}) collective-permute-start(bf16[1184,384]{1,0:T(8,128)(2,1)} %reshape.330.refs_0_), channel_id=1, source_target_pairs={{0,1},{1,2},{2,3},{3,0},{4,5},{5,6},{6,7},{7,4},{8,9},{9,10},{10,1... | collective-permute-start | bytes 2727944 | tf_op jit(solution)/shard_map/ppermute | solution.py:47
  71.4 40.8 %collective-permute-start.8 = (bf16[1184,384]{1,0:T(8,128)(2,1)}, bf16[1184,384]{1,0:T(8,128)(2,1)}, u32[]{:S(2)}, u32[]{:S(2)}) collective-permute-start(bf16[1184,384]{1,0:T(8,128)(2,1)} %reshape.330.refs_0_), channel_id=1, source_target_pairs={{0,2},{1,3},{2,0},{3,1},{4,6},{5,7},{6,4},{7,5},{8,10},{9,11},{10,... | collective-permute-start | bytes 2727944 | tf_op jit(solution)/shard_map/ppermute | solution.py:47
  72.5 40.2 %collective-permute-start.9 = (bf16[1184,384]{1,0:T(8,128)(2,1)}, bf16[1184,384]{1,0:T(8,128)(2,1)}, u32[]{:S(2)}, u32[]{:S(2)}) collective-permute-start(bf16[1184,384]{1,0:T(8,128)(2,1)} %reshape.330.refs_0_), channel_id=1, source_target_pairs={{0,3},{1,0},{2,1},{3,2},{4,7},{5,4},{6,5},{7,6},{8,11},{9,8},{10,9... | collective-permute-start | bytes 2727944 | tf_op jit(solution)/shard_map/ppermute | solution.py:47
  132.4 20.1 %collective-permute-start.10 = (bf16[4,37,1536]{2,1,0:T(8,128)(2,1)S(1)}, bf16[4,37,1536]{2,1,0:T(8,128)(2,1)S(1)}, u32[]{:S(2)}, u32[]{:S(2)}) collective-permute-start(bf16[4,37,1536]{2,1,0:T(8,128)(2,1)S(1)} %get-tuple-element.31), channel_id=1, source_target_pairs={{4,0},{8,4},{12,8},{16,12},{20,16},{24,20},{28,24},{0,28},{5,1},{9... | collective-permute-start | bytes 1363976 | tf_op jit(solution)/shard_map/ppermute | solution.py:37
  141.4 34.2 %collective-permute-start.11 = (bf16[4,37,1536]{2,1,0:T(8,128)(2,1)S(1)}, bf16[4,37,1536]{2,1,0:T(8,128)(2,1)S(1)}, u32[]{:S(2)}, u32[]{:S(2)}) collective-permute-start(bf16[4,37,1536]{2,1,0:T(8,128)(2,1)S(1)} %get-tuple-element.32), channel_id=1, source_target_pairs={{8,0},{12,4},{16,8},{20,12},{24,16},{28,20},{0,24},{4,28},{9,1},{1... | collective-permute-start | bytes 1363976 | tf_op jit(solution)/shard_map/ppermute | solution.py:37
  143.6 32.6 %collective-permute-start.12 = (bf16[4,37,1536]{2,1,0:T(8,128)(2,1)S(1)}, bf16[4,37,1536]{2,1,0:T(8,128)(2,1)S(1)}, u32[]{:S(2)}, u32[]{:S(2)}) collective-permute-start(bf16[4,37,1536]{2,1,0:T(8,128)(2,1)S(1)} %get-tuple-element.33), channel_id=1, source_target_pairs={{12,0},{16,4},{20,8},{24,12},{28,16},{0,20},{4,24},{8,28},{13,1},{... | collective-permute-start | bytes 1363976 | tf_op jit(solution)/shard_map/ppermute | solution.py:37
  146.9 29.3 %collective-permute-start.13 = (bf16[4,37,1536]{2,1,0:T(8,128)(2,1)S(1)}, bf16[4,37,1536]{2,1,0:T(8,128)(2,1)S(1)}, u32[]{:S(2)}, u32[]{:S(2)}) collective-permute-start(bf16[4,37,1536]{2,1,0:T(8,128)(2,1)S(1)} %get-tuple-element.34), channel_id=1, source_target_pairs={{16,0},{20,4},{24,8},{28,12},{0,16},{4,20},{8,24},{12,28},{17,1},{... | collective-permute-start | bytes 1363976 | tf_op jit(solution)/shard_map/ppermute | solution.py:37
  146.9 30.4 %collective-permute-start.14 = (bf16[4,37,1536]{2,1,0:T(8,128)(2,1)S(1)}, bf16[4,37,1536]{2,1,0:T(8,128)(2,1)S(1)}, u32[]{:S(2)}, u32[]{:S(2)}) collective-permute-start(bf16[4,37,1536]{2,1,0:T(8,128)(2,1)S(1)} %get-tuple-element.35), channel_id=1, source_target_pairs={{20,0},{24,4},{28,8},{0,12},{4,16},{8,20},{12,24},{16,28},{21,1},{... | collective-permute-start | bytes 1363976 | tf_op jit(solution)/shard_map/ppermute | solution.py:37
  152.4 28.5 %collective-permute-start.15 = (bf16[4,37,1536]{2,1,0:T(8,128)(2,1)S(1)}, bf16[4,37,1536]{2,1,0:T(8,128)(2,1)S(1)}, u32[]{:S(2)}, u32[]{:S(2)}) collective-permute-start(bf16[4,37,1536]{2,1,0:T(8,128)(2,1)S(1)} %get-tuple-element.37), channel_id=1, source_target_pairs={{24,0},{28,4},{0,8},{4,12},{8,16},{12,20},{16,24},{20,28},{25,1},{... | collective-permute-start | bytes 1363976 | tf_op jit(solution)/shard_map/ppermute | solution.py:37
  175.6 23.0 %collective-permute-start.16 = (bf16[4,37,1536]{2,1,0:T(8,128)(2,1)S(1)}, bf16[4,37,1536]{2,1,0:T(8,128)(2,1)S(1)}, u32[]{:S(2)}, u32[]{:S(2)}) collective-permute-start(bf16[4,37,1536]{2,1,0:T(8,128)(2,1)S(1)} %get-tuple-element.36), channel_id=1, source_target_pairs={{28,0},{0,4},{4,8},{8,12},{12,16},{16,20},{20,24},{24,28},{29,1},{... | collective-permute-start | bytes 1363976 | tf_op jit(solution)/shard_map/ppermute | solution.py:37
  200.5 15.5 %collective-permute-start.17 = (bf16[4,37,1536]{2,1,0:T(8,128)(2,1)S(1)}, bf16[4,37,1536]{2,1,0:T(8,128)(2,1)S(1)}, u32[]{:S(2)}, u32[]{:S(2)}) collective-permute-start(bf16[4,37,1536]{2,1,0:T(8,128)(2,1)S(1)} %pad_maximum_fusion.5), channel_id=1, source_target_pairs={{0,4},{4,8},{8,12},{12,16},{16,20},{20,24},{24,28},{28,0},{1,5},{5... | collective-permute-start | bytes 1363976 | tf_op jit(solution)/shard_map/ppermute | solution.py:29
  200.6 36.3 %collective-permute-start.18 = (bf16[4,37,1536]{2,1,0:T(8,128)(2,1)S(1)}, bf16[4,37,1536]{2,1,0:T(8,128)(2,1)S(1)}, u32[]{:S(2)}, u32[]{:S(2)}) collective-permute-start(bf16[4,37,1536]{2,1,0:T(8,128)(2,1)S(1)} %pad_maximum_fusion.5), channel_id=1, source_target_pairs={{0,8},{4,12},{8,16},{12,20},{16,24},{20,28},{24,0},{28,4},{1,9},{5... | collective-permute-start | bytes 1363976 | tf_op jit(solution)/shard_map/ppermute | solution.py:29
  200.7 36.3 %collective-permute-start.19 = (bf16[4,37,1536]{2,1,0:T(8,128)(2,1)S(1)}, bf16[4,37,1536]{2,1,0:T(8,128)(2,1)S(1)}, u32[]{:S(2)}, u32[]{:S(2)}) collective-permute-start(bf16[4,37,1536]{2,1,0:T(8,128)(2,1)S(1)} %pad_maximum_fusion.5), channel_id=1, source_target_pairs={{0,12},{4,16},{8,20},{12,24},{16,28},{20,0},{24,4},{28,8},{1,13},{... | collective-permute-start | bytes 1363976 | tf_op jit(solution)/shard_map/ppermute | solution.py:29
  204.8 43.6 %collective-permute-start.20 = (bf16[4,37,1536]{2,1,0:T(8,128)(2,1)S(1)}, bf16[4,37,1536]{2,1,0:T(8,128)(2,1)S(1)}, u32[]{:S(2)}, u32[]{:S(2)}) collective-permute-start(bf16[4,37,1536]{2,1,0:T(8,128)(2,1)S(1)} %pad_maximum_fusion.5), channel_id=1, source_target_pairs={{0,16},{4,20},{8,24},{12,28},{16,0},{20,4},{24,8},{28,12},{1,17},{... | collective-permute-start | bytes 1363976 | tf_op jit(solution)/shard_map/ppermute | solution.py:29
  206.8 41.6 %collective-permute-start.21 = (bf16[4,37,1536]{2,1,0:T(8,128)(2,1)S(1)}, bf16[4,37,1536]{2,1,0:T(8,128)(2,1)S(1)}, u32[]{:S(2)}, u32[]{:S(2)}) collective-permute-start(bf16[4,37,1536]{2,1,0:T(8,128)(2,1)S(1)} %pad_maximum_fusion.5), channel_id=1, source_target_pairs={{0,20},{4,24},{8,28},{12,0},{16,4},{20,8},{24,12},{28,16},{1,21},{... | collective-permute-start | bytes 1363976 | tf_op jit(solution)/shard_map/ppermute | solution.py:29
  216.0 33.2 %collective-permute-start.22 = (bf16[4,37,1536]{2,1,0:T(8,128)(2,1)S(1)}, bf16[4,37,1536]{2,1,0:T(8,128)(2,1)S(1)}, u32[]{:S(2)}, u32[]{:S(2)}) collective-permute-start(bf16[4,37,1536]{2,1,0:T(8,128)(2,1)S(1)} %pad_maximum_fusion.5), channel_id=1, source_target_pairs={{0,24},{4,28},{8,0},{12,4},{16,8},{20,12},{24,16},{28,20},{1,25},{... | collective-permute-start | bytes 1363976 | tf_op jit(solution)/shard_map/ppermute | solution.py:29
  236.9 13.0 %collective-permute-start.23 = (bf16[4,37,1536]{2,1,0:T(8,128)(2,1)S(1)}, bf16[4,37,1536]{2,1,0:T(8,128)(2,1)S(1)}, u32[]{:S(2)}, u32[]{:S(2)}) collective-permute-start(bf16[4,37,1536]{2,1,0:T(8,128)(2,1)S(1)} %pad_maximum_fusion.5), channel_id=1, source_target_pairs={{0,28},{4,0},{8,4},{12,8},{16,12},{20,16},{24,20},{28,24},{1,29},{... | collective-permute-start | bytes 1363976 | tf_op jit(solution)/shard_map/ppermute | solution.py:29
  265.7 17.5 %collective-permute-start.24 = (bf16[4,37,1536]{2,1,0:T(8,128)(2,1)S(1)}, bf16[4,37,1536]{2,1,0:T(8,128)(2,1)S(1)}, u32[]{:S(2)}, u32[]{:S(2)}) collective-permute-start(bf16[4,37,1536]{2,1,0:T(8,128)(2,1)S(1)} %get-tuple-element.24), channel_id=1, source_target_pairs={{4,0},{8,4},{12,8},{16,12},{20,16},{24,20},{28,24},{0,28},{5,1},{9... | collective-permute-start | bytes 1363976 | tf_op jit(solution)/shard_map/ppermute | solution.py:37
  265.7 53.5 %collective-permute-start.25 = (bf16[4,37,1536]{2,1,0:T(8,128)(2,1)S(1)}, bf16[4,37,1536]{2,1,0:T(8,128)(2,1)S(1)}, u32[]{:S(2)}, u32[]{:S(2)}) collective-permute-start(bf16[4,37,1536]{2,1,0:T(8,128)(2,1)S(1)} %get-tuple-element.25), channel_id=1, source_target_pairs={{8,0},{12,4},{16,8},{20,12},{24,16},{28,20},{0,24},{4,28},{9,1},{1... | collective-permute-start | bytes 1363976 | tf_op jit(solution)/shard_map/ppermute | solution.py:37
  279.2 40.3 %collective-permute-start.26 = (bf16[4,37,1536]{2,1,0:T(8,128)(2,1)S(1)}, bf16[4,37,1536]{2,1,0:T(8,128)(2,1)S(1)}, u32[]{:S(2)}, u32[]{:S(2)}) collective-permute-start(bf16[4,37,1536]{2,1,0:T(8,128)(2,1)S(1)} %get-tuple-element.26), channel_id=1, source_target_pairs={{12,0},{16,4},{20,8},{24,12},{28,16},{0,20},{4,24},{8,28},{13,1},{... | collective-permute-start | bytes 1363976 | tf_op jit(solution)/shard_map/ppermute | solution.py:37
  279.3 40.2 %collective-permute-start.27 = (bf16[4,37,1536]{2,1,0:T(8,128)(2,1)S(1)}, bf16[4,37,1536]{2,1,0:T(8,128)(2,1)S(1)}, u32[]{:S(2)}, u32[]{:S(2)}) collective-permute-start(bf16[4,37,1536]{2,1,0:T(8,128)(2,1)S(1)} %get-tuple-element.27), channel_id=1, source_target_pairs={{16,0},{20,4},{24,8},{28,12},{0,16},{4,20},{8,24},{12,28},{17,1},{... | collective-permute-start | bytes 1363976 | tf_op jit(solution)/shard_map/ppermute | solution.py:37
  280.3 39.2 %collective-permute-start.28 = (bf16[4,37,1536]{2,1,0:T(8,128)(2,1)S(1)}, bf16[4,37,1536]{2,1,0:T(8,128)(2,1)S(1)}, u32[]{:S(2)}, u32[]{:S(2)}) collective-permute-start(bf16[4,37,1536]{2,1,0:T(8,128)(2,1)S(1)} %get-tuple-element.28), channel_id=1, source_target_pairs={{20,0},{24,4},{28,8},{0,12},{4,16},{8,20},{12,24},{16,28},{21,1},{... | collective-permute-start | bytes 1363976 | tf_op jit(solution)/shard_map/ppermute | solution.py:37
  283.1 36.4 %collective-permute-start.29 = (bf16[4,37,1536]{2,1,0:T(8,128)(2,1)S(1)}, bf16[4,37,1536]{2,1,0:T(8,128)(2,1)S(1)}, u32[]{:S(2)}, u32[]{:S(2)}) collective-permute-start(bf16[4,37,1536]{2,1,0:T(8,128)(2,1)S(1)} %get-tuple-element.30), channel_id=1, source_target_pairs={{24,0},{28,4},{0,8},{4,12},{8,16},{12,20},{16,24},{20,28},{25,1},{... | collective-permute-start | bytes 1363976 | tf_op jit(solution)/shard_map/ppermute | solution.py:37
  319.3 13.6 %collective-permute-start.30 = (bf16[4,37,1536]{2,1,0:T(8,128)(2,1)S(1)}, bf16[4,37,1536]{2,1,0:T(8,128)(2,1)S(1)}, u32[]{:S(2)}, u32[]{:S(2)}) collective-permute-start(bf16[4,37,1536]{2,1,0:T(8,128)(2,1)S(1)} %get-tuple-element.29), channel_id=1, source_target_pairs={{28,0},{0,4},{4,8},{8,12},{12,16},{16,20},{20,24},{24,28},{29,1},{... | collective-permute-start | bytes 1363976 | tf_op jit(solution)/shard_map/ppermute | solution.py:37
  345.1 8.7 %collective-permute-start.33 = (bf16[4,10,1,16]{3,2,1,0:T(2,128)(2,1)S(1)}, bf16[4,10,1,16]{3,2,1,0:T(2,128)(2,1)S(1)}, u32[]{:S(2)}, u32[]{:S(2)}) collective-permute-start(bf16[4,10,1,16]{3,2,1,0:T(2,128)(2,1)S(1)} %get-tuple-element.50), channel_id=1, source_target_pairs={{0,1},{1,2},{2,3},{4,5},{5,6},{6,7},{8,9},{9,10},{10,11},{12,13},{... | collective-permute-start | bytes 3848 | tf_op jit(solution)/shard_map/ppermute | solution.py:17
  (40 other events, 702.5 us)

commit v2 on v1

--- a/solution.py
+++ b/solution.py
@@ -78,6 +78,16 @@
         out_specs=pl.BlockSpec((None, rows, tile), lambda r, h: (r, 0, h)),
         out_shape=jax.ShapeDtypeStruct((requests, rows, lanes), jnp.bfloat16),
     )(query_rows, *pair_blocks, usable)
+
+
+def return_slots(parts, axis):
+    count = lax.axis_size(axis)
+    total = parts[0].astype(jnp.float32)
+    for shift in range(1, count):
+        total = total + lax.ppermute(
+            parts[shift], axis, [((i + shift) % count, i) for i in range(count)]
+        ).astype(jnp.float32)
+    return total
 
 
 def per_request(vector, values, axis):
@@ -224,18 +234,24 @@
     text_mid = own_f[:, image_tile:] + per_request(text_mod[:, 2], own_f, 0) * attn[:, image_tile:]
     image_local = modulate(image_mid, image_mod[:, 3], image_mod[:, 4], 0).astype(jnp.bfloat16)
     text_local = modulate(text_mid, text_mod[:, 3], text_mod[:, 4], 0).astype(jnp.bfloat16)
-    ff_in = gather_slots(jnp.concatenate([image_local, text_local], 1), "head")
-    image_hid = jax.nn.gelu(
-        jnp.einsum("arnd,df->arnf", ff_in[:, :, :image_tile], image_up, preferred_element_type=jnp.float32),
-        approximate=True,
-    ).astype(jnp.bfloat16)
-    text_hid = jax.nn.gelu(
-        jnp.einsum("arnd,df->arnf", ff_in[:, :, image_tile:], text_up, preferred_element_type=jnp.float32),
-        approximate=True,
-    ).astype(jnp.bfloat16)
-    image_back = jnp.einsum("arnf,fd->arnd", image_hid, image_down, preferred_element_type=jnp.float32)
-    text_back = jnp.einsum("arnf,fd->arnd", text_hid, text_down, preferred_element_type=jnp.float32)
-    mlp = scatter_slots(jnp.concatenate([image_back, text_back], 2).astype(jnp.bfloat16), "head")
+    ff_blocks = send_slots(jnp.concatenate([image_local, text_local], 1), "head")
+    ff_parts = []
+    half = groups // 2
+    for first in (0, half):
+        ff_in = jnp.stack(ff_blocks[first:first + half])
+        image_hid = jax.nn.gelu(
+            jnp.einsum("arnd,df->arnf", ff_in[:, :, :image_tile], image_up, preferred_element_type=jnp.float32),
+            approximate=True,
+        ).astype(jnp.bfloat16)
+        text_hid = jax.nn.gelu(
+            jnp.einsum("arnd,df->arnf", ff_in[:, :, image_tile:], text_up, preferred_element_type=jnp.float32),
+            approximate=True,
+        ).astype(jnp.bfloat16)
+        image_back = jnp.einsum("arnf,fd->arnd", image_hid, image_down, preferred_element_type=jnp.float32)
+        text_back = jnp.einsum("arnf,fd->arnd", text_hid, text_down, preferred_element_type=jnp.float32)
+        back = jnp.concatenate([image_back, text_back], 2).astype(jnp.bfloat16)
+        ff_parts.extend(back[k] for k in range(half))
+    mlp = return_slots(ff_parts, "head")
     image_out = image_mid + per_request(image_mod[:, 5], image_mid, 0) * mlp[:, :image_tile]
     text_out = text_mid + per_request(text_mod[:, 5], text_mid, 0) * mlp[:, image_tile:]
     image_states = image_out.reshape(requests, tile_rows, tile_cols, model_width).astype(jnp.bfloat16)

time: 359 us -> 369 us (1.028); the launches traced: 357 us -> 363 us
  waiting for transfers between devices: 177 us -> 158 us
  starting transfers between devices: 80.5 us -> 89.8 us
  matrix products: 36.7 us -> 45.5 us
  other arithmetic: 20.1 us -> 27.9 us
    ppermute x14 -> x7, waiting for transfers between devices: 92.7 us -> 42 us  [scatter_slots(): lax.ppermute(partial[shift], axis, [((i + shift) % count, i) for i in ran...]
    ppermute x0 -> x7, waiting for transfers between devices: none -> 38.1 us  [return_slots(): lax.ppermute(parts[shift], axis, [((i + shift) % count, i) for i in range...]
    ppermute x14 -> x7, waiting for transfers between devices: 53.7 us -> 20.5 us  [gather_slots(): lax.ppermute(block, axis, [(i, (i + shift) % count) for i in range(count)])]
    ppermute x3 -> x10, waiting for transfers between devices: 27.6 us -> 50.1 us  [send_slots(): lax.ppermute(block, axis, [(i, (i + shift) % count) for i in range(count)])]
    ppermute x14 -> x7, starting transfers between devices: 40.4 us -> 21 us  [scatter_slots(): lax.ppermute(partial[shift], axis, [((i + shift) % count, i) for i in ran...]
    ppermute x3 -> x10, starting transfers between devices: 2.89 us -> 21.3 us  [send_slots(): lax.ppermute(block, axis, [(i, (i + shift) % count) for i in range(count)])]
    ppermute x0 -> x7, starting transfers between devices: none -> 13.4 us  [return_slots(): lax.ppermute(parts[shift], axis, [((i + shift) % count, i) for i in range...]
    ppermute x2, starting transfers between devices: 3.2 us -> 16 us  [extended(): lax.ppermute(lax.slice_in_dim(block, block.shape[dim] - width, None, axis...]
  transfers between devices with their start and end apart: 35 -> 35, of which waited for: 20 -> 18; matrix products, arithmetic and copies ran while one was open for 11% -> 13% of each run, Pallas kernels for 0% -> 0%
where the time goes in v2:
time: 369 us; the launch traced here: 363 us
  waiting for transfers between devices  158 us (43%)
  starting transfers between devices  89.8 us (24%)
  matrix products  45.5 us (12%)
  other arithmetic  27.9 us (8%)
  local copies, waits for them, and re-layouts  25.8 us (7%)
  Pallas kernels  14.2 us (4%)
    ppermute x10, waiting for transfers between devices, send_slots(): lax.ppermute(block, axis, [(i, (i + shift) % count) for i in range(count)])  50.1 us
    ppermute x7, waiting for transfers between devices, scatter_slots(): lax.ppermute(partial[shift], axis, [((i + shift) % count, i) for i in ran...  42 us
    ppermute x7, waiting for transfers between devices, return_slots(): lax.ppermute(parts[shift], axis, [((i + shift) % count, i) for i in range...  38.1 us
    ppermute x10, starting transfers between devices, send_slots(): lax.ppermute(block, axis, [(i, (i + shift) % count) for i in range(count)])  21.3 us
    ppermute x7, starting transfers between devices, scatter_slots(): lax.ppermute(partial[shift], axis, [((i + shift) % count, i) for i in ran...  21 us
    ppermute x7, waiting for transfers between devices, gather_slots(): lax.ppermute(block, axis, [(i, (i + shift) % count) for i in range(count)])  20.5 us
    ppermute x2, starting transfers between devices, extended(): lax.ppermute(lax.slice_in_dim(block, block.shape[dim] - width, None, axis...  16 us
    ppermute x7, starting transfers between devices, gather_slots(): lax.ppermute(block, axis, [(i, (i + shift) % count) for i in range(count)])  14.8 us
  transfers between devices with their start and end apart: 35, of which 18 were waited for; matrix products, arithmetic and copies ran while one was open for 13% of the time, Pallas kernels for 0%

profile of v2, /device:TPU:1, one launch (start us, length us, event | category | flops | bytes accessed | tf_op | source)
XLA Modules:
  0.0 362.6 jit_solution(9407113179998745686)
XLA Ops:
  4.0 3.6 collective-permute-start
  12.8 5.2 %collective-permute-start.4 = (bf16[4,37,1536]{2,1,0:T(8,128)(2,1)}, bf16[4,37,1536]{2,1,0:T(8,128)(2,1)}, u32[]{:S(2)}, u32[]{:S(2)}) collective-permute-start(bf16[4,37,1536]{2,1,0:T(8,128)(2,1)} %get-tuple-element.49), channel_id=1, source_target_pairs={{0,20},{4,24},{8,28},{12,0},{16,4},{20,8},{24,12},{28,16},{1,21},{... | collective-permute-start | bytes 1363976 | tf_op jit(solution)/shard_map/ppermute | solution.py:29
  33.3 10.8 %collective-permute-done.1 = bf16[4,37,1536]{2,1,0:T(8,128)(2,1)} collective-permute-done((bf16[4,37,1536]{2,1,0:T(8,128)(2,1)}, bf16[4,37,1536]{2,1,0:T(8,128)(2,1)}, u32[]{:S(2)}, u32[]{:S(2)}) %collective-permute-start.1) | collective-permute-done | bytes 454688 | tf_op jit(solution)/shard_map/ppermute | solution.py:29
  46.4 9.3 %collective-permute-done.3 = bf16[4,37,1536]{2,1,0:T(8,128)(2,1)} collective-permute-done((bf16[4,37,1536]{2,1,0:T(8,128)(2,1)}, bf16[4,37,1536]{2,1,0:T(8,128)(2,1)}, u32[]{:S(2)}, u32[]{:S(2)}) %collective-permute-start.3) | collective-permute-done | bytes 454688 | tf_op jit(solution)/shard_map/ppermute | solution.py:29
  65.0 3.3 select_convert_fusion
  78.4 4.0 %fusion.305 = f32[8,4,32,384]{3,2,1,0:T(8,128)S(1)} fusion(bf16[1536,384,1,1]{0,1,3,2:T(8,128)(2,1)S(1)} %bitcast.323, f32[8,4,37,1536]{3,2,1,0:T(8,128)} %copy-done.1, f32[4,1536]{1,0:T(4,128)S(1)} %get-tuple-element.62, f32[4,1536]{1,0:T(4,128)S(1)} %bitcast.336, f32[8,4,32]{2,1,0:T(4,128)S(1)} %add_rsqrt_fusion.1, ...), kind=kOutput, calls=%fused_computation.412 | convolution fusion | flops 1215823872 | bytes 9101312 | tf_op jit(solution)/shard_map/arnd,de->arne/dot_general | solution.py:139
  82.5 3.2 multiply_convert_fusion
  87.2 5.9 %collective-permute-done.7.refs_1_ = bf16[1184,384]{1,0:T(8,128)(2,1)} collective-permute-done((bf16[1184,384]{1,0:T(8,128)(2,1)}, bf16[1184,384]{1,0:T(8,128)(2,1)}, u32[]{:S(2)}, u32[]{:S(2)}) %collective-permute-start.7) | collective-permute-done | bytes 909344 | tf_op jit(solution)/shard_map/ppermute | solution.py:47
  93.1 21.1 %collective-permute-done.8.refs_2_ = bf16[1184,384]{1,0:T(8,128)(2,1)} collective-permute-done((bf16[1184,384]{1,0:T(8,128)(2,1)}, bf16[1184,384]{1,0:T(8,128)(2,1)}, u32[]{:S(2)}, u32[]{:S(2)}) %collective-permute-start.8) | collective-permute-done | bytes 909344 | tf_op jit(solution)/shard_map/ppermute | solution.py:47
  114.7 14.2 %shard_map.219 = bf16[4,296,384]{2,1,0:T(8,128)(2,1)} custom-call(bf16[4,296,384]{2,1,0:T(8,128)(2,1)} %copy.103.query_ref, bf16[1184,384]{1,0:T(8,128)(2,1)} %reshape.330.refs_0_, bf16[1184,384]{1,0:T(8,128)(2,1)} %collective-permute-done.7.refs_1_, bf16[1184,384]{1,0:T(8,128)(2,1)} %collective-permute-done.8.refs_2_, ...), custom_call_target="tpu_custom_call" | custom-call | tf_op jit(solution)/shard_map/pallas_call | solution.py:72
  134.3 7.7 %collective-permute-start.10 = (bf16[4,37,1536]{2,1,0:T(8,128)(2,1)S(1)}, bf16[4,37,1536]{2,1,0:T(8,128)(2,1)S(1)}, u32[]{:S(2)}, u32[]{:S(2)}) collective-permute-start(bf16[4,37,1536]{2,1,0:T(8,128)(2,1)S(1)} %get-tuple-element.24), channel_id=1, source_target_pairs={{4,0},{8,4},{12,8},{16,12},{20,16},{24,20},{28,24},{0,28},{5,1},{9... | collective-permute-start | bytes 1363976 | tf_op jit(solution)/shard_map/ppermute | solution.py:37
  142.1 3.5 collective-permute-start.11
  145.5 3.3 collective-permute-start.12
  152.8 4.6 %collective-permute-start.15 = (bf16[4,37,1536]{2,1,0:T(8,128)(2,1)S(1)}, bf16[4,37,1536]{2,1,0:T(8,128)(2,1)S(1)}, u32[]{:S(2)}, u32[]{:S(2)}) collective-permute-start(bf16[4,37,1536]{2,1,0:T(8,128)(2,1)S(1)} %get-tuple-element.30), channel_id=1, source_target_pairs={{24,0},{28,4},{0,8},{4,12},{8,16},{12,20},{16,24},{20,28},{25,1},{... | collective-permute-start | bytes 1363976 | tf_op jit(solution)/shard_map/ppermute | solution.py:37
  157.4 28.8 %collective-permute-done.11 = bf16[4,37,1536]{2,1,0:T(8,128)(2,1)S(1)} collective-permute-done((bf16[4,37,1536]{2,1,0:T(8,128)(2,1)S(1)}, bf16[4,37,1536]{2,1,0:T(8,128)(2,1)S(1)}, u32[]{:S(2)}, u32[]{:S(2)}) %collective-permute-start.11) | collective-permute-done | bytes 454688 | tf_op jit(solution)/shard_map/ppermute | solution.py:37
  186.3 3.2 collective-permute-done.15
  189.5 8.0 %collective-permute-done.16 = bf16[4,37,1536]{2,1,0:T(8,128)(2,1)S(1)} collective-permute-done((bf16[4,37,1536]{2,1,0:T(8,128)(2,1)S(1)}, bf16[4,37,1536]{2,1,0:T(8,128)(2,1)S(1)}, u32[]{:S(2)}, u32[]{:S(2)}) %collective-permute-start.16) | collective-permute-done | bytes 454688 | tf_op jit(solution)/shard_map/ppermute | solution.py:37
  200.2 5.2 %collective-permute-start.19 = (bf16[4,37,1536]{2,1,0:T(8,128)(2,1)}, bf16[4,37,1536]{2,1,0:T(8,128)(2,1)S(1)}, u32[]{:S(2)}, u32[]{:S(2)}) collective-permute-start(bf16[4,37,1536]{2,1,0:T(8,128)(2,1)} %get-tuple-element.47), channel_id=1, source_target_pairs={{0,12},{4,16},{8,20},{12,24},{16,28},{20,0},{24,4},{28,8},{1,13},{... | collective-permute-start | bytes 1363976 | tf_op jit(solution)/shard_map/ppermute | solution.py:47
  209.3 7.7 %collective-permute-done.17 = bf16[4,37,1536]{2,1,0:T(8,128)(2,1)S(1)} collective-permute-done((bf16[4,37,1536]{2,1,0:T(8,128)(2,1)}, bf16[4,37,1536]{2,1,0:T(8,128)(2,1)S(1)}, u32[]{:S(2)}, u32[]{:S(2)}) %collective-permute-start.17) | collective-permute-done | bytes 454688 | tf_op jit(solution)/shard_map/ppermute | solution.py:47
  218.0 13.1 %collective-permute-done.18 = bf16[4,37,1536]{2,1,0:T(8,128)(2,1)S(1)} collective-permute-done((bf16[4,37,1536]{2,1,0:T(8,128)(2,1)}, bf16[4,37,1536]{2,1,0:T(8,128)(2,1)S(1)}, u32[]{:S(2)}, u32[]{:S(2)}) %collective-permute-start.18) | collective-permute-done | bytes 454688 | tf_op jit(solution)/shard_map/ppermute | solution.py:47
  231.0 8.9 %collective-permute-start.26 = (bf16[4,37,1536]{2,1,0:T(8,128)(2,1)}, bf16[4,37,1536]{2,1,0:T(8,128)(2,1)}, u32[]{:S(2)}, u32[]{:S(2)}) collective-permute-start(bf16[4,37,1536]{2,1,0:T(8,128)(2,1)} %get-tuple-element.47), channel_id=1, source_target_pairs={{0,28},{4,0},{8,4},{12,8},{16,12},{20,16},{24,20},{28,24},{1,29},{... | collective-permute-start | bytes 1363976 | tf_op jit(solution)/shard_map/ppermute | solution.py:47
  242.4 3.9 %convolution_convert_fusion.5 = bf16[4,4,5,1536]{3,2,1,0:T(8,128)(2,1)S(1)} fusion(bf16[768,1536]{1,0:T(8,128)(2,1)} %param.37, bf16[1536,768]{1,0:T(8,128)(2,1)} %param.35, bf16[1,4,37,1536]{3,2,1,0:T(8,128)(2,1)} %bitcast.316, bf16[1,4,37,1536]{3,2,1,0:T(8,128)(2,1)} %bitcast.314, bf16[1,4,37,1536]{3,2,1,0:T(8,128)(2,1)} %bitcast.312, ...), kind=kOutput, calls=%fused_computation.30 | convolution fusion | flops 379146240 | bytes 6782976 | tf_op jit(solution)/shard_map/arnf,fd->arnd/dot_general | solution.py:251
  248.2 4.6 %convolution_convert_fusion.4 = bf16[4,4,5,1536]{3,2,1,0:T(8,128)(2,1)} fusion(bf16[768,1536]{1,0:T(8,128)(2,1)} %param.37, bf16[1536,768]{1,0:T(8,128)(2,1)} %param.35, bf16[1,4,37,1536]{3,2,1,0:T(8,128)(2,1)} %bitcast.84, bf16[1,4,37,1536]{3,2,1,0:T(8,128)(2,1)} %bitcast.83, bf16[1,4,37,1536]{3,2,1,0:T(8,128)(2,1)} %bitcast.82, ...), kind=kOutput, calls=%fused_computation.29 | convolution fusion | flops 379146240 | bytes 6782976 | tf_op jit(solution)/shard_map/arnf,fd->arnd/dot_general | solution.py:251
  255.8 6.5 %convolution_convert_fusion.2 = bf16[4,4,32,1536]{3,2,1,0:T(8,128)(2,1)} fusion(bf16[768,1536]{1,0:T(8,128)(2,1)S(1)} %copy-done, bf16[1536,768]{1,0:T(8,128)(2,1)} %param.34, bf16[4,4,37,1536]{3,2,1,0:T(8,128)(2,1)} %pad_maximum_fusion), kind=kOutput, calls=%fused_computation.27 | convolution fusion | flops 2420244480 | bytes 7864320 | tf_op jit(solution)/shard_map/arnf,fd->arnd/dot_general | solution.py:250
  264.8 3.4 collective-permute-start.20
  268.2 4.7 %collective-permute-start.21 = (bf16[4,37,1536]{2,1,0:T(8,128)(2,1)}, bf16[4,37,1536]{2,1,0:T(8,128)(2,1)}, u32[]{:S(2)}, u32[]{:S(2)}) collective-permute-start(bf16[4,37,1536]{2,1,0:T(8,128)(2,1)} %get-tuple-element.33), channel_id=1, source_target_pairs={{8,0},{12,4},{16,8},{20,12},{24,16},{28,20},{0,24},{4,28},{9,1},{1... | collective-permute-start | bytes 1363976 | tf_op jit(solution)/shard_map/ppermute | solution.py:87
  273.0 6.6 %convolution_convert_fusion.1 = bf16[4,4,32,1536]{3,2,1,0:T(8,128)(2,1)} fusion(bf16[768,1536]{1,0:T(8,128)(2,1)S(1)} %copy-done, bf16[1536,768]{1,0:T(8,128)(2,1)} %param.34, bf16[4,4,37,1536]{3,2,1,0:T(8,128)(2,1)} %pad_maximum_fusion.1), kind=kOutput, calls=%fused_computation.26 | convolution fusion | flops 2420244480 | bytes 7864320 | tf_op jit(solution)/shard_map/arnf,fd->arnd/dot_general | solution.py:250
  286.5 24.0 %collective-permute-done.21 = bf16[4,37,1536]{2,1,0:T(8,128)(2,1)} collective-permute-done((bf16[4,37,1536]{2,1,0:T(8,128)(2,1)}, bf16[4,37,1536]{2,1,0:T(8,128)(2,1)}, u32[]{:S(2)}, u32[]{:S(2)}) %collective-permute-start.21) | collective-permute-done | bytes 454688 | tf_op jit(solution)/shard_map/ppermute | solution.py:87
  310.6 4.6 %collective-permute-done.27 = bf16[4,37,1536]{2,1,0:T(8,128)(2,1)S(1)} collective-permute-done((bf16[4,37,1536]{2,1,0:T(8,128)(2,1)S(1)}, bf16[4,37,1536]{2,1,0:T(8,128)(2,1)S(1)}, u32[]{:S(2)}, u32[]{:S(2)}) %collective-permute-start.27) | collective-permute-done | bytes 454688 | tf_op jit(solution)/shard_map/ppermute | solution.py:87
  315.2 9.5 %collective-permute-done.29 = bf16[4,37,1536]{2,1,0:T(8,128)(2,1)S(1)} collective-permute-done((bf16[4,37,1536]{2,1,0:T(8,128)(2,1)S(1)}, bf16[4,37,1536]{2,1,0:T(8,128)(2,1)S(1)}, u32[]{:S(2)}, u32[]{:S(2)}) %collective-permute-start.29) | collective-permute-done | bytes 454688 | tf_op jit(solution)/shard_map/ppermute | solution.py:87
  335.5 4.3 %collective-permute-done.32 = bf16[4,1,16,16]{3,2,1,0:T(8,128)(2,1)S(1)} collective-permute-done((bf16[4,1,16,16]{3,2,1,0:T(8,128)(2,1)S(1)}, bf16[4,1,16,16]{3,2,1,0:T(8,128)(2,1)S(1)}, u32[]{:S(2)}, u32[]{:S(2)}) %collective-permute-start.32) | collective-permute-done | bytes 2080 | tf_op jit(solution)/shard_map/ppermute | solution.py:20
  339.9 14.8 %collective-permute-start.33 = (bf16[4,10,1,16]{3,2,1,0:T(2,128)(2,1)S(1)}, bf16[4,10,1,16]{3,2,1,0:T(2,128)(2,1)S(1)}, u32[]{:S(2)}, u32[]{:S(2)}) collective-permute-start(bf16[4,10,1,16]{3,2,1,0:T(2,128)(2,1)S(1)} %get-tuple-element.52), channel_id=1, source_target_pairs={{0,1},{1,2},{2,3},{4,5},{5,6},{6,7},{8,9},{9,10},{10,11},{12,13},{... | collective-permute-start | bytes 3848 | tf_op jit(solution)/shard_map/ppermute | solution.py:17
  (226 shorter events, 99.5 us)
Async XLA Ops:
  4.0 27.4 %collective-permute-start = (bf16[4,37,1536]{2,1,0:T(8,128)(2,1)}, bf16[4,37,1536]{2,1,0:T(8,128)(2,1)}, u32[]{:S(2)}, u32[]{:S(2)}) collective-permute-start(bf16[4,37,1536]{2,1,0:T(8,128)(2,1)} %get-tuple-element.49), channel_id=1, source_target_pairs={{0,4},{4,8},{8,12},{12,16},{16,20},{20,24},{24,28},{28,0},{1,5},{5... | collective-permute-start | bytes 1363976 | tf_op jit(solution)/shard_map/ppermute | solution.py:29
  7.6 36.5 %collective-permute-start.1 = (bf16[4,37,1536]{2,1,0:T(8,128)(2,1)}, bf16[4,37,1536]{2,1,0:T(8,128)(2,1)}, u32[]{:S(2)}, u32[]{:S(2)}) collective-permute-start(bf16[4,37,1536]{2,1,0:T(8,128)(2,1)} %get-tuple-element.49), channel_id=1, source_target_pairs={{0,8},{4,12},{8,16},{12,20},{16,24},{20,28},{24,0},{28,4},{1,9},{5... | collective-permute-start | bytes 1363976 | tf_op jit(solution)/shard_map/ppermute | solution.py:29
  9.2 36.1 %collective-permute-start.2 = (bf16[4,37,1536]{2,1,0:T(8,128)(2,1)}, bf16[4,37,1536]{2,1,0:T(8,128)(2,1)}, u32[]{:S(2)}, u32[]{:S(2)}) collective-permute-start(bf16[4,37,1536]{2,1,0:T(8,128)(2,1)} %get-tuple-element.49), channel_id=1, source_target_pairs={{0,12},{4,16},{8,20},{12,24},{16,28},{20,0},{24,4},{28,8},{1,13},{... | collective-permute-start | bytes 1363976 | tf_op jit(solution)/shard_map/ppermute | solution.py:29
  11.9 43.9 %collective-permute-start.3 = (bf16[4,37,1536]{2,1,0:T(8,128)(2,1)}, bf16[4,37,1536]{2,1,0:T(8,128)(2,1)}, u32[]{:S(2)}, u32[]{:S(2)}) collective-permute-start(bf16[4,37,1536]{2,1,0:T(8,128)(2,1)} %get-tuple-element.49), channel_id=1, source_target_pairs={{0,16},{4,20},{8,24},{12,28},{16,0},{20,4},{24,8},{28,12},{1,17},{... | collective-permute-start | bytes 1363976 | tf_op jit(solution)/shard_map/ppermute | solution.py:29
  12.8 44.1 %collective-permute-start.4 = (bf16[4,37,1536]{2,1,0:T(8,128)(2,1)}, bf16[4,37,1536]{2,1,0:T(8,128)(2,1)}, u32[]{:S(2)}, u32[]{:S(2)}) collective-permute-start(bf16[4,37,1536]{2,1,0:T(8,128)(2,1)} %get-tuple-element.49), channel_id=1, source_target_pairs={{0,20},{4,24},{8,28},{12,0},{16,4},{20,8},{24,12},{28,16},{1,21},{... | collective-permute-start | bytes 1363976 | tf_op jit(solution)/shard_map/ppermute | solution.py:29
  31.5 26.5 %collective-permute-start.5 = (bf16[4,37,1536]{2,1,0:T(8,128)(2,1)}, bf16[4,37,1536]{2,1,0:T(8,128)(2,1)S(1)}, u32[]{:S(2)}, u32[]{:S(2)}) collective-permute-start(bf16[4,37,1536]{2,1,0:T(8,128)(2,1)} %get-tuple-element.49), channel_id=1, source_target_pairs={{0,24},{4,28},{8,0},{12,4},{16,8},{20,12},{24,16},{28,20},{1,25},{... | collective-permute-start | bytes 1363976 | tf_op jit(solution)/shard_map/ppermute | solution.py:29
  44.1 14.2 %collective-permute-start.6 = (bf16[4,37,1536]{2,1,0:T(8,128)(2,1)}, bf16[4,37,1536]{2,1,0:T(8,128)(2,1)S(1)}, u32[]{:S(2)}, u32[]{:S(2)}) collective-permute-start(bf16[4,37,1536]{2,1,0:T(8,128)(2,1)} %get-tuple-element.49), channel_id=1, source_target_pairs={{0,28},{4,0},{8,4},{12,8},{16,12},{20,16},{24,20},{28,24},{1,29},{... | collective-permute-start | bytes 1363976 | tf_op jit(solution)/shard_map/ppermute | solution.py:29
  71.8 21.3 %collective-permute-start.7 = (bf16[1184,384]{1,0:T(8,128)(2,1)}, bf16[1184,384]{1,0:T(8,128)(2,1)}, u32[]{:S(2)}, u32[]{:S(2)}) collective-permute-start(bf16[1184,384]{1,0:T(8,128)(2,1)} %reshape.330.refs_0_), channel_id=1, source_target_pairs={{0,1},{1,2},{2,3},{3,0},{4,5},{5,6},{6,7},{7,4},{8,9},{9,10},{10,1... | collective-permute-start | bytes 2727944 | tf_op jit(solution)/shard_map/ppermute | solution.py:47
  73.3 40.8 %collective-permute-start.8 = (bf16[1184,384]{1,0:T(8,128)(2,1)}, bf16[1184,384]{1,0:T(8,128)(2,1)}, u32[]{:S(2)}, u32[]{:S(2)}) collective-permute-start(bf16[1184,384]{1,0:T(8,128)(2,1)} %reshape.330.refs_0_), channel_id=1, source_target_pairs={{0,2},{1,3},{2,0},{3,1},{4,6},{5,7},{6,4},{7,5},{8,10},{9,11},{10,... | collective-permute-start | bytes 2727944 | tf_op jit(solution)/shard_map/ppermute | solution.py:47
  74.5 40.2 %collective-permute-start.9 = (bf16[1184,384]{1,0:T(8,128)(2,1)}, bf16[1184,384]{1,0:T(8,128)(2,1)}, u32[]{:S(2)}, u32[]{:S(2)}) collective-permute-start(bf16[1184,384]{1,0:T(8,128)(2,1)} %reshape.330.refs_0_), channel_id=1, source_target_pairs={{0,3},{1,0},{2,1},{3,2},{4,7},{5,4},{6,5},{7,6},{8,11},{9,8},{10,9... | collective-permute-start | bytes 2727944 | tf_op jit(solution)/shard_map/ppermute | solution.py:47
  134.3 18.5 %collective-permute-start.10 = (bf16[4,37,1536]{2,1,0:T(8,128)(2,1)S(1)}, bf16[4,37,1536]{2,1,0:T(8,128)(2,1)S(1)}, u32[]{:S(2)}, u32[]{:S(2)}) collective-permute-start(bf16[4,37,1536]{2,1,0:T(8,128)(2,1)S(1)} %get-tuple-element.24), channel_id=1, source_target_pairs={{4,0},{8,4},{12,8},{16,12},{20,16},{24,20},{28,24},{0,28},{5,1},{9... | collective-permute-start | bytes 1363976 | tf_op jit(solution)/shard_map/ppermute | solution.py:37
  142.1 44.1 %collective-permute-start.11 = (bf16[4,37,1536]{2,1,0:T(8,128)(2,1)S(1)}, bf16[4,37,1536]{2,1,0:T(8,128)(2,1)S(1)}, u32[]{:S(2)}, u32[]{:S(2)}) collective-permute-start(bf16[4,37,1536]{2,1,0:T(8,128)(2,1)S(1)} %get-tuple-element.25), channel_id=1, source_target_pairs={{8,0},{12,4},{16,8},{20,12},{24,16},{28,20},{0,24},{4,28},{9,1},{1... | collective-permute-start | bytes 1363976 | tf_op jit(solution)/shard_map/ppermute | solution.py:37
  145.5 40.8 %collective-permute-start.12 = (bf16[4,37,1536]{2,1,0:T(8,128)(2,1)S(1)}, bf16[4,37,1536]{2,1,0:T(8,128)(2,1)S(1)}, u32[]{:S(2)}, u32[]{:S(2)}) collective-permute-start(bf16[4,37,1536]{2,1,0:T(8,128)(2,1)S(1)} %get-tuple-element.26), channel_id=1, source_target_pairs={{12,0},{16,4},{20,8},{24,12},{28,16},{0,20},{4,24},{8,28},{13,1},{... | collective-permute-start | bytes 1363976 | tf_op jit(solution)/shard_map/ppermute | solution.py:37
  148.8 37.5 %collective-permute-start.13 = (bf16[4,37,1536]{2,1,0:T(8,128)(2,1)S(1)}, bf16[4,37,1536]{2,1,0:T(8,128)(2,1)S(1)}, u32[]{:S(2)}, u32[]{:S(2)}) collective-permute-start(bf16[4,37,1536]{2,1,0:T(8,128)(2,1)S(1)} %get-tuple-element.27), channel_id=1, source_target_pairs={{16,0},{20,4},{24,8},{28,12},{0,16},{4,20},{8,24},{12,28},{17,1},{... | collective-permute-start | bytes 1363976 | tf_op jit(solution)/shard_map/ppermute | solution.py:37
  148.8 37.5 %collective-permute-start.14 = (bf16[4,37,1536]{2,1,0:T(8,128)(2,1)S(1)}, bf16[4,37,1536]{2,1,0:T(8,128)(2,1)S(1)}, u32[]{:S(2)}, u32[]{:S(2)}) collective-permute-start(bf16[4,37,1536]{2,1,0:T(8,128)(2,1)S(1)} %get-tuple-element.28), channel_id=1, source_target_pairs={{20,0},{24,4},{28,8},{0,12},{4,16},{8,20},{12,24},{16,28},{21,1},{... | collective-permute-start | bytes 1363976 | tf_op jit(solution)/shard_map/ppermute | solution.py:37
  152.8 36.7 %collective-permute-start.15 = (bf16[4,37,1536]{2,1,0:T(8,128)(2,1)S(1)}, bf16[4,37,1536]{2,1,0:T(8,128)(2,1)S(1)}, u32[]{:S(2)}, u32[]{:S(2)}) collective-permute-start(bf16[4,37,1536]{2,1,0:T(8,128)(2,1)S(1)} %get-tuple-element.30), channel_id=1, source_target_pairs={{24,0},{28,4},{0,8},{4,12},{8,16},{12,20},{16,24},{20,28},{25,1},{... | collective-permute-start | bytes 1363976 | tf_op jit(solution)/shard_map/ppermute | solution.py:37
  186.2 11.3 %collective-permute-start.16 = (bf16[4,37,1536]{2,1,0:T(8,128)(2,1)S(1)}, bf16[4,37,1536]{2,1,0:T(8,128)(2,1)S(1)}, u32[]{:S(2)}, u32[]{:S(2)}) collective-permute-start(bf16[4,37,1536]{2,1,0:T(8,128)(2,1)S(1)} %get-tuple-element.29), channel_id=1, source_target_pairs={{28,0},{0,4},{4,8},{8,12},{12,16},{16,20},{20,24},{24,28},{29,1},{... | collective-permute-start | bytes 1363976 | tf_op jit(solution)/shard_map/ppermute | solution.py:37
  200.2 16.8 %collective-permute-start.17 = (bf16[4,37,1536]{2,1,0:T(8,128)(2,1)}, bf16[4,37,1536]{2,1,0:T(8,128)(2,1)S(1)}, u32[]{:S(2)}, u32[]{:S(2)}) collective-permute-start(bf16[4,37,1536]{2,1,0:T(8,128)(2,1)} %get-tuple-element.47), channel_id=1, source_target_pairs={{0,4},{4,8},{8,12},{12,16},{16,20},{20,24},{24,28},{28,0},{1,5},{5... | collective-permute-start | bytes 1363976 | tf_op jit(solution)/shard_map/ppermute | solution.py:47
  200.2 30.8 %collective-permute-start.18 = (bf16[4,37,1536]{2,1,0:T(8,128)(2,1)}, bf16[4,37,1536]{2,1,0:T(8,128)(2,1)S(1)}, u32[]{:S(2)}, u32[]{:S(2)}) collective-permute-start(bf16[4,37,1536]{2,1,0:T(8,128)(2,1)} %get-tuple-element.47), channel_id=1, source_target_pairs={{0,8},{4,12},{8,16},{12,20},{16,24},{20,28},{24,0},{28,4},{1,9},{5... | collective-permute-start | bytes 1363976 | tf_op jit(solution)/shard_map/ppermute | solution.py:47
  200.2 39.8 %collective-permute-start.19 = (bf16[4,37,1536]{2,1,0:T(8,128)(2,1)}, bf16[4,37,1536]{2,1,0:T(8,128)(2,1)S(1)}, u32[]{:S(2)}, u32[]{:S(2)}) collective-permute-start(bf16[4,37,1536]{2,1,0:T(8,128)(2,1)} %get-tuple-element.47), channel_id=1, source_target_pairs={{0,12},{4,16},{8,20},{12,24},{16,28},{20,0},{24,4},{28,8},{1,13},{... | collective-permute-start | bytes 1363976 | tf_op jit(solution)/shard_map/ppermute | solution.py:47
  206.0 40.2 %collective-permute-start.23 = (bf16[4,37,1536]{2,1,0:T(8,128)(2,1)}, bf16[4,37,1536]{2,1,0:T(8,128)(2,1)}, u32[]{:S(2)}, u32[]{:S(2)}) collective-permute-start(bf16[4,37,1536]{2,1,0:T(8,128)(2,1)} %get-tuple-element.47), channel_id=1, source_target_pairs={{0,16},{4,20},{8,24},{12,28},{16,0},{20,4},{24,8},{28,12},{1,17},{... | collective-permute-start | bytes 1363976 | tf_op jit(solution)/shard_map/ppermute | solution.py:47
  207.1 39.1 %collective-permute-start.24 = (bf16[4,37,1536]{2,1,0:T(8,128)(2,1)}, bf16[4,37,1536]{2,1,0:T(8,128)(2,1)}, u32[]{:S(2)}, u32[]{:S(2)}) collective-permute-start(bf16[4,37,1536]{2,1,0:T(8,128)(2,1)} %get-tuple-element.47), channel_id=1, source_target_pairs={{0,20},{4,24},{8,28},{12,0},{16,4},{20,8},{24,12},{28,16},{1,21},{... | collective-permute-start | bytes 1363976 | tf_op jit(solution)/shard_map/ppermute | solution.py:47
  217.0 31.2 %collective-permute-start.25 = (bf16[4,37,1536]{2,1,0:T(8,128)(2,1)}, bf16[4,37,1536]{2,1,0:T(8,128)(2,1)}, u32[]{:S(2)}, u32[]{:S(2)}) collective-permute-start(bf16[4,37,1536]{2,1,0:T(8,128)(2,1)} %get-tuple-element.47), channel_id=1, source_target_pairs={{0,24},{4,28},{8,0},{12,4},{16,8},{20,12},{24,16},{28,20},{1,25},{... | collective-permute-start | bytes 1363976 | tf_op jit(solution)/shard_map/ppermute | solution.py:47
  231.0 17.1 %collective-permute-start.26 = (bf16[4,37,1536]{2,1,0:T(8,128)(2,1)}, bf16[4,37,1536]{2,1,0:T(8,128)(2,1)}, u32[]{:S(2)}, u32[]{:S(2)}) collective-permute-start(bf16[4,37,1536]{2,1,0:T(8,128)(2,1)} %get-tuple-element.47), channel_id=1, source_target_pairs={{0,28},{4,0},{8,4},{12,8},{16,12},{20,16},{24,20},{28,24},{1,29},{... | collective-permute-start | bytes 1363976 | tf_op jit(solution)/shard_map/ppermute | solution.py:47
  264.8 20.7 %collective-permute-start.20 = (bf16[4,37,1536]{2,1,0:T(8,128)(2,1)}, bf16[4,37,1536]{2,1,0:T(8,128)(2,1)}, u32[]{:S(2)}, u32[]{:S(2)}) collective-permute-start(bf16[4,37,1536]{2,1,0:T(8,128)(2,1)} %get-tuple-element.31), channel_id=1, source_target_pairs={{4,0},{8,4},{12,8},{16,12},{20,16},{24,20},{28,24},{0,28},{5,1},{9... | collective-permute-start | bytes 1363976 | tf_op jit(solution)/shard_map/ppermute | solution.py:87
  268.2 42.4 %collective-permute-start.21 = (bf16[4,37,1536]{2,1,0:T(8,128)(2,1)}, bf16[4,37,1536]{2,1,0:T(8,128)(2,1)}, u32[]{:S(2)}, u32[]{:S(2)}) collective-permute-start(bf16[4,37,1536]{2,1,0:T(8,128)(2,1)} %get-tuple-element.33), channel_id=1, source_target_pairs={{8,0},{12,4},{16,8},{20,12},{24,16},{28,20},{0,24},{4,28},{9,1},{1... | collective-permute-start | bytes 1363976 | tf_op jit(solution)/shard_map/ppermute | solution.py:87
  272.9 37.8 %collective-permute-start.22 = (bf16[4,37,1536]{2,1,0:T(8,128)(2,1)}, bf16[4,37,1536]{2,1,0:T(8,128)(2,1)}, u32[]{:S(2)}, u32[]{:S(2)}) collective-permute-start(bf16[4,37,1536]{2,1,0:T(8,128)(2,1)} %get-tuple-element.32), channel_id=1, source_target_pairs={{12,0},{16,4},{20,8},{24,12},{28,16},{0,20},{4,24},{8,28},{13,1},{... | collective-permute-start | bytes 1363976 | tf_op jit(solution)/shard_map/ppermute | solution.py:87
  281.4 33.8 %collective-permute-start.27 = (bf16[4,37,1536]{2,1,0:T(8,128)(2,1)S(1)}, bf16[4,37,1536]{2,1,0:T(8,128)(2,1)S(1)}, u32[]{:S(2)}, u32[]{:S(2)}) collective-permute-start(bf16[4,37,1536]{2,1,0:T(8,128)(2,1)S(1)} %get-tuple-element.34), channel_id=1, source_target_pairs={{16,0},{20,4},{24,8},{28,12},{0,16},{4,20},{8,24},{12,28},{17,1},{... | collective-permute-start | bytes 1363976 | tf_op jit(solution)/shard_map/ppermute | solution.py:87
  283.0 32.2 %collective-permute-start.28 = (bf16[4,37,1536]{2,1,0:T(8,128)(2,1)S(1)}, bf16[4,37,1536]{2,1,0:T(8,128)(2,1)S(1)}, u32[]{:S(2)}, u32[]{:S(2)}) collective-permute-start(bf16[4,37,1536]{2,1,0:T(8,128)(2,1)S(1)} %get-tuple-element.35), channel_id=1, source_target_pairs={{20,0},{24,4},{28,8},{0,12},{4,16},{8,20},{12,24},{16,28},{21,1},{... | collective-permute-start | bytes 1363976 | tf_op jit(solution)/shard_map/ppermute | solution.py:87
  285.4 39.3 %collective-permute-start.29 = (bf16[4,37,1536]{2,1,0:T(8,128)(2,1)S(1)}, bf16[4,37,1536]{2,1,0:T(8,128)(2,1)S(1)}, u32[]{:S(2)}, u32[]{:S(2)}) collective-permute-start(bf16[4,37,1536]{2,1,0:T(8,128)(2,1)S(1)} %get-tuple-element.37), channel_id=1, source_target_pairs={{24,0},{28,4},{0,8},{4,12},{8,16},{12,20},{16,24},{20,28},{25,1},{... | collective-permute-start | bytes 1363976 | tf_op jit(solution)/shard_map/ppermute | solution.py:87
  310.6 14.2 %collective-permute-start.30 = (bf16[4,37,1536]{2,1,0:T(8,128)(2,1)S(1)}, bf16[4,37,1536]{2,1,0:T(8,128)(2,1)S(1)}, u32[]{:S(2)}, u32[]{:S(2)}) collective-permute-start(bf16[4,37,1536]{2,1,0:T(8,128)(2,1)S(1)} %get-tuple-element.36), channel_id=1, source_target_pairs={{28,0},{0,4},{4,8},{8,12},{12,16},{16,20},{20,24},{24,28},{29,1},{... | collective-permute-start | bytes 1363976 | tf_op jit(solution)/shard_map/ppermute | solution.py:87
  339.9 17.2 %collective-permute-start.33 = (bf16[4,10,1,16]{3,2,1,0:T(2,128)(2,1)S(1)}, bf16[4,10,1,16]{3,2,1,0:T(2,128)(2,1)S(1)}, u32[]{:S(2)}, u32[]{:S(2)}) collective-permute-start(bf16[4,10,1,16]{3,2,1,0:T(2,128)(2,1)S(1)} %get-tuple-element.52), channel_id=1, source_target_pairs={{0,1},{1,2},{2,3},{4,5},{5,6},{6,7},{8,9},{9,10},{10,11},{12,13},{... | collective-permute-start | bytes 3848 | tf_op jit(solution)/shard_map/ppermute | solution.py:17
  (36 other events, 626.3 us)

commit v3 on v1

--- a/solution.py
+++ b/solution.py
@@ -193,13 +193,22 @@
     local_heads = queries.shape[-1] // tile
     local_width = local_heads * HD
     score_scale = 1.0 / math.sqrt(HD)
-    pair_blocks = send_slots(key_value.transpose(1, 0, 2, 3).reshape(-1, local_heads * tile), "blk")
+    own_pairs = key_value.transpose(1, 0, 2, 3).reshape(-1, local_heads * tile)
+    flip_core = [(j, j ^ 1) for j in range(blocks)]
+    flip_chip = [(j, j ^ 2) for j in range(blocks)]
+    far = lax.ppermute(own_pairs, "blk", flip_chip)
+    pair_blocks = [
+        own_pairs,
+        lax.ppermute(own_pairs, "blk", flip_core),
+        far,
+        lax.ppermute(far, "blk", flip_core),
+    ]
     query_rows = groups * tile_tokens
     query_piece = queries.transpose(1, 0, 2, 3).reshape(requests, query_rows, local_heads * tile)
     position = jnp.arange(query_rows, dtype=jnp.int32)
     group = (lax.axis_index("head") - position // tile_tokens) % groups
     within = position % tile_tokens
-    source = (lax.axis_index("blk") - jnp.arange(blocks, dtype=jnp.int32)) % blocks
+    source = jnp.bitwise_xor(lax.axis_index("blk"), jnp.arange(blocks, dtype=jnp.int32))
     slot_ids = (group[None, :] * blocks + source[:, None]) * text_slice + (within - image_tile)[None, :]
     usable = (within < image_tile)[None, None, :] | (
         slot_ids[None, :, :] < text_lengths[:, None, None]

time: 359 us -> 351 us (0.978); the launches traced: 357 us -> 345 us
  waiting for transfers between devices: 177 us -> 171 us
  starting transfers between devices: 80.5 us -> 75.3 us
    ppermute x3, waiting for transfers between devices: 27.6 us -> 10.6 us  [the longest x1 10.6 us: body(): far = lax.ppermute(own_pairs, 'blk', flip_chip)]
    ppermute x14, waiting for transfers between devices: 53.7 us -> 63.6 us  [gather_slots(): lax.ppermute(block, axis, [(i, (i + shift) % count) for i in range(count)])]
    ppermute x14, starting transfers between devices: 40.4 us -> 35.4 us  [scatter_slots(): lax.ppermute(partial[shift], axis, [((i + shift) % count, i) for i in ran...]
    unnamed x97 -> x131, local copies, waits for them, and re-layouts: 10.4 us -> 10.7 us
  transfers between devices with their start and end apart: 35 -> 35, of which waited for: 20 -> 16; matrix products, arithmetic and copies ran while one was open for 11% -> 11% of each run, Pallas kernels for 0% -> 0%
where the time goes in v3:
time: 351 us; the launch traced here: 345 us
  waiting for transfers between devices  171 us (49%)
  starting transfers between devices  75.3 us (21%)
  matrix products  36.6 us (10%)
  local copies, waits for them, and re-layouts  25.2 us (7%)
  other arithmetic  20.6 us (6%)
  Pallas kernels  14.2 us (4%)
    ppermute x14, waiting for transfers between devices, scatter_slots(): lax.ppermute(partial[shift], axis, [((i + shift) % count, i) for i in ran...  93.9 us
    ppermute x14, waiting for transfers between devices, gather_slots(): lax.ppermute(block, axis, [(i, (i + shift) % count) for i in range(count)])  63.6 us
    ppermute x14, starting transfers between devices, scatter_slots(): lax.ppermute(partial[shift], axis, [((i + shift) % count, i) for i in ran...  35.4 us
    ppermute x14, starting transfers between devices, gather_slots(): lax.ppermute(block, axis, [(i, (i + shift) % count) for i in range(count)])  24.7 us
    pallas_call x1, Pallas kernels, attend(): pl.pallas_call(attention_kernel, grid=(requests, heads), in_specs=[pl.Blo...  14.2 us
    unnamed x131, local copies, waits for them, and re-layouts  10.7 us
    ppermute x1, waiting for transfers between devices, body(): far = lax.ppermute(own_pairs, 'blk', flip_chip)  10.6 us
    dot_general x4, matrix products, normalized(): jnp.dot(values * values, spread, precision=lax.Precision.HIGHEST)  8.54 us
  transfers between devices with their start and end apart: 35, of which 16 were waited for; matrix products, arithmetic and copies ran while one was open for 11% of the time, Pallas kernels for 0%

profile of v3, /device:TPU:1, one launch (start us, length us, event | category | flops | bytes accessed | tf_op | source)
XLA Modules:
  0.0 345.2 jit_solution(16594840934265956532)
XLA Ops:
  4.0 3.6 %collective-permute-start = (bf16[4,37,1536]{2,1,0:T(8,128)(2,1)}, bf16[4,37,1536]{2,1,0:T(8,128)(2,1)}, u32[]{:S(2)}, u32[]{:S(2)}) collective-permute-start(bf16[4,37,1536]{2,1,0:T(8,128)(2,1)} %get-tuple-element.47), channel_id=1, source_target_pairs={{0,4},{4,8},{8,12},{12,16},{16,20},{20,24},{24,28},{28,0},{1,5},{5... | collective-permute-start | bytes 1363976 | tf_op jit(solution)/shard_map/ppermute | solution.py:29
  9.2 2.6 collective-permute-start.2
  12.8 5.2 %collective-permute-start.4 = (bf16[4,37,1536]{2,1,0:T(8,128)(2,1)}, bf16[4,37,1536]{2,1,0:T(8,128)(2,1)}, u32[]{:S(2)}, u32[]{:S(2)}) collective-permute-start(bf16[4,37,1536]{2,1,0:T(8,128)(2,1)} %get-tuple-element.47), channel_id=1, source_target_pairs={{0,20},{4,24},{8,28},{12,0},{16,4},{20,8},{24,12},{28,16},{1,21},{... | collective-permute-start | bytes 1363976 | tf_op jit(solution)/shard_map/ppermute | solution.py:29
  32.1 12.0 %collective-permute-done.1 = bf16[4,37,1536]{2,1,0:T(8,128)(2,1)} collective-permute-done((bf16[4,37,1536]{2,1,0:T(8,128)(2,1)}, bf16[4,37,1536]{2,1,0:T(8,128)(2,1)}, u32[]{:S(2)}, u32[]{:S(2)}) %collective-permute-start.1) | collective-permute-done | bytes 454688 | tf_op jit(solution)/shard_map/ppermute | solution.py:29
  46.4 9.3 %collective-permute-done.3 = bf16[4,37,1536]{2,1,0:T(8,128)(2,1)} collective-permute-done((bf16[4,37,1536]{2,1,0:T(8,128)(2,1)}, bf16[4,37,1536]{2,1,0:T(8,128)(2,1)}, u32[]{:S(2)}, u32[]{:S(2)}) %collective-permute-start.3) | collective-permute-done | bytes 454688 | tf_op jit(solution)/shard_map/ppermute | solution.py:29
  65.2 3.3 select_convert_fusion
  79.9 10.6 %collective-permute-done.8.refs_2_ = bf16[1184,384]{1,0:T(8,128)(2,1)S(1)} collective-permute-done((bf16[1184,384]{1,0:T(8,128)(2,1)}, bf16[1184,384]{1,0:T(8,128)(2,1)S(1)}, u32[]{:S(2)}, u32[]{:S(2)}) %collective-permute-start.8) | collective-permute-done | bytes 909344 | tf_op jit(solution)/shard_map/ppermute | solution.py:199
  92.8 4.0 %fusion.216 = f32[8,4,32,384]{3,2,1,0:T(8,128)S(1)} fusion(bf16[1536,384,1,1]{0,1,3,2:T(8,128)(2,1)S(1)} %bitcast.305, f32[8,4,37,1536]{3,2,1,0:T(8,128)} %copy-done.1, f32[4,1536]{1,0:T(4,128)S(1)} %copy-done.28, f32[4,1536]{1,0:T(4,128)S(1)} %bitcast.314, f32[8,4,32]{2,1,0:T(4,128)S(1)} %copy-done.37, f32[8,4,32]{2,1,0:T(4,128)S(1)} %broadcast_multiply_fusion.1), kind=kOutput, calls=%fused_computation.357 | convolution fusion | flops 1215823872 | bytes 9101312 | tf_op jit(solution)/shard_map/arnd,de->arne/dot_general | solution.py:129
  96.8 3.3 multiply_convert_fusion
  102.6 14.2 %shard_map.219 = bf16[4,296,384]{2,1,0:T(8,128)(2,1)} custom-call(bf16[4,296,384]{2,1,0:T(8,128)(2,1)} %copy.107.query_ref, bf16[1184,384]{1,0:T(8,128)(2,1)} %reshape.319.refs_0_, bf16[1184,384]{1,0:T(8,128)(2,1)} %copy-done.10, bf16[1184,384]{1,0:T(8,128)(2,1)} %copy-done.9, bf16[1184,384]{1,0:T(8,128)(2,1)} %collective-permute-done.9.refs_3_, ...), custom_call_target="tpu_custom_call" | custom-call | tf_op jit(solution)/shard_map/pallas_call | solution.py:72
  121.6 6.3 %collective-permute-start.10 = (bf16[4,37,1536]{2,1,0:T(8,128)(2,1)S(1)}, bf16[4,37,1536]{2,1,0:T(8,128)(2,1)S(1)}, u32[]{:S(2)}, u32[]{:S(2)}) collective-permute-start(bf16[4,37,1536]{2,1,0:T(8,128)(2,1)S(1)} %get-tuple-element.31), channel_id=1, source_target_pairs={{4,0},{8,4},{12,8},{16,12},{20,16},{24,20},{28,24},{0,28},{5,1},{9... | collective-permute-start | bytes 1363976 | tf_op jit(solution)/shard_map/ppermute | solution.py:37
  127.8 5.0 %collective-permute-start.11 = (bf16[4,37,1536]{2,1,0:T(8,128)(2,1)S(1)}, bf16[4,37,1536]{2,1,0:T(8,128)(2,1)S(1)}, u32[]{:S(2)}, u32[]{:S(2)}) collective-permute-start(bf16[4,37,1536]{2,1,0:T(8,128)(2,1)S(1)} %get-tuple-element.32), channel_id=1, source_target_pairs={{8,0},{12,4},{16,8},{20,12},{24,16},{28,20},{0,24},{4,28},{9,1},{1... | collective-permute-start | bytes 1363976 | tf_op jit(solution)/shard_map/ppermute | solution.py:37
  132.8 3.3 collective-permute-start.12
  138.3 6.2 %collective-permute-start.15 = (bf16[4,37,1536]{2,1,0:T(8,128)(2,1)S(1)}, bf16[4,37,1536]{2,1,0:T(8,128)(2,1)S(1)}, u32[]{:S(2)}, u32[]{:S(2)}) collective-permute-start(bf16[4,37,1536]{2,1,0:T(8,128)(2,1)S(1)} %get-tuple-element.37), channel_id=1, source_target_pairs={{24,0},{28,4},{0,8},{4,12},{8,16},{12,20},{16,24},{20,28},{25,1},{... | collective-permute-start | bytes 1363976 | tf_op jit(solution)/shard_map/ppermute | solution.py:37
  144.5 29.9 %collective-permute-done.11 = bf16[4,37,1536]{2,1,0:T(8,128)(2,1)S(1)} collective-permute-done((bf16[4,37,1536]{2,1,0:T(8,128)(2,1)S(1)}, bf16[4,37,1536]{2,1,0:T(8,128)(2,1)S(1)}, u32[]{:S(2)}, u32[]{:S(2)}) %collective-permute-start.11) | collective-permute-done | bytes 454688 | tf_op jit(solution)/shard_map/ppermute | solution.py:37
  174.5 3.5 %collective-permute-done.15 = bf16[4,37,1536]{2,1,0:T(8,128)(2,1)S(1)} collective-permute-done((bf16[4,37,1536]{2,1,0:T(8,128)(2,1)S(1)}, bf16[4,37,1536]{2,1,0:T(8,128)(2,1)S(1)}, u32[]{:S(2)}, u32[]{:S(2)}) %collective-permute-start.15) | collective-permute-done | bytes 454688 | tf_op jit(solution)/shard_map/ppermute | solution.py:37
  178.1 11.2 %collective-permute-done.16 = bf16[4,37,1536]{2,1,0:T(8,128)(2,1)S(1)} collective-permute-done((bf16[4,37,1536]{2,1,0:T(8,128)(2,1)S(1)}, bf16[4,37,1536]{2,1,0:T(8,128)(2,1)S(1)}, u32[]{:S(2)}, u32[]{:S(2)}) %collective-permute-start.16) | collective-permute-done | bytes 454688 | tf_op jit(solution)/shard_map/ppermute | solution.py:37
  191.4 5.4 %collective-permute-start.19 = (bf16[4,37,1536]{2,1,0:T(8,128)(2,1)S(1)}, bf16[4,37,1536]{2,1,0:T(8,128)(2,1)S(1)}, u32[]{:S(2)}, u32[]{:S(2)}) collective-permute-start(bf16[4,37,1536]{2,1,0:T(8,128)(2,1)S(1)} %pad_maximum_fusion.5), channel_id=1, source_target_pairs={{0,12},{4,16},{8,20},{12,24},{16,28},{20,0},{24,4},{28,8},{1,13},{... | collective-permute-start | bytes 1363976 | tf_op jit(solution)/shard_map/ppermute | solution.py:29
  197.5 2.6 collective-permute-start.21
  200.2 5.1 %collective-permute-done.17 = bf16[4,37,1536]{2,1,0:T(8,128)(2,1)S(1)} collective-permute-done((bf16[4,37,1536]{2,1,0:T(8,128)(2,1)S(1)}, bf16[4,37,1536]{2,1,0:T(8,128)(2,1)S(1)}, u32[]{:S(2)}, u32[]{:S(2)}) %collective-permute-start.17) | collective-permute-done | bytes 454688 | tf_op jit(solution)/shard_map/ppermute | solution.py:29
  206.2 18.1 %collective-permute-done.18 = bf16[4,37,1536]{2,1,0:T(8,128)(2,1)S(1)} collective-permute-done((bf16[4,37,1536]{2,1,0:T(8,128)(2,1)S(1)}, bf16[4,37,1536]{2,1,0:T(8,128)(2,1)S(1)}, u32[]{:S(2)}, u32[]{:S(2)}) %collective-permute-start.18) | collective-permute-done | bytes 454688 | tf_op jit(solution)/shard_map/ppermute | solution.py:29
  224.5 11.1 %collective-permute-done.20 = bf16[4,37,1536]{2,1,0:T(8,128)(2,1)S(1)} collective-permute-done((bf16[4,37,1536]{2,1,0:T(8,128)(2,1)S(1)}, bf16[4,37,1536]{2,1,0:T(8,128)(2,1)S(1)}, u32[]{:S(2)}, u32[]{:S(2)}) %collective-permute-start.20) | collective-permute-done | bytes 454688 | tf_op jit(solution)/shard_map/ppermute | solution.py:29
  235.7 7.5 %collective-permute-done.22 = bf16[4,37,1536]{2,1,0:T(8,128)(2,1)S(1)} collective-permute-done((bf16[4,37,1536]{2,1,0:T(8,128)(2,1)S(1)}, bf16[4,37,1536]{2,1,0:T(8,128)(2,1)S(1)}, u32[]{:S(2)}, u32[]{:S(2)}) %collective-permute-start.22) | collective-permute-done | bytes 454688 | tf_op jit(solution)/shard_map/ppermute | solution.py:29
  244.3 4.2 %fusion.8 = bf16[8,4,32,768]{3,2,1,0:T(8,128)(2,1)} fusion(bf16[1536,768]{1,0:T(8,128)(2,1)S(1)} %copy-done.49, bf16[8,4,37,1536]{3,2,1,0:T(8,128)(2,1)S(1)} %bitcast_dynamic-update-slice_fusion), kind=kOutput, calls=%fused_computation.43 | convolution fusion | flops 2422996992 | bytes 7077888 | tf_op jit(solution)/shard_map/arnd,df->arnf/dot_general | solution.py:238
  248.5 4.7 %convolution_convert_fusion.3 = bf16[8,4,5,1536]{3,0,2,1:T(8,128)(2,1)} fusion(bf16[768,1536]{1,0:T(8,128)(2,1)} %param.37, bf16[1536,768]{1,0:T(8,128)(2,1)} %param.35, bf16[8,4,5,1536]{3,2,1,0:T(8,128)(2,1)} %slice.333), kind=kOutput, calls=%fused_computation.47 | convolution fusion | flops 756326400 | bytes 5701632 | tf_op jit(solution)/shard_map/arnf,fd->arnd/dot_general | solution.py:246
  254.4 4.2 %convolution_convert_fusion = bf16[8,4,32,1536]{3,2,1,0:T(8,128)(2,1)S(1)} fusion(bf16[8,4,32,768]{3,2,1,0:T(8,128)(2,1)} %fusion.8, bf16[768,1536]{1,0:T(8,128)(2,1)S(1)} %copy-done), kind=kOutput, calls=%fused_computation.19 | convolution fusion | flops 2417491968 | bytes 7077888 | tf_op jit(solution)/shard_map/arnf,fd->arnd/dot_general | solution.py:245
  259.2 8.3 %collective-permute-start.25 = (bf16[4,37,1536]{2,1,0:T(8,128)(2,1)S(1)}, bf16[4,37,1536]{2,1,0:T(8,128)(2,1)S(1)}, u32[]{:S(2)}, u32[]{:S(2)}) collective-permute-start(bf16[4,37,1536]{2,1,0:T(8,128)(2,1)S(1)} %get-tuple-element.25), channel_id=1, source_target_pairs={{8,0},{12,4},{16,8},{20,12},{24,16},{28,20},{0,24},{4,28},{9,1},{1... | collective-permute-start | bytes 1363976 | tf_op jit(solution)/shard_map/ppermute | solution.py:37
  268.7 2.8 collective-permute-start.28
  273.0 34.6 %collective-permute-done.25 = bf16[4,37,1536]{2,1,0:T(8,128)(2,1)S(1)} collective-permute-done((bf16[4,37,1536]{2,1,0:T(8,128)(2,1)S(1)}, bf16[4,37,1536]{2,1,0:T(8,128)(2,1)S(1)}, u32[]{:S(2)}, u32[]{:S(2)}) %collective-permute-start.25) | collective-permute-done | bytes 454688 | tf_op jit(solution)/shard_map/ppermute | solution.py:37
  307.9 13.3 %collective-permute-done.30 = bf16[4,37,1536]{2,1,0:T(8,128)(2,1)S(1)} collective-permute-done((bf16[4,37,1536]{2,1,0:T(8,128)(2,1)S(1)}, bf16[4,37,1536]{2,1,0:T(8,128)(2,1)S(1)}, u32[]{:S(2)}, u32[]{:S(2)}) %collective-permute-start.30) | collective-permute-done | bytes 454688 | tf_op jit(solution)/shard_map/ppermute | solution.py:37
  330.5 2.8 collective-permute-done.32
  335.2 6.3 %collective-permute-start.34 = (bf16[4,10,1,16]{3,2,1,0:T(2,128)(2,1)S(1)}, bf16[4,10,1,16]{3,2,1,0:T(2,128)(2,1)S(1)}, u32[]{:S(2)}, u32[]{:S(2)}) collective-permute-start(bf16[4,10,1,16]{3,2,1,0:T(2,128)(2,1)S(1)} %get-tuple-element.51), channel_id=1, source_target_pairs={{1,0},{2,1},{3,2},{5,4},{6,5},{7,6},{9,8},{10,9},{11,10},{13,12},{... | collective-permute-start | bytes 3848 | tf_op jit(solution)/shard_map/ppermute | solution.py:20
  (274 shorter events, 78.6 us)
Async XLA Ops:
  4.0 26.2 %collective-permute-start = (bf16[4,37,1536]{2,1,0:T(8,128)(2,1)}, bf16[4,37,1536]{2,1,0:T(8,128)(2,1)}, u32[]{:S(2)}, u32[]{:S(2)}) collective-permute-start(bf16[4,37,1536]{2,1,0:T(8,128)(2,1)} %get-tuple-element.47), channel_id=1, source_target_pairs={{0,4},{4,8},{8,12},{12,16},{16,20},{20,24},{24,28},{28,0},{1,5},{5... | collective-permute-start | bytes 1363976 | tf_op jit(solution)/shard_map/ppermute | solution.py:29
  7.6 36.5 %collective-permute-start.1 = (bf16[4,37,1536]{2,1,0:T(8,128)(2,1)}, bf16[4,37,1536]{2,1,0:T(8,128)(2,1)}, u32[]{:S(2)}, u32[]{:S(2)}) collective-permute-start(bf16[4,37,1536]{2,1,0:T(8,128)(2,1)} %get-tuple-element.47), channel_id=1, source_target_pairs={{0,8},{4,12},{8,16},{12,20},{16,24},{20,28},{24,0},{28,4},{1,9},{5... | collective-permute-start | bytes 1363976 | tf_op jit(solution)/shard_map/ppermute | solution.py:29
  9.2 36.1 %collective-permute-start.2 = (bf16[4,37,1536]{2,1,0:T(8,128)(2,1)}, bf16[4,37,1536]{2,1,0:T(8,128)(2,1)}, u32[]{:S(2)}, u32[]{:S(2)}) collective-permute-start(bf16[4,37,1536]{2,1,0:T(8,128)(2,1)} %get-tuple-element.47), channel_id=1, source_target_pairs={{0,12},{4,16},{8,20},{12,24},{16,28},{20,0},{24,4},{28,8},{1,13},{... | collective-permute-start | bytes 1363976 | tf_op jit(solution)/shard_map/ppermute | solution.py:29
  11.9 43.9 %collective-permute-start.3 = (bf16[4,37,1536]{2,1,0:T(8,128)(2,1)}, bf16[4,37,1536]{2,1,0:T(8,128)(2,1)}, u32[]{:S(2)}, u32[]{:S(2)}) collective-permute-start(bf16[4,37,1536]{2,1,0:T(8,128)(2,1)} %get-tuple-element.47), channel_id=1, source_target_pairs={{0,16},{4,20},{8,24},{12,28},{16,0},{20,4},{24,8},{28,12},{1,17},{... | collective-permute-start | bytes 1363976 | tf_op jit(solution)/shard_map/ppermute | solution.py:29
  12.8 44.1 %collective-permute-start.4 = (bf16[4,37,1536]{2,1,0:T(8,128)(2,1)}, bf16[4,37,1536]{2,1,0:T(8,128)(2,1)}, u32[]{:S(2)}, u32[]{:S(2)}) collective-permute-start(bf16[4,37,1536]{2,1,0:T(8,128)(2,1)} %get-tuple-element.47), channel_id=1, source_target_pairs={{0,20},{4,24},{8,28},{12,0},{16,4},{20,8},{24,12},{28,16},{1,21},{... | collective-permute-start | bytes 1363976 | tf_op jit(solution)/shard_map/ppermute | solution.py:29
  30.2 27.7 %collective-permute-start.5 = (bf16[4,37,1536]{2,1,0:T(8,128)(2,1)}, bf16[4,37,1536]{2,1,0:T(8,128)(2,1)S(1)}, u32[]{:S(2)}, u32[]{:S(2)}) collective-permute-start(bf16[4,37,1536]{2,1,0:T(8,128)(2,1)} %get-tuple-element.47), channel_id=1, source_target_pairs={{0,24},{4,28},{8,0},{12,4},{16,8},{20,12},{24,16},{28,20},{1,25},{... | collective-permute-start | bytes 1363976 | tf_op jit(solution)/shard_map/ppermute | solution.py:29
  44.1 14.2 %collective-permute-start.6 = (bf16[4,37,1536]{2,1,0:T(8,128)(2,1)}, bf16[4,37,1536]{2,1,0:T(8,128)(2,1)S(1)}, u32[]{:S(2)}, u32[]{:S(2)}) collective-permute-start(bf16[4,37,1536]{2,1,0:T(8,128)(2,1)} %get-tuple-element.47), channel_id=1, source_target_pairs={{0,28},{4,0},{8,4},{12,8},{16,12},{20,16},{24,20},{28,24},{1,29},{... | collective-permute-start | bytes 1363976 | tf_op jit(solution)/shard_map/ppermute | solution.py:29
  70.0 20.5 %collective-permute-start.8 = (bf16[1184,384]{1,0:T(8,128)(2,1)}, bf16[1184,384]{1,0:T(8,128)(2,1)S(1)}, u32[]{:S(2)}, u32[]{:S(2)}) collective-permute-start(bf16[1184,384]{1,0:T(8,128)(2,1)} %reshape.319.refs_0_), channel_id=1, source_target_pairs={{0,2},{1,3},{2,0},{3,1},{4,6},{5,7},{6,4},{7,5},{8,10},{9,11},{10,... | collective-permute-start | bytes 2727944 | tf_op jit(solution)/shard_map/ppermute | solution.py:199
  74.8 26.9 %collective-permute-start.7 = (bf16[1184,384]{1,0:T(8,128)(2,1)S(1)}, bf16[1184,384]{1,0:T(8,128)(2,1)S(1)}, u32[]{:S(2)}, u32[]{:S(2)}) collective-permute-start(bf16[1184,384]{1,0:T(8,128)(2,1)S(1)} %copy-done.5), channel_id=1, source_target_pairs={{0,1},{1,0},{2,3},{3,2},{4,5},{5,4},{6,7},{7,6},{8,9},{9,8},{10,11... | collective-permute-start | bytes 2727944 | tf_op jit(solution)/shard_map/ppermute | solution.py:202
  90.5 12.1 %collective-permute-start.9 = (bf16[1184,384]{1,0:T(8,128)(2,1)S(1)}, bf16[1184,384]{1,0:T(8,128)(2,1)}, u32[]{:S(2)}, u32[]{:S(2)}) collective-permute-start(bf16[1184,384]{1,0:T(8,128)(2,1)S(1)} %collective-permute-done.8.refs_2_), channel_id=1, source_target_pairs={{0,1},{1,0},{2,3},{3,2},{4,5},{5,4},{6,7},{7,6},{8,9},{9,8},{10,11... | collective-permute-start | bytes 2727944 | tf_op jit(solution)/shard_map/ppermute | solution.py:204
  121.6 16.7 %collective-permute-start.10 = (bf16[4,37,1536]{2,1,0:T(8,128)(2,1)S(1)}, bf16[4,37,1536]{2,1,0:T(8,128)(2,1)S(1)}, u32[]{:S(2)}, u32[]{:S(2)}) collective-permute-start(bf16[4,37,1536]{2,1,0:T(8,128)(2,1)S(1)} %get-tuple-element.31), channel_id=1, source_target_pairs={{4,0},{8,4},{12,8},{16,12},{20,16},{24,20},{28,24},{0,28},{5,1},{9... | collective-permute-start | bytes 1363976 | tf_op jit(solution)/shard_map/ppermute | solution.py:37
  127.8 46.5 %collective-permute-start.11 = (bf16[4,37,1536]{2,1,0:T(8,128)(2,1)S(1)}, bf16[4,37,1536]{2,1,0:T(8,128)(2,1)S(1)}, u32[]{:S(2)}, u32[]{:S(2)}) collective-permute-start(bf16[4,37,1536]{2,1,0:T(8,128)(2,1)S(1)} %get-tuple-element.32), channel_id=1, source_target_pairs={{8,0},{12,4},{16,8},{20,12},{24,16},{28,20},{0,24},{4,28},{9,1},{1... | collective-permute-start | bytes 1363976 | tf_op jit(solution)/shard_map/ppermute | solution.py:37
  132.8 41.7 %collective-permute-start.12 = (bf16[4,37,1536]{2,1,0:T(8,128)(2,1)S(1)}, bf16[4,37,1536]{2,1,0:T(8,128)(2,1)S(1)}, u32[]{:S(2)}, u32[]{:S(2)}) collective-permute-start(bf16[4,37,1536]{2,1,0:T(8,128)(2,1)S(1)} %get-tuple-element.33), channel_id=1, source_target_pairs={{12,0},{16,4},{20,8},{24,12},{28,16},{0,20},{4,24},{8,28},{13,1},{... | collective-permute-start | bytes 1363976 | tf_op jit(solution)/shard_map/ppermute | solution.py:37
  136.1 38.4 %collective-permute-start.13 = (bf16[4,37,1536]{2,1,0:T(8,128)(2,1)S(1)}, bf16[4,37,1536]{2,1,0:T(8,128)(2,1)S(1)}, u32[]{:S(2)}, u32[]{:S(2)}) collective-permute-start(bf16[4,37,1536]{2,1,0:T(8,128)(2,1)S(1)} %get-tuple-element.34), channel_id=1, source_target_pairs={{16,0},{20,4},{24,8},{28,12},{0,16},{4,20},{8,24},{12,28},{17,1},{... | collective-permute-start | bytes 1363976 | tf_op jit(solution)/shard_map/ppermute | solution.py:37
  136.5 38.0 %collective-permute-start.14 = (bf16[4,37,1536]{2,1,0:T(8,128)(2,1)S(1)}, bf16[4,37,1536]{2,1,0:T(8,128)(2,1)S(1)}, u32[]{:S(2)}, u32[]{:S(2)}) collective-permute-start(bf16[4,37,1536]{2,1,0:T(8,128)(2,1)S(1)} %get-tuple-element.35), channel_id=1, source_target_pairs={{20,0},{24,4},{28,8},{0,12},{4,16},{8,20},{12,24},{16,28},{21,1},{... | collective-permute-start | bytes 1363976 | tf_op jit(solution)/shard_map/ppermute | solution.py:37
  138.3 39.8 %collective-permute-start.15 = (bf16[4,37,1536]{2,1,0:T(8,128)(2,1)S(1)}, bf16[4,37,1536]{2,1,0:T(8,128)(2,1)S(1)}, u32[]{:S(2)}, u32[]{:S(2)}) collective-permute-start(bf16[4,37,1536]{2,1,0:T(8,128)(2,1)S(1)} %get-tuple-element.37), channel_id=1, source_target_pairs={{24,0},{28,4},{0,8},{4,12},{8,16},{12,20},{16,24},{20,28},{25,1},{... | collective-permute-start | bytes 1363976 | tf_op jit(solution)/shard_map/ppermute | solution.py:37
  174.4 14.9 %collective-permute-start.16 = (bf16[4,37,1536]{2,1,0:T(8,128)(2,1)S(1)}, bf16[4,37,1536]{2,1,0:T(8,128)(2,1)S(1)}, u32[]{:S(2)}, u32[]{:S(2)}) collective-permute-start(bf16[4,37,1536]{2,1,0:T(8,128)(2,1)S(1)} %get-tuple-element.36), channel_id=1, source_target_pairs={{28,0},{0,4},{4,8},{8,12},{12,16},{16,20},{20,24},{24,28},{29,1},{... | collective-permute-start | bytes 1363976 | tf_op jit(solution)/shard_map/ppermute | solution.py:37
  191.2 14.0 %collective-permute-start.17 = (bf16[4,37,1536]{2,1,0:T(8,128)(2,1)S(1)}, bf16[4,37,1536]{2,1,0:T(8,128)(2,1)S(1)}, u32[]{:S(2)}, u32[]{:S(2)}) collective-permute-start(bf16[4,37,1536]{2,1,0:T(8,128)(2,1)S(1)} %pad_maximum_fusion.5), channel_id=1, source_target_pairs={{0,4},{4,8},{8,12},{12,16},{16,20},{20,24},{24,28},{28,0},{1,5},{5... | collective-permute-start | bytes 1363976 | tf_op jit(solution)/shard_map/ppermute | solution.py:29
  191.3 33.1 %collective-permute-start.18 = (bf16[4,37,1536]{2,1,0:T(8,128)(2,1)S(1)}, bf16[4,37,1536]{2,1,0:T(8,128)(2,1)S(1)}, u32[]{:S(2)}, u32[]{:S(2)}) collective-permute-start(bf16[4,37,1536]{2,1,0:T(8,128)(2,1)S(1)} %pad_maximum_fusion.5), channel_id=1, source_target_pairs={{0,8},{4,12},{8,16},{12,20},{16,24},{20,28},{24,0},{28,4},{1,9},{5... | collective-permute-start | bytes 1363976 | tf_op jit(solution)/shard_map/ppermute | solution.py:29
  191.4 33.1 %collective-permute-start.19 = (bf16[4,37,1536]{2,1,0:T(8,128)(2,1)S(1)}, bf16[4,37,1536]{2,1,0:T(8,128)(2,1)S(1)}, u32[]{:S(2)}, u32[]{:S(2)}) collective-permute-start(bf16[4,37,1536]{2,1,0:T(8,128)(2,1)S(1)} %pad_maximum_fusion.5), channel_id=1, source_target_pairs={{0,12},{4,16},{8,20},{12,24},{16,28},{20,0},{24,4},{28,8},{1,13},{... | collective-permute-start | bytes 1363976 | tf_op jit(solution)/shard_map/ppermute | solution.py:29
  196.7 38.9 %collective-permute-start.20 = (bf16[4,37,1536]{2,1,0:T(8,128)(2,1)S(1)}, bf16[4,37,1536]{2,1,0:T(8,128)(2,1)S(1)}, u32[]{:S(2)}, u32[]{:S(2)}) collective-permute-start(bf16[4,37,1536]{2,1,0:T(8,128)(2,1)S(1)} %pad_maximum_fusion.5), channel_id=1, source_target_pairs={{0,16},{4,20},{8,24},{12,28},{16,0},{20,4},{24,8},{28,12},{1,17},{... | collective-permute-start | bytes 1363976 | tf_op jit(solution)/shard_map/ppermute | solution.py:29
  197.5 38.1 %collective-permute-start.21 = (bf16[4,37,1536]{2,1,0:T(8,128)(2,1)S(1)}, bf16[4,37,1536]{2,1,0:T(8,128)(2,1)S(1)}, u32[]{:S(2)}, u32[]{:S(2)}) collective-permute-start(bf16[4,37,1536]{2,1,0:T(8,128)(2,1)S(1)} %pad_maximum_fusion.5), channel_id=1, source_target_pairs={{0,20},{4,24},{8,28},{12,0},{16,4},{20,8},{24,12},{28,16},{1,21},{... | collective-permute-start | bytes 1363976 | tf_op jit(solution)/shard_map/ppermute | solution.py:29
  205.2 38.0 %collective-permute-start.22 = (bf16[4,37,1536]{2,1,0:T(8,128)(2,1)S(1)}, bf16[4,37,1536]{2,1,0:T(8,128)(2,1)S(1)}, u32[]{:S(2)}, u32[]{:S(2)}) collective-permute-start(bf16[4,37,1536]{2,1,0:T(8,128)(2,1)S(1)} %pad_maximum_fusion.5), channel_id=1, source_target_pairs={{0,24},{4,28},{8,0},{12,4},{16,8},{20,12},{24,16},{28,20},{1,25},{... | collective-permute-start | bytes 1363976 | tf_op jit(solution)/shard_map/ppermute | solution.py:29
  224.4 18.9 %collective-permute-start.23 = (bf16[4,37,1536]{2,1,0:T(8,128)(2,1)S(1)}, bf16[4,37,1536]{2,1,0:T(8,128)(2,1)S(1)}, u32[]{:S(2)}, u32[]{:S(2)}) collective-permute-start(bf16[4,37,1536]{2,1,0:T(8,128)(2,1)S(1)} %pad_maximum_fusion.5), channel_id=1, source_target_pairs={{0,28},{4,0},{8,4},{12,8},{16,12},{20,16},{24,20},{28,24},{1,29},{... | collective-permute-start | bytes 1363976 | tf_op jit(solution)/shard_map/ppermute | solution.py:29
  259.1 13.9 %collective-permute-start.24 = (bf16[4,37,1536]{2,1,0:T(8,128)(2,1)S(1)}, bf16[4,37,1536]{2,1,0:T(8,128)(2,1)S(1)}, u32[]{:S(2)}, u32[]{:S(2)}) collective-permute-start(bf16[4,37,1536]{2,1,0:T(8,128)(2,1)S(1)} %get-tuple-element.24), channel_id=1, source_target_pairs={{4,0},{8,4},{12,8},{16,12},{20,16},{24,20},{28,24},{0,28},{5,1},{9... | collective-permute-start | bytes 1363976 | tf_op jit(solution)/shard_map/ppermute | solution.py:37
  259.2 48.4 %collective-permute-start.25 = (bf16[4,37,1536]{2,1,0:T(8,128)(2,1)S(1)}, bf16[4,37,1536]{2,1,0:T(8,128)(2,1)S(1)}, u32[]{:S(2)}, u32[]{:S(2)}) collective-permute-start(bf16[4,37,1536]{2,1,0:T(8,128)(2,1)S(1)} %get-tuple-element.25), channel_id=1, source_target_pairs={{8,0},{12,4},{16,8},{20,12},{24,16},{28,20},{0,24},{4,28},{9,1},{1... | collective-permute-start | bytes 1363976 | tf_op jit(solution)/shard_map/ppermute | solution.py:37
  267.6 40.3 %collective-permute-start.26 = (bf16[4,37,1536]{2,1,0:T(8,128)(2,1)S(1)}, bf16[4,37,1536]{2,1,0:T(8,128)(2,1)S(1)}, u32[]{:S(2)}, u32[]{:S(2)}) collective-permute-start(bf16[4,37,1536]{2,1,0:T(8,128)(2,1)S(1)} %get-tuple-element.26), channel_id=1, source_target_pairs={{12,0},{16,4},{20,8},{24,12},{28,16},{0,20},{4,24},{8,28},{13,1},{... | collective-permute-start | bytes 1363976 | tf_op jit(solution)/shard_map/ppermute | solution.py:37
  267.6 40.2 %collective-permute-start.27 = (bf16[4,37,1536]{2,1,0:T(8,128)(2,1)S(1)}, bf16[4,37,1536]{2,1,0:T(8,128)(2,1)S(1)}, u32[]{:S(2)}, u32[]{:S(2)}) collective-permute-start(bf16[4,37,1536]{2,1,0:T(8,128)(2,1)S(1)} %get-tuple-element.27), channel_id=1, source_target_pairs={{16,0},{20,4},{24,8},{28,12},{0,16},{4,20},{8,24},{12,28},{17,1},{... | collective-permute-start | bytes 1363976 | tf_op jit(solution)/shard_map/ppermute | solution.py:37
  268.7 39.2 %collective-permute-start.28 = (bf16[4,37,1536]{2,1,0:T(8,128)(2,1)S(1)}, bf16[4,37,1536]{2,1,0:T(8,128)(2,1)S(1)}, u32[]{:S(2)}, u32[]{:S(2)}) collective-permute-start(bf16[4,37,1536]{2,1,0:T(8,128)(2,1)S(1)} %get-tuple-element.28), channel_id=1, source_target_pairs={{20,0},{24,4},{28,8},{0,12},{4,16},{8,20},{12,24},{16,28},{21,1},{... | collective-permute-start | bytes 1363976 | tf_op jit(solution)/shard_map/ppermute | solution.py:37
  273.0 34.9 %collective-permute-start.29 = (bf16[4,37,1536]{2,1,0:T(8,128)(2,1)S(1)}, bf16[4,37,1536]{2,1,0:T(8,128)(2,1)S(1)}, u32[]{:S(2)}, u32[]{:S(2)}) collective-permute-start(bf16[4,37,1536]{2,1,0:T(8,128)(2,1)S(1)} %get-tuple-element.30), channel_id=1, source_target_pairs={{24,0},{28,4},{0,8},{4,12},{8,16},{12,20},{16,24},{20,28},{25,1},{... | collective-permute-start | bytes 1363976 | tf_op jit(solution)/shard_map/ppermute | solution.py:37
  307.6 13.5 %collective-permute-start.30 = (bf16[4,37,1536]{2,1,0:T(8,128)(2,1)S(1)}, bf16[4,37,1536]{2,1,0:T(8,128)(2,1)S(1)}, u32[]{:S(2)}, u32[]{:S(2)}) collective-permute-start(bf16[4,37,1536]{2,1,0:T(8,128)(2,1)S(1)} %get-tuple-element.29), channel_id=1, source_target_pairs={{28,0},{0,4},{4,8},{8,12},{12,16},{16,20},{20,24},{24,28},{29,1},{... | collective-permute-start | bytes 1363976 | tf_op jit(solution)/shard_map/ppermute | solution.py:37
  333.3 8.8 %collective-permute-start.33 = (bf16[4,10,1,16]{3,2,1,0:T(2,128)(2,1)S(1)}, bf16[4,10,1,16]{3,2,1,0:T(2,128)(2,1)S(1)}, u32[]{:S(2)}, u32[]{:S(2)}) collective-permute-start(bf16[4,10,1,16]{3,2,1,0:T(2,128)(2,1)S(1)} %get-tuple-element.50), channel_id=1, source_target_pairs={{0,1},{1,2},{2,3},{4,5},{5,6},{6,7},{8,9},{9,10},{10,11},{12,13},{... | collective-permute-start | bytes 3848 | tf_op jit(solution)/shard_map/ppermute | solution.py:17
  (57 other events, 790.0 us)

commit v4 on v3

--- a/solution.py
+++ b/solution.py
@@ -48,9 +48,7 @@
     return parts
 
 
-def attention_kernel(query_ref, *refs):
-    *pair_refs, mask_ref, out_ref = refs
-    query = query_ref[...]
+def attention_sums(query, pair_refs, mask_ref, first):
     numerator = None
     denominator = None
     for block, pair_ref in enumerate(pair_refs):
@@ -58,26 +56,52 @@
         scores = lax.dot_general(
             query, pairs, (((1,), (1,)), ((), ())), preferred_element_type=jnp.float32
         ) * (1.0 / math.sqrt(HD))
-        weights = jnp.exp(scores) * mask_ref[block]
+        weights = jnp.exp(scores) * mask_ref[first + block]
         part_den = jnp.sum(weights, axis=1, keepdims=True)
         part_num = jnp.dot(weights.astype(jnp.bfloat16), pairs, preferred_element_type=jnp.float32)
         numerator = part_num if numerator is None else numerator + part_num
         denominator = part_den if denominator is None else denominator + part_den
-    out_ref[...] = (numerator / denominator).astype(out_ref.dtype)
+    return numerator, denominator
+
+
+def near_kernel(query_ref, *refs):
+    *pair_refs, mask_ref, num_ref, den_ref = refs
+    numerator, denominator = attention_sums(query_ref[...], pair_refs, mask_ref, 0)
+    num_ref[...] = numerator
+    den_ref[...] = denominator
+
+
+def far_kernel(query_ref, *refs):
+    *pair_refs, mask_ref, num_in_ref, den_in_ref, out_ref = refs
+    numerator, denominator = attention_sums(query_ref[...], pair_refs, mask_ref, len(pair_refs))
+    out_ref[...] = ((numerator + num_in_ref[...]) / (denominator + den_in_ref[...])).astype(out_ref.dtype)
 
 
 def attend(query_rows, pair_blocks, usable, heads, tile):
     requests, rows, lanes = query_rows.shape
     keys = pair_blocks[0].shape[0] // requests
+    half = len(pair_blocks) // 2
+    row_spec = pl.BlockSpec((None, rows, tile), lambda r, h: (r, 0, h))
+    pair_spec = pl.BlockSpec((keys, tile), lambda r, h: (r, h))
+    mask_spec = pl.BlockSpec((None, len(pair_blocks), 1, keys), lambda r, h: (r, 0, 0, 0))
+    den_spec = pl.BlockSpec((None, None, rows, 1), lambda r, h: (r, h, 0, 0))
+    numerator, denominator = pl.pallas_call(
+        near_kernel,
+        grid=(requests, heads),
+        in_specs=[row_spec] + [pair_spec] * half + [mask_spec],
+        out_specs=[row_spec, den_spec],
+        out_shape=[
+            jax.ShapeDtypeStruct((requests, rows, lanes), jnp.float32),
+            jax.ShapeDtypeStruct((requests, heads, rows, 1), jnp.float32),
+        ],
+    )(query_rows, *pair_blocks[:half], usable)
     return pl.pallas_call(
-        attention_kernel,
+        far_kernel,
         grid=(requests, heads),
-        in_specs=[pl.BlockSpec((None, rows, tile), lambda r, h: (r, 0, h))]
-        + [pl.BlockSpec((keys, tile), lambda r, h: (r, h)) for _ in pair_blocks]
-        + [pl.BlockSpec((None, len(pair_blocks), 1, keys), lambda r, h: (r, 0, 0, 0))],
-        out_specs=pl.BlockSpec((None, rows, tile), lambda r, h: (r, 0, h)),
+        in_specs=[row_spec] + [pair_spec] * half + [mask_spec, row_spec, den_spec],
+        out_specs=row_spec,
         out_shape=jax.ShapeDtypeStruct((requests, rows, lanes), jnp.bfloat16),
-    )(query_rows, *pair_blocks, usable)
+    )(query_rows, *pair_blocks[half:], usable, numerator, denominator)
 
 
 def per_request(vector, values, axis):

time: 351 us -> 360 us (1.026)
  Pallas kernels: 14.2 us -> 23 us
    pallas_call x1 -> x2, Pallas kernels: 14.2 us -> 23 us  [the longest x1 11.7 us: attend(): pl.pallas_call(near_kernel, grid=(requests, heads), in_specs=[row_spec] +...]
    unnamed x131 -> x127, local copies, waits for them, and re-layouts: 10.7 us -> 10.2 us
  transfers between devices with their start and end apart: 35 -> 35, of which waited for: 16 -> 17; matrix products, arithmetic and copies ran while one was open for 11% -> 11% of each run, Pallas kernels for 0% -> 3%
where the time goes in v4:
time: 360 us; the launch traced here: 355 us
  waiting for transfers between devices  171 us (48%)
  starting transfers between devices  76.4 us (21%)
  matrix products  36.5 us (10%)
  local copies, waits for them, and re-layouts  24.1 us (7%)
  Pallas kernels  23 us (6%)
  other arithmetic  21.8 us (6%)
    ppermute x14, waiting for transfers between devices, scatter_slots(): lax.ppermute(partial[shift], axis, [((i + shift) % count, i) for i in ran...  95.4 us
    ppermute x14, waiting for transfers between devices, gather_slots(): lax.ppermute(block, axis, [(i, (i + shift) % count) for i in range(count)])  62.2 us
    ppermute x14, starting transfers between devices, scatter_slots(): lax.ppermute(partial[shift], axis, [((i + shift) % count, i) for i in ran...  36.1 us
    ppermute x14, starting transfers between devices, gather_slots(): lax.ppermute(block, axis, [(i, (i + shift) % count) for i in range(count)])  25.4 us
    pallas_call x1, Pallas kernels, attend(): pl.pallas_call(near_kernel, grid=(requests, heads), in_specs=[row_spec] +...  11.7 us
    pallas_call x1, Pallas kernels, attend(): pl.pallas_call(far_kernel, grid=(requests, heads), in_specs=[row_spec] +...  11.2 us
    ppermute x1, waiting for transfers between devices, body(): far = lax.ppermute(own_pairs, 'blk', flip_chip)  10.6 us
    unnamed x127, local copies, waits for them, and re-layouts  10.2 us
  transfers between devices with their start and end apart: 35, of which 17 were waited for; matrix products, arithmetic and copies ran while one was open for 11% of the time, Pallas kernels for 3%

profile of v4, /device:TPU:1, one launch (start us, length us, event | category | flops | bytes accessed | tf_op | source)
XLA Modules:
  0.0 355.2 jit_solution(5048050307400268496)
XLA Ops:
  4.0 3.6 %collective-permute-start = (bf16[4,37,1536]{2,1,0:T(8,128)(2,1)}, bf16[4,37,1536]{2,1,0:T(8,128)(2,1)}, u32[]{:S(2)}, u32[]{:S(2)}) collective-permute-start(bf16[4,37,1536]{2,1,0:T(8,128)(2,1)} %get-tuple-element.51), channel_id=1, source_target_pairs={{0,4},{4,8},{8,12},{12,16},{16,20},{20,24},{24,28},{28,0},{1,5},{5... | collective-permute-start | bytes 1363976 | tf_op jit(solution)/shard_map/ppermute | solution.py:29
  12.8 5.2 %collective-permute-start.4 = (bf16[4,37,1536]{2,1,0:T(8,128)(2,1)}, bf16[4,37,1536]{2,1,0:T(8,128)(2,1)}, u32[]{:S(2)}, u32[]{:S(2)}) collective-permute-start(bf16[4,37,1536]{2,1,0:T(8,128)(2,1)} %get-tuple-element.51), channel_id=1, source_target_pairs={{0,20},{4,24},{8,28},{12,0},{16,4},{20,8},{24,12},{28,16},{1,21},{... | collective-permute-start | bytes 1363976 | tf_op jit(solution)/shard_map/ppermute | solution.py:29
  32.7 11.4 %collective-permute-done.1 = bf16[4,37,1536]{2,1,0:T(8,128)(2,1)} collective-permute-done((bf16[4,37,1536]{2,1,0:T(8,128)(2,1)}, bf16[4,37,1536]{2,1,0:T(8,128)(2,1)}, u32[]{:S(2)}, u32[]{:S(2)}) %collective-permute-start.1) | collective-permute-done | bytes 454688 | tf_op jit(solution)/shard_map/ppermute | solution.py:29
  46.4 9.3 %collective-permute-done.3 = bf16[4,37,1536]{2,1,0:T(8,128)(2,1)} collective-permute-done((bf16[4,37,1536]{2,1,0:T(8,128)(2,1)}, bf16[4,37,1536]{2,1,0:T(8,128)(2,1)}, u32[]{:S(2)}, u32[]{:S(2)}) %collective-permute-start.3) | collective-permute-done | bytes 454688 | tf_op jit(solution)/shard_map/ppermute | solution.py:29
  65.6 3.2 select_convert_fusion
  80.4 10.6 %collective-permute-done.7.refs_0_ = bf16[1184,384]{1,0:T(8,128)(2,1)} collective-permute-done((bf16[1184,384]{1,0:T(8,128)(2,1)}, bf16[1184,384]{1,0:T(8,128)(2,1)}, u32[]{:S(2)}, u32[]{:S(2)}) %collective-permute-start.7) | collective-permute-done | bytes 909344 | tf_op jit(solution)/shard_map/ppermute | solution.py:223
  93.3 4.0 %fusion.216 = f32[8,4,32,384]{3,2,1,0:T(8,128)S(1)} fusion(bf16[1536,384,1,1]{0,1,3,2:T(8,128)(2,1)S(1)} %bitcast.305, f32[8,4,37,1536]{3,2,1,0:T(8,128)} %copy-done.1, f32[4,1536]{1,0:T(4,128)S(1)} %copy-done.28, f32[4,1536]{1,0:T(4,128)S(1)} %bitcast.316, f32[8,4,32]{2,1,0:T(4,128)S(1)} %copy-done.35, f32[8,4,32]{2,1,0:T(4,128)S(1)} %broadcast_multiply_fusion.1), kind=kOutput, calls=%fused_computation.357 | convolution fusion | flops 1215823872 | bytes 9101312 | tf_op jit(solution)/shard_map/arnd,de->arne/dot_general | solution.py:153
  97.3 3.3 multiply_convert_fusion
  102.1 11.7 %shard_map.219 = (f32[4,296,384]{2,1,0:T(8,128)}, f32[4,3,296,1]{3,2,1,0:T(8,128)}) custom-call(bf16[4,296,384]{2,1,0:T(8,128)(2,1)} %copy.109.query_ref, bf16[1184,384]{1,0:T(8,128)(2,1)} %reshape.319.refs_0_, bf16[1184,384]{1,0:T(8,128)(2,1)} %collective-permute-done.9.refs_1_, f32[4,4,1,296]{3,2,1,0:T(1,128)} %or_convert_fusion.refs_2_), custom_call_target="tpu_custom_call" | custom-call | tf_op jit(solution)/shard_map/pallas_call | solution.py:88
  113.9 11.2 %shard_map.220 = bf16[4,296,384]{2,1,0:T(8,128)(2,1)} custom-call(bf16[4,296,384]{2,1,0:T(8,128)(2,1)} %copy.109.query_ref, bf16[1184,384]{1,0:T(8,128)(2,1)} %collective-permute-done.7.refs_0_, bf16[1184,384]{1,0:T(8,128)(2,1)} %collective-permute-done.8.refs_1_, f32[4,4,1,296]{3,2,1,0:T(1,128)} %or_convert_fusion.refs_2_, ...), custom_call_target="tpu_custom_call" | custom-call | tf_op jit(solution)/shard_map/pallas_call | solution.py:98
  129.8 7.1 %collective-permute-start.10 = (bf16[4,37,1536]{2,1,0:T(8,128)(2,1)S(1)}, bf16[4,37,1536]{2,1,0:T(8,128)(2,1)S(1)}, u32[]{:S(2)}, u32[]{:S(2)}) collective-permute-start(bf16[4,37,1536]{2,1,0:T(8,128)(2,1)S(1)} %get-tuple-element.35), channel_id=1, source_target_pairs={{4,0},{8,4},{12,8},{16,12},{20,16},{24,20},{28,24},{0,28},{5,1},{9... | collective-permute-start | bytes 1363976 | tf_op jit(solution)/shard_map/ppermute | solution.py:37
  136.9 4.1 %collective-permute-start.11 = (bf16[4,37,1536]{2,1,0:T(8,128)(2,1)S(1)}, bf16[4,37,1536]{2,1,0:T(8,128)(2,1)S(1)}, u32[]{:S(2)}, u32[]{:S(2)}) collective-permute-start(bf16[4,37,1536]{2,1,0:T(8,128)(2,1)S(1)} %get-tuple-element.36), channel_id=1, source_target_pairs={{8,0},{12,4},{16,8},{20,12},{24,16},{28,20},{0,24},{4,28},{9,1},{1... | collective-permute-start | bytes 1363976 | tf_op jit(solution)/shard_map/ppermute | solution.py:37
  141.0 3.7 %collective-permute-start.12 = (bf16[4,37,1536]{2,1,0:T(8,128)(2,1)S(1)}, bf16[4,37,1536]{2,1,0:T(8,128)(2,1)S(1)}, u32[]{:S(2)}, u32[]{:S(2)}) collective-permute-start(bf16[4,37,1536]{2,1,0:T(8,128)(2,1)S(1)} %get-tuple-element.37), channel_id=1, source_target_pairs={{12,0},{16,4},{20,8},{24,12},{28,16},{0,20},{4,24},{8,28},{13,1},{... | collective-permute-start | bytes 1363976 | tf_op jit(solution)/shard_map/ppermute | solution.py:37
  147.5 5.5 %collective-permute-start.15 = (bf16[4,37,1536]{2,1,0:T(8,128)(2,1)S(1)}, bf16[4,37,1536]{2,1,0:T(8,128)(2,1)S(1)}, u32[]{:S(2)}, u32[]{:S(2)}) collective-permute-start(bf16[4,37,1536]{2,1,0:T(8,128)(2,1)S(1)} %get-tuple-element.41), channel_id=1, source_target_pairs={{24,0},{28,4},{0,8},{4,12},{8,16},{12,20},{16,24},{20,28},{25,1},{... | collective-permute-start | bytes 1363976 | tf_op jit(solution)/shard_map/ppermute | solution.py:37
  153.0 29.9 %collective-permute-done.11 = bf16[4,37,1536]{2,1,0:T(8,128)(2,1)S(1)} collective-permute-done((bf16[4,37,1536]{2,1,0:T(8,128)(2,1)S(1)}, bf16[4,37,1536]{2,1,0:T(8,128)(2,1)S(1)}, u32[]{:S(2)}, u32[]{:S(2)}) %collective-permute-start.11) | collective-permute-done | bytes 454688 | tf_op jit(solution)/shard_map/ppermute | solution.py:37
  183.0 3.7 %collective-permute-done.15 = bf16[4,37,1536]{2,1,0:T(8,128)(2,1)S(1)} collective-permute-done((bf16[4,37,1536]{2,1,0:T(8,128)(2,1)S(1)}, bf16[4,37,1536]{2,1,0:T(8,128)(2,1)S(1)}, u32[]{:S(2)}, u32[]{:S(2)}) %collective-permute-start.15) | collective-permute-done | bytes 454688 | tf_op jit(solution)/shard_map/ppermute | solution.py:37
  186.7 11.3 %collective-permute-done.16 = bf16[4,37,1536]{2,1,0:T(8,128)(2,1)S(1)} collective-permute-done((bf16[4,37,1536]{2,1,0:T(8,128)(2,1)S(1)}, bf16[4,37,1536]{2,1,0:T(8,128)(2,1)S(1)}, u32[]{:S(2)}, u32[]{:S(2)}) %collective-permute-start.16) | collective-permute-done | bytes 454688 | tf_op jit(solution)/shard_map/ppermute | solution.py:37
  200.1 5.7 %collective-permute-start.19 = (bf16[4,37,1536]{2,1,0:T(8,128)(2,1)S(1)}, bf16[4,37,1536]{2,1,0:T(8,128)(2,1)S(1)}, u32[]{:S(2)}, u32[]{:S(2)}) collective-permute-start(bf16[4,37,1536]{2,1,0:T(8,128)(2,1)S(1)} %pad_maximum_fusion.5), channel_id=1, source_target_pairs={{0,12},{4,16},{8,20},{12,24},{16,28},{20,0},{24,4},{28,8},{1,13},{... | collective-permute-start | bytes 1363976 | tf_op jit(solution)/shard_map/ppermute | solution.py:29
  206.3 2.9 collective-permute-start.21
  209.2 5.0 %collective-permute-done.17 = bf16[4,37,1536]{2,1,0:T(8,128)(2,1)S(1)} collective-permute-done((bf16[4,37,1536]{2,1,0:T(8,128)(2,1)S(1)}, bf16[4,37,1536]{2,1,0:T(8,128)(2,1)S(1)}, u32[]{:S(2)}, u32[]{:S(2)}) %collective-permute-start.17) | collective-permute-done | bytes 454688 | tf_op jit(solution)/shard_map/ppermute | solution.py:29
  215.6 17.5 %collective-permute-done.18 = bf16[4,37,1536]{2,1,0:T(8,128)(2,1)S(1)} collective-permute-done((bf16[4,37,1536]{2,1,0:T(8,128)(2,1)S(1)}, bf16[4,37,1536]{2,1,0:T(8,128)(2,1)S(1)}, u32[]{:S(2)}, u32[]{:S(2)}) %collective-permute-start.18) | collective-permute-done | bytes 454688 | tf_op jit(solution)/shard_map/ppermute | solution.py:29
  233.2 11.4 %collective-permute-done.20 = bf16[4,37,1536]{2,1,0:T(8,128)(2,1)S(1)} collective-permute-done((bf16[4,37,1536]{2,1,0:T(8,128)(2,1)S(1)}, bf16[4,37,1536]{2,1,0:T(8,128)(2,1)S(1)}, u32[]{:S(2)}, u32[]{:S(2)}) %collective-permute-start.20) | collective-permute-done | bytes 454688 | tf_op jit(solution)/shard_map/ppermute | solution.py:29
  244.7 7.3 %collective-permute-done.22 = bf16[4,37,1536]{2,1,0:T(8,128)(2,1)S(1)} collective-permute-done((bf16[4,37,1536]{2,1,0:T(8,128)(2,1)S(1)}, bf16[4,37,1536]{2,1,0:T(8,128)(2,1)S(1)}, u32[]{:S(2)}, u32[]{:S(2)}) %collective-permute-start.22) | collective-permute-done | bytes 454688 | tf_op jit(solution)/shard_map/ppermute | solution.py:29
  253.0 4.1 %fusion.8 = bf16[8,4,32,768]{3,2,1,0:T(8,128)(2,1)} fusion(bf16[1536,768]{1,0:T(8,128)(2,1)S(1)} %copy-done.47, bf16[8,4,37,1536]{3,2,1,0:T(8,128)(2,1)S(1)} %bitcast_dynamic-update-slice_fusion), kind=kOutput, calls=%fused_computation.43 | convolution fusion | flops 2422996992 | bytes 7077888 | tf_op jit(solution)/shard_map/arnd,df->arnf/dot_general | solution.py:262
  257.1 4.7 %convolution_convert_fusion.3 = bf16[8,4,5,1536]{3,0,2,1:T(8,128)(2,1)} fusion(bf16[768,1536]{1,0:T(8,128)(2,1)} %param.37, bf16[1536,768]{1,0:T(8,128)(2,1)} %param.35, bf16[8,4,5,1536]{3,2,1,0:T(8,128)(2,1)} %slice.333), kind=kOutput, calls=%fused_computation.47 | convolution fusion | flops 756326400 | bytes 5701632 | tf_op jit(solution)/shard_map/arnf,fd->arnd/dot_general | solution.py:270
  263.0 4.2 %convolution_convert_fusion = bf16[8,4,32,1536]{3,2,1,0:T(8,128)(2,1)S(1)} fusion(bf16[8,4,32,768]{3,2,1,0:T(8,128)(2,1)} %fusion.8, bf16[768,1536]{1,0:T(8,128)(2,1)S(1)} %copy-done), kind=kOutput, calls=%fused_computation.19 | convolution fusion | flops 2417491968 | bytes 7077888 | tf_op jit(solution)/shard_map/arnf,fd->arnd/dot_general | solution.py:269
  267.8 9.1 %collective-permute-start.25 = (bf16[4,37,1536]{2,1,0:T(8,128)(2,1)S(1)}, bf16[4,37,1536]{2,1,0:T(8,128)(2,1)S(1)}, u32[]{:S(2)}, u32[]{:S(2)}) collective-permute-start(bf16[4,37,1536]{2,1,0:T(8,128)(2,1)S(1)} %get-tuple-element.29), channel_id=1, source_target_pairs={{8,0},{12,4},{16,8},{20,12},{24,16},{28,20},{0,24},{4,28},{9,1},{1... | collective-permute-start | bytes 1363976 | tf_op jit(solution)/shard_map/ppermute | solution.py:37
  278.1 2.8 collective-permute-start.28
  282.2 35.2 %collective-permute-done.25 = bf16[4,37,1536]{2,1,0:T(8,128)(2,1)S(1)} collective-permute-done((bf16[4,37,1536]{2,1,0:T(8,128)(2,1)S(1)}, bf16[4,37,1536]{2,1,0:T(8,128)(2,1)S(1)}, u32[]{:S(2)}, u32[]{:S(2)}) %collective-permute-start.25) | collective-permute-done | bytes 454688 | tf_op jit(solution)/shard_map/ppermute | solution.py:37
  317.7 13.7 %collective-permute-done.30 = bf16[4,37,1536]{2,1,0:T(8,128)(2,1)S(1)} collective-permute-done((bf16[4,37,1536]{2,1,0:T(8,128)(2,1)S(1)}, bf16[4,37,1536]{2,1,0:T(8,128)(2,1)S(1)}, u32[]{:S(2)}, u32[]{:S(2)}) %collective-permute-start.30) | collective-permute-done | bytes 454688 | tf_op jit(solution)/shard_map/ppermute | solution.py:37
  340.8 2.8 collective-permute-done.32
  345.6 6.0 %collective-permute-start.34 = (bf16[4,10,1,16]{3,2,1,0:T(2,128)(2,1)S(1)}, bf16[4,10,1,16]{3,2,1,0:T(2,128)(2,1)S(1)}, u32[]{:S(2)}, u32[]{:S(2)}) collective-permute-start(bf16[4,10,1,16]{3,2,1,0:T(2,128)(2,1)S(1)} %get-tuple-element.55), channel_id=1, source_target_pairs={{1,0},{2,1},{3,2},{5,4},{6,5},{7,6},{9,8},{10,9},{11,10},{13,12},{... | collective-permute-start | bytes 3848 | tf_op jit(solution)/shard_map/ppermute | solution.py:20
  (271 shorter events, 81.9 us)
Async XLA Ops:
  4.0 26.8 %collective-permute-start = (bf16[4,37,1536]{2,1,0:T(8,128)(2,1)}, bf16[4,37,1536]{2,1,0:T(8,128)(2,1)}, u32[]{:S(2)}, u32[]{:S(2)}) collective-permute-start(bf16[4,37,1536]{2,1,0:T(8,128)(2,1)} %get-tuple-element.51), channel_id=1, source_target_pairs={{0,4},{4,8},{8,12},{12,16},{16,20},{20,24},{24,28},{28,0},{1,5},{5... | collective-permute-start | bytes 1363976 | tf_op jit(solution)/shard_map/ppermute | solution.py:29
  7.6 36.5 %collective-permute-start.1 = (bf16[4,37,1536]{2,1,0:T(8,128)(2,1)}, bf16[4,37,1536]{2,1,0:T(8,128)(2,1)}, u32[]{:S(2)}, u32[]{:S(2)}) collective-permute-start(bf16[4,37,1536]{2,1,0:T(8,128)(2,1)} %get-tuple-element.51), channel_id=1, source_target_pairs={{0,8},{4,12},{8,16},{12,20},{16,24},{20,28},{24,0},{28,4},{1,9},{5... | collective-permute-start | bytes 1363976 | tf_op jit(solution)/shard_map/ppermute | solution.py:29
  9.2 36.1 %collective-permute-start.2 = (bf16[4,37,1536]{2,1,0:T(8,128)(2,1)}, bf16[4,37,1536]{2,1,0:T(8,128)(2,1)}, u32[]{:S(2)}, u32[]{:S(2)}) collective-permute-start(bf16[4,37,1536]{2,1,0:T(8,128)(2,1)} %get-tuple-element.51), channel_id=1, source_target_pairs={{0,12},{4,16},{8,20},{12,24},{16,28},{20,0},{24,4},{28,8},{1,13},{... | collective-permute-start | bytes 1363976 | tf_op jit(solution)/shard_map/ppermute | solution.py:29
  11.9 43.9 %collective-permute-start.3 = (bf16[4,37,1536]{2,1,0:T(8,128)(2,1)}, bf16[4,37,1536]{2,1,0:T(8,128)(2,1)}, u32[]{:S(2)}, u32[]{:S(2)}) collective-permute-start(bf16[4,37,1536]{2,1,0:T(8,128)(2,1)} %get-tuple-element.51), channel_id=1, source_target_pairs={{0,16},{4,20},{8,24},{12,28},{16,0},{20,4},{24,8},{28,12},{1,17},{... | collective-permute-start | bytes 1363976 | tf_op jit(solution)/shard_map/ppermute | solution.py:29
  12.8 44.1 %collective-permute-start.4 = (bf16[4,37,1536]{2,1,0:T(8,128)(2,1)}, bf16[4,37,1536]{2,1,0:T(8,128)(2,1)}, u32[]{:S(2)}, u32[]{:S(2)}) collective-permute-start(bf16[4,37,1536]{2,1,0:T(8,128)(2,1)} %get-tuple-element.51), channel_id=1, source_target_pairs={{0,20},{4,24},{8,28},{12,0},{16,4},{20,8},{24,12},{28,16},{1,21},{... | collective-permute-start | bytes 1363976 | tf_op jit(solution)/shard_map/ppermute | solution.py:29
  30.9 27.1 %collective-permute-start.5 = (bf16[4,37,1536]{2,1,0:T(8,128)(2,1)}, bf16[4,37,1536]{2,1,0:T(8,128)(2,1)S(1)}, u32[]{:S(2)}, u32[]{:S(2)}) collective-permute-start(bf16[4,37,1536]{2,1,0:T(8,128)(2,1)} %get-tuple-element.51), channel_id=1, source_target_pairs={{0,24},{4,28},{8,0},{12,4},{16,8},{20,12},{24,16},{28,20},{1,25},{... | collective-permute-start | bytes 1363976 | tf_op jit(solution)/shard_map/ppermute | solution.py:29
  44.1 14.2 %collective-permute-start.6 = (bf16[4,37,1536]{2,1,0:T(8,128)(2,1)}, bf16[4,37,1536]{2,1,0:T(8,128)(2,1)S(1)}, u32[]{:S(2)}, u32[]{:S(2)}) collective-permute-start(bf16[4,37,1536]{2,1,0:T(8,128)(2,1)} %get-tuple-element.51), channel_id=1, source_target_pairs={{0,28},{4,0},{8,4},{12,8},{16,12},{20,16},{24,20},{28,24},{1,29},{... | collective-permute-start | bytes 1363976 | tf_op jit(solution)/shard_map/ppermute | solution.py:29
  70.4 20.6 %collective-permute-start.7 = (bf16[1184,384]{1,0:T(8,128)(2,1)}, bf16[1184,384]{1,0:T(8,128)(2,1)}, u32[]{:S(2)}, u32[]{:S(2)}) collective-permute-start(bf16[1184,384]{1,0:T(8,128)(2,1)} %reshape.319.refs_0_), channel_id=1, source_target_pairs={{0,2},{1,3},{2,0},{3,1},{4,6},{5,7},{6,4},{7,5},{8,10},{9,11},{10,... | collective-permute-start | bytes 2727944 | tf_op jit(solution)/shard_map/ppermute | solution.py:223
  75.2 26.9 %collective-permute-start.9 = (bf16[1184,384]{1,0:T(8,128)(2,1)S(1)}, bf16[1184,384]{1,0:T(8,128)(2,1)}, u32[]{:S(2)}, u32[]{:S(2)}) collective-permute-start(bf16[1184,384]{1,0:T(8,128)(2,1)S(1)} %copy-done.5), channel_id=1, source_target_pairs={{0,1},{1,0},{2,3},{3,2},{4,5},{5,4},{6,7},{7,6},{8,9},{9,8},{10,11... | collective-permute-start | bytes 2727944 | tf_op jit(solution)/shard_map/ppermute | solution.py:226
  91.0 22.8 %collective-permute-start.8 = (bf16[1184,384]{1,0:T(8,128)(2,1)}, bf16[1184,384]{1,0:T(8,128)(2,1)}, u32[]{:S(2)}, u32[]{:S(2)}) collective-permute-start(bf16[1184,384]{1,0:T(8,128)(2,1)} %collective-permute-done.7.refs_0_), channel_id=1, source_target_pairs={{0,1},{1,0},{2,3},{3,2},{4,5},{5,4},{6,7},{7,6},{8,9},{9,8},{10,11... | collective-permute-start | bytes 2727944 | tf_op jit(solution)/shard_map/ppermute | solution.py:228
  129.8 17.7 %collective-permute-start.10 = (bf16[4,37,1536]{2,1,0:T(8,128)(2,1)S(1)}, bf16[4,37,1536]{2,1,0:T(8,128)(2,1)S(1)}, u32[]{:S(2)}, u32[]{:S(2)}) collective-permute-start(bf16[4,37,1536]{2,1,0:T(8,128)(2,1)S(1)} %get-tuple-element.35), channel_id=1, source_target_pairs={{4,0},{8,4},{12,8},{16,12},{20,16},{24,20},{28,24},{0,28},{5,1},{9... | collective-permute-start | bytes 1363976 | tf_op jit(solution)/shard_map/ppermute | solution.py:37
  136.9 45.9 %collective-permute-start.11 = (bf16[4,37,1536]{2,1,0:T(8,128)(2,1)S(1)}, bf16[4,37,1536]{2,1,0:T(8,128)(2,1)S(1)}, u32[]{:S(2)}, u32[]{:S(2)}) collective-permute-start(bf16[4,37,1536]{2,1,0:T(8,128)(2,1)S(1)} %get-tuple-element.36), channel_id=1, source_target_pairs={{8,0},{12,4},{16,8},{20,12},{24,16},{28,20},{0,24},{4,28},{9,1},{1... | collective-permute-start | bytes 1363976 | tf_op jit(solution)/shard_map/ppermute | solution.py:37
  141.0 41.9 %collective-permute-start.12 = (bf16[4,37,1536]{2,1,0:T(8,128)(2,1)S(1)}, bf16[4,37,1536]{2,1,0:T(8,128)(2,1)S(1)}, u32[]{:S(2)}, u32[]{:S(2)}) collective-permute-start(bf16[4,37,1536]{2,1,0:T(8,128)(2,1)S(1)} %get-tuple-element.37), channel_id=1, source_target_pairs={{12,0},{16,4},{20,8},{24,12},{28,16},{0,20},{4,24},{8,28},{13,1},{... | collective-permute-start | bytes 1363976 | tf_op jit(solution)/shard_map/ppermute | solution.py:37
  144.8 38.2 %collective-permute-start.13 = (bf16[4,37,1536]{2,1,0:T(8,128)(2,1)S(1)}, bf16[4,37,1536]{2,1,0:T(8,128)(2,1)S(1)}, u32[]{:S(2)}, u32[]{:S(2)}) collective-permute-start(bf16[4,37,1536]{2,1,0:T(8,128)(2,1)S(1)} %get-tuple-element.38), channel_id=1, source_target_pairs={{16,0},{20,4},{24,8},{28,12},{0,16},{4,20},{8,24},{12,28},{17,1},{... | collective-permute-start | bytes 1363976 | tf_op jit(solution)/shard_map/ppermute | solution.py:37
  144.8 38.2 %collective-permute-start.14 = (bf16[4,37,1536]{2,1,0:T(8,128)(2,1)S(1)}, bf16[4,37,1536]{2,1,0:T(8,128)(2,1)S(1)}, u32[]{:S(2)}, u32[]{:S(2)}) collective-permute-start(bf16[4,37,1536]{2,1,0:T(8,128)(2,1)S(1)} %get-tuple-element.39), channel_id=1, source_target_pairs={{20,0},{24,4},{28,8},{0,12},{4,16},{8,20},{12,24},{16,28},{21,1},{... | collective-permute-start | bytes 1363976 | tf_op jit(solution)/shard_map/ppermute | solution.py:37
  147.5 39.2 %collective-permute-start.15 = (bf16[4,37,1536]{2,1,0:T(8,128)(2,1)S(1)}, bf16[4,37,1536]{2,1,0:T(8,128)(2,1)S(1)}, u32[]{:S(2)}, u32[]{:S(2)}) collective-permute-start(bf16[4,37,1536]{2,1,0:T(8,128)(2,1)S(1)} %get-tuple-element.41), channel_id=1, source_target_pairs={{24,0},{28,4},{0,8},{4,12},{8,16},{12,20},{16,24},{20,28},{25,1},{... | collective-permute-start | bytes 1363976 | tf_op jit(solution)/shard_map/ppermute | solution.py:37
  182.9 15.1 %collective-permute-start.16 = (bf16[4,37,1536]{2,1,0:T(8,128)(2,1)S(1)}, bf16[4,37,1536]{2,1,0:T(8,128)(2,1)S(1)}, u32[]{:S(2)}, u32[]{:S(2)}) collective-permute-start(bf16[4,37,1536]{2,1,0:T(8,128)(2,1)S(1)} %get-tuple-element.40), channel_id=1, source_target_pairs={{28,0},{0,4},{4,8},{8,12},{12,16},{16,20},{20,24},{24,28},{29,1},{... | collective-permute-start | bytes 1363976 | tf_op jit(solution)/shard_map/ppermute | solution.py:37
  199.9 14.2 %collective-permute-start.17 = (bf16[4,37,1536]{2,1,0:T(8,128)(2,1)S(1)}, bf16[4,37,1536]{2,1,0:T(8,128)(2,1)S(1)}, u32[]{:S(2)}, u32[]{:S(2)}) collective-permute-start(bf16[4,37,1536]{2,1,0:T(8,128)(2,1)S(1)} %pad_maximum_fusion.5), channel_id=1, source_target_pairs={{0,4},{4,8},{8,12},{12,16},{16,20},{20,24},{24,28},{28,0},{1,5},{5... | collective-permute-start | bytes 1363976 | tf_op jit(solution)/shard_map/ppermute | solution.py:29
  200.0 33.1 %collective-permute-start.18 = (bf16[4,37,1536]{2,1,0:T(8,128)(2,1)S(1)}, bf16[4,37,1536]{2,1,0:T(8,128)(2,1)S(1)}, u32[]{:S(2)}, u32[]{:S(2)}) collective-permute-start(bf16[4,37,1536]{2,1,0:T(8,128)(2,1)S(1)} %pad_maximum_fusion.5), channel_id=1, source_target_pairs={{0,8},{4,12},{8,16},{12,20},{16,24},{20,28},{24,0},{28,4},{1,9},{5... | collective-permute-start | bytes 1363976 | tf_op jit(solution)/shard_map/ppermute | solution.py:29
  200.1 33.1 %collective-permute-start.19 = (bf16[4,37,1536]{2,1,0:T(8,128)(2,1)S(1)}, bf16[4,37,1536]{2,1,0:T(8,128)(2,1)S(1)}, u32[]{:S(2)}, u32[]{:S(2)}) collective-permute-start(bf16[4,37,1536]{2,1,0:T(8,128)(2,1)S(1)} %pad_maximum_fusion.5), channel_id=1, source_target_pairs={{0,12},{4,16},{8,20},{12,24},{16,28},{20,0},{24,4},{28,8},{1,13},{... | collective-permute-start | bytes 1363976 | tf_op jit(solution)/shard_map/ppermute | solution.py:29
  205.8 38.9 %collective-permute-start.20 = (bf16[4,37,1536]{2,1,0:T(8,128)(2,1)S(1)}, bf16[4,37,1536]{2,1,0:T(8,128)(2,1)S(1)}, u32[]{:S(2)}, u32[]{:S(2)}) collective-permute-start(bf16[4,37,1536]{2,1,0:T(8,128)(2,1)S(1)} %pad_maximum_fusion.5), channel_id=1, source_target_pairs={{0,16},{4,20},{8,24},{12,28},{16,0},{20,4},{24,8},{28,12},{1,17},{... | collective-permute-start | bytes 1363976 | tf_op jit(solution)/shard_map/ppermute | solution.py:29
  206.3 38.4 %collective-permute-start.21 = (bf16[4,37,1536]{2,1,0:T(8,128)(2,1)S(1)}, bf16[4,37,1536]{2,1,0:T(8,128)(2,1)S(1)}, u32[]{:S(2)}, u32[]{:S(2)}) collective-permute-start(bf16[4,37,1536]{2,1,0:T(8,128)(2,1)S(1)} %pad_maximum_fusion.5), channel_id=1, source_target_pairs={{0,20},{4,24},{8,28},{12,0},{16,4},{20,8},{24,12},{28,16},{1,21},{... | collective-permute-start | bytes 1363976 | tf_op jit(solution)/shard_map/ppermute | solution.py:29
  214.2 37.8 %collective-permute-start.22 = (bf16[4,37,1536]{2,1,0:T(8,128)(2,1)S(1)}, bf16[4,37,1536]{2,1,0:T(8,128)(2,1)S(1)}, u32[]{:S(2)}, u32[]{:S(2)}) collective-permute-start(bf16[4,37,1536]{2,1,0:T(8,128)(2,1)S(1)} %pad_maximum_fusion.5), channel_id=1, source_target_pairs={{0,24},{4,28},{8,0},{12,4},{16,8},{20,12},{24,16},{28,20},{1,25},{... | collective-permute-start | bytes 1363976 | tf_op jit(solution)/shard_map/ppermute | solution.py:29
  233.1 18.9 %collective-permute-start.23 = (bf16[4,37,1536]{2,1,0:T(8,128)(2,1)S(1)}, bf16[4,37,1536]{2,1,0:T(8,128)(2,1)S(1)}, u32[]{:S(2)}, u32[]{:S(2)}) collective-permute-start(bf16[4,37,1536]{2,1,0:T(8,128)(2,1)S(1)} %pad_maximum_fusion.5), channel_id=1, source_target_pairs={{0,28},{4,0},{8,4},{12,8},{16,12},{20,16},{24,20},{28,24},{1,29},{... | collective-permute-start | bytes 1363976 | tf_op jit(solution)/shard_map/ppermute | solution.py:29
  267.7 13.9 %collective-permute-start.24 = (bf16[4,37,1536]{2,1,0:T(8,128)(2,1)S(1)}, bf16[4,37,1536]{2,1,0:T(8,128)(2,1)S(1)}, u32[]{:S(2)}, u32[]{:S(2)}) collective-permute-start(bf16[4,37,1536]{2,1,0:T(8,128)(2,1)S(1)} %get-tuple-element.28), channel_id=1, source_target_pairs={{4,0},{8,4},{12,8},{16,12},{20,16},{24,20},{28,24},{0,28},{5,1},{9... | collective-permute-start | bytes 1363976 | tf_op jit(solution)/shard_map/ppermute | solution.py:37
  267.8 49.6 %collective-permute-start.25 = (bf16[4,37,1536]{2,1,0:T(8,128)(2,1)S(1)}, bf16[4,37,1536]{2,1,0:T(8,128)(2,1)S(1)}, u32[]{:S(2)}, u32[]{:S(2)}) collective-permute-start(bf16[4,37,1536]{2,1,0:T(8,128)(2,1)S(1)} %get-tuple-element.29), channel_id=1, source_target_pairs={{8,0},{12,4},{16,8},{20,12},{24,16},{28,20},{0,24},{4,28},{9,1},{1... | collective-permute-start | bytes 1363976 | tf_op jit(solution)/shard_map/ppermute | solution.py:37
  277.0 40.7 %collective-permute-start.26 = (bf16[4,37,1536]{2,1,0:T(8,128)(2,1)S(1)}, bf16[4,37,1536]{2,1,0:T(8,128)(2,1)S(1)}, u32[]{:S(2)}, u32[]{:S(2)}) collective-permute-start(bf16[4,37,1536]{2,1,0:T(8,128)(2,1)S(1)} %get-tuple-element.30), channel_id=1, source_target_pairs={{12,0},{16,4},{20,8},{24,12},{28,16},{0,20},{4,24},{8,28},{13,1},{... | collective-permute-start | bytes 1363976 | tf_op jit(solution)/shard_map/ppermute | solution.py:37
  277.0 40.6 %collective-permute-start.27 = (bf16[4,37,1536]{2,1,0:T(8,128)(2,1)S(1)}, bf16[4,37,1536]{2,1,0:T(8,128)(2,1)S(1)}, u32[]{:S(2)}, u32[]{:S(2)}) collective-permute-start(bf16[4,37,1536]{2,1,0:T(8,128)(2,1)S(1)} %get-tuple-element.31), channel_id=1, source_target_pairs={{16,0},{20,4},{24,8},{28,12},{0,16},{4,20},{8,24},{12,28},{17,1},{... | collective-permute-start | bytes 1363976 | tf_op jit(solution)/shard_map/ppermute | solution.py:37
  278.1 39.6 %collective-permute-start.28 = (bf16[4,37,1536]{2,1,0:T(8,128)(2,1)S(1)}, bf16[4,37,1536]{2,1,0:T(8,128)(2,1)S(1)}, u32[]{:S(2)}, u32[]{:S(2)}) collective-permute-start(bf16[4,37,1536]{2,1,0:T(8,128)(2,1)S(1)} %get-tuple-element.32), channel_id=1, source_target_pairs={{20,0},{24,4},{28,8},{0,12},{4,16},{8,20},{12,24},{16,28},{21,1},{... | collective-permute-start | bytes 1363976 | tf_op jit(solution)/shard_map/ppermute | solution.py:37
  281.6 36.1 %collective-permute-start.29 = (bf16[4,37,1536]{2,1,0:T(8,128)(2,1)S(1)}, bf16[4,37,1536]{2,1,0:T(8,128)(2,1)S(1)}, u32[]{:S(2)}, u32[]{:S(2)}) collective-permute-start(bf16[4,37,1536]{2,1,0:T(8,128)(2,1)S(1)} %get-tuple-element.34), channel_id=1, source_target_pairs={{24,0},{28,4},{0,8},{4,12},{8,16},{12,20},{16,24},{20,28},{25,1},{... | collective-permute-start | bytes 1363976 | tf_op jit(solution)/shard_map/ppermute | solution.py:37
  317.4 14.0 %collective-permute-start.30 = (bf16[4,37,1536]{2,1,0:T(8,128)(2,1)S(1)}, bf16[4,37,1536]{2,1,0:T(8,128)(2,1)S(1)}, u32[]{:S(2)}, u32[]{:S(2)}) collective-permute-start(bf16[4,37,1536]{2,1,0:T(8,128)(2,1)S(1)} %get-tuple-element.33), channel_id=1, source_target_pairs={{28,0},{0,4},{4,8},{8,12},{12,16},{16,20},{20,24},{24,28},{29,1},{... | collective-permute-start | bytes 1363976 | tf_op jit(solution)/shard_map/ppermute | solution.py:37
  343.6 8.5 %collective-permute-start.33 = (bf16[4,10,1,16]{3,2,1,0:T(2,128)(2,1)S(1)}, bf16[4,10,1,16]{3,2,1,0:T(2,128)(2,1)S(1)}, u32[]{:S(2)}, u32[]{:S(2)}) collective-permute-start(bf16[4,10,1,16]{3,2,1,0:T(2,128)(2,1)S(1)} %get-tuple-element.54), channel_id=1, source_target_pairs={{0,1},{1,2},{2,3},{4,5},{5,6},{6,7},{8,9},{9,10},{10,11},{12,13},{... | collective-permute-start | bytes 3848 | tf_op jit(solution)/shard_map/ppermute | solution.py:17
  (55 other events, 830.4 us)

commit v5 on v3

--- a/solution.py
+++ b/solution.py
@@ -136,15 +136,16 @@
 def convolve(padded, kernel):
     out_rows = padded.shape[1] - 2
     out_cols = padded.shape[2] - 2
-    summed = jnp.zeros((padded.shape[0], out_rows, out_cols, kernel.shape[-1]), jnp.float32)
-    for row_off in range(3):
-        for col_off in range(3):
-            summed = summed + jnp.einsum(
-                "rhwc,co->rhwo",
-                padded[:, row_off : row_off + out_rows, col_off : col_off + out_cols],
-                kernel[row_off, col_off],
-                preferred_element_type=jnp.float32,
-            )
+    taps = jnp.concatenate(
+        [
+            padded[:, row_off : row_off + out_rows, col_off : col_off + out_cols]
+            for row_off in range(3)
+            for col_off in range(3)
+        ],
+        -1,
+    )
+    flat_kernel = kernel.reshape(-1, kernel.shape[-1])
+    summed = jnp.einsum("rhwc,co->rhwo", taps, flat_kernel, preferred_element_type=jnp.float32)
     return summed.astype(jnp.bfloat16)
 
 

time: 351 us -> 354 us (level)
    unnamed x131 -> x129, local copies, waits for them, and re-layouts: 10.7 us -> 11.1 us
  transfers between devices with their start and end apart: 35 -> 35, of which waited for: 16 -> 17; matrix products, arithmetic and copies ran while one was open for 11% -> 10% of each run, Pallas kernels for 0% -> 0%
where the time goes in v5:
time: 354 us; the launch traced here: 348 us
  waiting for transfers between devices  171 us (48%)
  starting transfers between devices  76.6 us (22%)
  matrix products  35.2 us (10%)
  local copies, waits for them, and re-layouts  27.2 us (8%)
  other arithmetic  21.7 us (6%)
  Pallas kernels  14.2 us (4%)
    ppermute x14, waiting for transfers between devices, scatter_slots(): lax.ppermute(partial[shift], axis, [((i + shift) % count, i) for i in ran...  94.4 us
    ppermute x14, waiting for transfers between devices, gather_slots(): lax.ppermute(block, axis, [(i, (i + shift) % count) for i in range(count)])  62.4 us
    ppermute x14, starting transfers between devices, scatter_slots(): lax.ppermute(partial[shift], axis, [((i + shift) % count, i) for i in ran...  36.5 us
    ppermute x14, starting transfers between devices, gather_slots(): lax.ppermute(block, axis, [(i, (i + shift) % count) for i in range(count)])  25.4 us
    pallas_call x1, Pallas kernels, attend(): pl.pallas_call(attention_kernel, grid=(requests, heads), in_specs=[pl.Blo...  14.2 us
    unnamed x129, local copies, waits for them, and re-layouts  11.1 us
    ppermute x1, waiting for transfers between devices, body(): far = lax.ppermute(own_pairs, 'blk', flip_chip)  10.5 us
    dot_general x4, matrix products, normalized(): jnp.dot(values * values, spread, precision=lax.Precision.HIGHEST)  8.49 us
  transfers between devices with their start and end apart: 35, of which 17 were waited for; matrix products, arithmetic and copies ran while one was open for 10% of the time, Pallas kernels for 0%

profile of v5, /device:TPU:1, one launch (start us, length us, event | category | flops | bytes accessed | tf_op | source)
XLA Modules:
  0.0 348.2 jit_solution(10084642758838687203)
XLA Ops:
  4.0 3.6 %collective-permute-start = (bf16[4,37,1536]{2,1,0:T(8,128)(2,1)}, bf16[4,37,1536]{2,1,0:T(8,128)(2,1)}, u32[]{:S(2)}, u32[]{:S(2)}) collective-permute-start(bf16[4,37,1536]{2,1,0:T(8,128)(2,1)} %get-tuple-element.47), channel_id=1, source_target_pairs={{0,4},{4,8},{8,12},{12,16},{16,20},{20,24},{24,28},{28,0},{1,5},{5... | collective-permute-start | bytes 1363976 | tf_op jit(solution)/shard_map/ppermute | solution.py:29
  9.2 2.6 collective-permute-start.2
  12.8 5.2 %collective-permute-start.4 = (bf16[4,37,1536]{2,1,0:T(8,128)(2,1)}, bf16[4,37,1536]{2,1,0:T(8,128)(2,1)}, u32[]{:S(2)}, u32[]{:S(2)}) collective-permute-start(bf16[4,37,1536]{2,1,0:T(8,128)(2,1)} %get-tuple-element.47), channel_id=1, source_target_pairs={{0,20},{4,24},{8,28},{12,0},{16,4},{20,8},{24,12},{28,16},{1,21},{... | collective-permute-start | bytes 1363976 | tf_op jit(solution)/shard_map/ppermute | solution.py:29
  32.5 11.6 %collective-permute-done.1 = bf16[4,37,1536]{2,1,0:T(8,128)(2,1)} collective-permute-done((bf16[4,37,1536]{2,1,0:T(8,128)(2,1)}, bf16[4,37,1536]{2,1,0:T(8,128)(2,1)}, u32[]{:S(2)}, u32[]{:S(2)}) %collective-permute-start.1) | collective-permute-done | bytes 454688 | tf_op jit(solution)/shard_map/ppermute | solution.py:29
  46.4 9.3 %collective-permute-done.3 = bf16[4,37,1536]{2,1,0:T(8,128)(2,1)} collective-permute-done((bf16[4,37,1536]{2,1,0:T(8,128)(2,1)}, bf16[4,37,1536]{2,1,0:T(8,128)(2,1)}, u32[]{:S(2)}, u32[]{:S(2)}) %collective-permute-start.3) | collective-permute-done | bytes 454688 | tf_op jit(solution)/shard_map/ppermute | solution.py:29
  65.6 3.2 select_convert_fusion
  80.3 10.5 %collective-permute-done.8.refs_2_ = bf16[1184,384]{1,0:T(8,128)(2,1)S(1)} collective-permute-done((bf16[1184,384]{1,0:T(8,128)(2,1)}, bf16[1184,384]{1,0:T(8,128)(2,1)S(1)}, u32[]{:S(2)}, u32[]{:S(2)}) %collective-permute-start.8) | collective-permute-done | bytes 909344 | tf_op jit(solution)/shard_map/ppermute | solution.py:200
  93.1 4.0 %fusion.170 = f32[8,4,32,384]{3,2,1,0:T(8,128)S(1)} fusion(bf16[1536,384,1,1]{0,1,3,2:T(8,128)(2,1)S(1)} %bitcast.248, f32[8,4,37,1536]{3,2,1,0:T(8,128)} %copy-done.1, f32[4,1536]{1,0:T(4,128)S(1)} %copy-done.29, f32[4,1536]{1,0:T(4,128)S(1)} %bitcast.260, f32[8,4,32]{2,1,0:T(4,128)S(1)} %copy-done.36, f32[8,4,32]{2,1,0:T(4,128)S(1)} %broadcast_multiply_fusion.1), kind=kOutput, calls=%fused_computation.312 | convolution fusion | flops 1215823872 | bytes 9101312 | tf_op jit(solution)/shard_map/arnd,de->arne/dot_general | solution.py:129
  97.2 3.3 multiply_convert_fusion
  102.9 14.2 %shard_map.219 = bf16[4,296,384]{2,1,0:T(8,128)(2,1)} custom-call(bf16[4,296,384]{2,1,0:T(8,128)(2,1)} %copy.107.query_ref, bf16[1184,384]{1,0:T(8,128)(2,1)} %reshape.322.refs_0_, bf16[1184,384]{1,0:T(8,128)(2,1)} %copy-done.10, bf16[1184,384]{1,0:T(8,128)(2,1)} %copy-done.9, bf16[1184,384]{1,0:T(8,128)(2,1)} %collective-permute-done.9.refs_3_, ...), custom_call_target="tpu_custom_call" | custom-call | tf_op jit(solution)/shard_map/pallas_call | solution.py:72
  121.8 7.0 %collective-permute-start.10 = (bf16[4,37,1536]{2,1,0:T(8,128)(2,1)S(1)}, bf16[4,37,1536]{2,1,0:T(8,128)(2,1)S(1)}, u32[]{:S(2)}, u32[]{:S(2)}) collective-permute-start(bf16[4,37,1536]{2,1,0:T(8,128)(2,1)S(1)} %get-tuple-element.31), channel_id=1, source_target_pairs={{4,0},{8,4},{12,8},{16,12},{20,16},{24,20},{28,24},{0,28},{5,1},{9... | collective-permute-start | bytes 1363976 | tf_op jit(solution)/shard_map/ppermute | solution.py:37
  128.8 4.3 %collective-permute-start.11 = (bf16[4,37,1536]{2,1,0:T(8,128)(2,1)S(1)}, bf16[4,37,1536]{2,1,0:T(8,128)(2,1)S(1)}, u32[]{:S(2)}, u32[]{:S(2)}) collective-permute-start(bf16[4,37,1536]{2,1,0:T(8,128)(2,1)S(1)} %get-tuple-element.32), channel_id=1, source_target_pairs={{8,0},{12,4},{16,8},{20,12},{24,16},{28,20},{0,24},{4,28},{9,1},{1... | collective-permute-start | bytes 1363976 | tf_op jit(solution)/shard_map/ppermute | solution.py:37
  133.1 3.3 collective-permute-start.12
  139.1 5.7 %collective-permute-start.15 = (bf16[4,37,1536]{2,1,0:T(8,128)(2,1)S(1)}, bf16[4,37,1536]{2,1,0:T(8,128)(2,1)S(1)}, u32[]{:S(2)}, u32[]{:S(2)}) collective-permute-start(bf16[4,37,1536]{2,1,0:T(8,128)(2,1)S(1)} %get-tuple-element.37), channel_id=1, source_target_pairs={{24,0},{28,4},{0,8},{4,12},{8,16},{12,20},{16,24},{20,28},{25,1},{... | collective-permute-start | bytes 1363976 | tf_op jit(solution)/shard_map/ppermute | solution.py:37
  144.8 29.7 %collective-permute-done.11 = bf16[4,37,1536]{2,1,0:T(8,128)(2,1)S(1)} collective-permute-done((bf16[4,37,1536]{2,1,0:T(8,128)(2,1)S(1)}, bf16[4,37,1536]{2,1,0:T(8,128)(2,1)S(1)}, u32[]{:S(2)}, u32[]{:S(2)}) %collective-permute-start.11) | collective-permute-done | bytes 454688 | tf_op jit(solution)/shard_map/ppermute | solution.py:37
  174.7 3.7 %collective-permute-done.15 = bf16[4,37,1536]{2,1,0:T(8,128)(2,1)S(1)} collective-permute-done((bf16[4,37,1536]{2,1,0:T(8,128)(2,1)S(1)}, bf16[4,37,1536]{2,1,0:T(8,128)(2,1)S(1)}, u32[]{:S(2)}, u32[]{:S(2)}) %collective-permute-start.15) | collective-permute-done | bytes 454688 | tf_op jit(solution)/shard_map/ppermute | solution.py:37
  178.3 10.9 %collective-permute-done.16 = bf16[4,37,1536]{2,1,0:T(8,128)(2,1)S(1)} collective-permute-done((bf16[4,37,1536]{2,1,0:T(8,128)(2,1)S(1)}, bf16[4,37,1536]{2,1,0:T(8,128)(2,1)S(1)}, u32[]{:S(2)}, u32[]{:S(2)}) %collective-permute-start.16) | collective-permute-done | bytes 454688 | tf_op jit(solution)/shard_map/ppermute | solution.py:37
  191.4 5.7 %collective-permute-start.19 = (bf16[4,37,1536]{2,1,0:T(8,128)(2,1)S(1)}, bf16[4,37,1536]{2,1,0:T(8,128)(2,1)S(1)}, u32[]{:S(2)}, u32[]{:S(2)}) collective-permute-start(bf16[4,37,1536]{2,1,0:T(8,128)(2,1)S(1)} %pad_maximum_fusion.5), channel_id=1, source_target_pairs={{0,12},{4,16},{8,20},{12,24},{16,28},{20,0},{24,4},{28,8},{1,13},{... | collective-permute-start | bytes 1363976 | tf_op jit(solution)/shard_map/ppermute | solution.py:29
  197.5 2.9 collective-permute-start.21
  200.4 4.6 %collective-permute-done.17 = bf16[4,37,1536]{2,1,0:T(8,128)(2,1)S(1)} collective-permute-done((bf16[4,37,1536]{2,1,0:T(8,128)(2,1)S(1)}, bf16[4,37,1536]{2,1,0:T(8,128)(2,1)S(1)}, u32[]{:S(2)}, u32[]{:S(2)}) %collective-permute-start.17) | collective-permute-done | bytes 454688 | tf_op jit(solution)/shard_map/ppermute | solution.py:29
  206.5 17.9 %collective-permute-done.18 = bf16[4,37,1536]{2,1,0:T(8,128)(2,1)S(1)} collective-permute-done((bf16[4,37,1536]{2,1,0:T(8,128)(2,1)S(1)}, bf16[4,37,1536]{2,1,0:T(8,128)(2,1)S(1)}, u32[]{:S(2)}, u32[]{:S(2)}) %collective-permute-start.18) | collective-permute-done | bytes 454688 | tf_op jit(solution)/shard_map/ppermute | solution.py:29
  224.5 11.4 %collective-permute-done.20 = bf16[4,37,1536]{2,1,0:T(8,128)(2,1)S(1)} collective-permute-done((bf16[4,37,1536]{2,1,0:T(8,128)(2,1)S(1)}, bf16[4,37,1536]{2,1,0:T(8,128)(2,1)S(1)}, u32[]{:S(2)}, u32[]{:S(2)}) %collective-permute-start.20) | collective-permute-done | bytes 454688 | tf_op jit(solution)/shard_map/ppermute | solution.py:29
  236.0 7.3 %collective-permute-done.22 = bf16[4,37,1536]{2,1,0:T(8,128)(2,1)S(1)} collective-permute-done((bf16[4,37,1536]{2,1,0:T(8,128)(2,1)S(1)}, bf16[4,37,1536]{2,1,0:T(8,128)(2,1)S(1)}, u32[]{:S(2)}, u32[]{:S(2)}) %collective-permute-start.22) | collective-permute-done | bytes 454688 | tf_op jit(solution)/shard_map/ppermute | solution.py:29
  244.3 4.1 %fusion.8 = bf16[8,4,32,768]{3,2,1,0:T(8,128)(2,1)} fusion(bf16[1536,768]{1,0:T(8,128)(2,1)S(1)} %copy-done.48, bf16[8,4,37,1536]{3,2,1,0:T(8,128)(2,1)S(1)} %bitcast_dynamic-update-slice_fusion), kind=kOutput, calls=%fused_computation.43 | convolution fusion | flops 2422996992 | bytes 7077888 | tf_op jit(solution)/shard_map/arnd,df->arnf/dot_general | solution.py:239
  248.4 4.7 %convolution_convert_fusion.3 = bf16[8,4,5,1536]{3,0,2,1:T(8,128)(2,1)} fusion(bf16[768,1536]{1,0:T(8,128)(2,1)} %param.37, bf16[1536,768]{1,0:T(8,128)(2,1)} %param.35, bf16[8,4,5,1536]{3,2,1,0:T(8,128)(2,1)} %slice.297), kind=kOutput, calls=%fused_computation.47 | convolution fusion | flops 756326400 | bytes 5701632 | tf_op jit(solution)/shard_map/arnf,fd->arnd/dot_general | solution.py:247
  254.3 4.2 %convolution_convert_fusion = bf16[8,4,32,1536]{3,2,1,0:T(8,128)(2,1)S(1)} fusion(bf16[8,4,32,768]{3,2,1,0:T(8,128)(2,1)} %fusion.8, bf16[768,1536]{1,0:T(8,128)(2,1)S(1)} %copy-done), kind=kOutput, calls=%fused_computation.19 | convolution fusion | flops 2417491968 | bytes 7077888 | tf_op jit(solution)/shard_map/arnf,fd->arnd/dot_general | solution.py:246
  259.1 9.2 %collective-permute-start.25 = (bf16[4,37,1536]{2,1,0:T(8,128)(2,1)S(1)}, bf16[4,37,1536]{2,1,0:T(8,128)(2,1)S(1)}, u32[]{:S(2)}, u32[]{:S(2)}) collective-permute-start(bf16[4,37,1536]{2,1,0:T(8,128)(2,1)S(1)} %get-tuple-element.25), channel_id=1, source_target_pairs={{8,0},{12,4},{16,8},{20,12},{24,16},{28,20},{0,24},{4,28},{9,1},{1... | collective-permute-start | bytes 1363976 | tf_op jit(solution)/shard_map/ppermute | solution.py:37
  269.4 2.8 collective-permute-start.28
  273.6 35.2 %collective-permute-done.25 = bf16[4,37,1536]{2,1,0:T(8,128)(2,1)S(1)} collective-permute-done((bf16[4,37,1536]{2,1,0:T(8,128)(2,1)S(1)}, bf16[4,37,1536]{2,1,0:T(8,128)(2,1)S(1)}, u32[]{:S(2)}, u32[]{:S(2)}) %collective-permute-start.25) | collective-permute-done | bytes 454688 | tf_op jit(solution)/shard_map/ppermute | solution.py:37
  309.1 13.8 %collective-permute-done.30 = bf16[4,37,1536]{2,1,0:T(8,128)(2,1)S(1)} collective-permute-done((bf16[4,37,1536]{2,1,0:T(8,128)(2,1)S(1)}, bf16[4,37,1536]{2,1,0:T(8,128)(2,1)S(1)}, u32[]{:S(2)}, u32[]{:S(2)}) %collective-permute-start.30) | collective-permute-done | bytes 454688 | tf_op jit(solution)/shard_map/ppermute | solution.py:37
  331.9 3.1 collective-permute-done.32
  337.0 5.8 %collective-permute-start.34 = (bf16[4,10,1,16]{3,2,1,0:T(2,128)(2,1)S(1)}, bf16[4,10,1,16]{3,2,1,0:T(2,128)(2,1)S(1)}, u32[]{:S(2)}, u32[]{:S(2)}) collective-permute-start(bf16[4,10,1,16]{3,2,1,0:T(2,128)(2,1)S(1)} %get-tuple-element.56), channel_id=1, source_target_pairs={{1,0},{2,1},{3,2},{5,4},{6,5},{7,6},{9,8},{10,9},{11,10},{13,12},{... | collective-permute-start | bytes 3848 | tf_op jit(solution)/shard_map/ppermute | solution.py:20
  (268 shorter events, 81.4 us)
Async XLA Ops:
  4.0 26.6 %collective-permute-start = (bf16[4,37,1536]{2,1,0:T(8,128)(2,1)}, bf16[4,37,1536]{2,1,0:T(8,128)(2,1)}, u32[]{:S(2)}, u32[]{:S(2)}) collective-permute-start(bf16[4,37,1536]{2,1,0:T(8,128)(2,1)} %get-tuple-element.47), channel_id=1, source_target_pairs={{0,4},{4,8},{8,12},{12,16},{16,20},{20,24},{24,28},{28,0},{1,5},{5... | collective-permute-start | bytes 1363976 | tf_op jit(solution)/shard_map/ppermute | solution.py:29
  7.6 36.5 %collective-permute-start.1 = (bf16[4,37,1536]{2,1,0:T(8,128)(2,1)}, bf16[4,37,1536]{2,1,0:T(8,128)(2,1)}, u32[]{:S(2)}, u32[]{:S(2)}) collective-permute-start(bf16[4,37,1536]{2,1,0:T(8,128)(2,1)} %get-tuple-element.47), channel_id=1, source_target_pairs={{0,8},{4,12},{8,16},{12,20},{16,24},{20,28},{24,0},{28,4},{1,9},{5... | collective-permute-start | bytes 1363976 | tf_op jit(solution)/shard_map/ppermute | solution.py:29
  9.2 36.1 %collective-permute-start.2 = (bf16[4,37,1536]{2,1,0:T(8,128)(2,1)}, bf16[4,37,1536]{2,1,0:T(8,128)(2,1)}, u32[]{:S(2)}, u32[]{:S(2)}) collective-permute-start(bf16[4,37,1536]{2,1,0:T(8,128)(2,1)} %get-tuple-element.47), channel_id=1, source_target_pairs={{0,12},{4,16},{8,20},{12,24},{16,28},{20,0},{24,4},{28,8},{1,13},{... | collective-permute-start | bytes 1363976 | tf_op jit(solution)/shard_map/ppermute | solution.py:29
  11.9 43.9 %collective-permute-start.3 = (bf16[4,37,1536]{2,1,0:T(8,128)(2,1)}, bf16[4,37,1536]{2,1,0:T(8,128)(2,1)}, u32[]{:S(2)}, u32[]{:S(2)}) collective-permute-start(bf16[4,37,1536]{2,1,0:T(8,128)(2,1)} %get-tuple-element.47), channel_id=1, source_target_pairs={{0,16},{4,20},{8,24},{12,28},{16,0},{20,4},{24,8},{28,12},{1,17},{... | collective-permute-start | bytes 1363976 | tf_op jit(solution)/shard_map/ppermute | solution.py:29
  12.8 44.1 %collective-permute-start.4 = (bf16[4,37,1536]{2,1,0:T(8,128)(2,1)}, bf16[4,37,1536]{2,1,0:T(8,128)(2,1)}, u32[]{:S(2)}, u32[]{:S(2)}) collective-permute-start(bf16[4,37,1536]{2,1,0:T(8,128)(2,1)} %get-tuple-element.47), channel_id=1, source_target_pairs={{0,20},{4,24},{8,28},{12,0},{16,4},{20,8},{24,12},{28,16},{1,21},{... | collective-permute-start | bytes 1363976 | tf_op jit(solution)/shard_map/ppermute | solution.py:29
  30.7 27.3 %collective-permute-start.5 = (bf16[4,37,1536]{2,1,0:T(8,128)(2,1)}, bf16[4,37,1536]{2,1,0:T(8,128)(2,1)S(1)}, u32[]{:S(2)}, u32[]{:S(2)}) collective-permute-start(bf16[4,37,1536]{2,1,0:T(8,128)(2,1)} %get-tuple-element.47), channel_id=1, source_target_pairs={{0,24},{4,28},{8,0},{12,4},{16,8},{20,12},{24,16},{28,20},{1,25},{... | collective-permute-start | bytes 1363976 | tf_op jit(solution)/shard_map/ppermute | solution.py:29
  44.1 14.2 %collective-permute-start.6 = (bf16[4,37,1536]{2,1,0:T(8,128)(2,1)}, bf16[4,37,1536]{2,1,0:T(8,128)(2,1)S(1)}, u32[]{:S(2)}, u32[]{:S(2)}) collective-permute-start(bf16[4,37,1536]{2,1,0:T(8,128)(2,1)} %get-tuple-element.47), channel_id=1, source_target_pairs={{0,28},{4,0},{8,4},{12,8},{16,12},{20,16},{24,20},{28,24},{1,29},{... | collective-permute-start | bytes 1363976 | tf_op jit(solution)/shard_map/ppermute | solution.py:29
  70.3 20.5 %collective-permute-start.8 = (bf16[1184,384]{1,0:T(8,128)(2,1)}, bf16[1184,384]{1,0:T(8,128)(2,1)S(1)}, u32[]{:S(2)}, u32[]{:S(2)}) collective-permute-start(bf16[1184,384]{1,0:T(8,128)(2,1)} %reshape.322.refs_0_), channel_id=1, source_target_pairs={{0,2},{1,3},{2,0},{3,1},{4,6},{5,7},{6,4},{7,5},{8,10},{9,11},{10,... | collective-permute-start | bytes 2727944 | tf_op jit(solution)/shard_map/ppermute | solution.py:200
  75.1 26.8 %collective-permute-start.7 = (bf16[1184,384]{1,0:T(8,128)(2,1)S(1)}, bf16[1184,384]{1,0:T(8,128)(2,1)S(1)}, u32[]{:S(2)}, u32[]{:S(2)}) collective-permute-start(bf16[1184,384]{1,0:T(8,128)(2,1)S(1)} %copy-done.5), channel_id=1, source_target_pairs={{0,1},{1,0},{2,3},{3,2},{4,5},{5,4},{6,7},{7,6},{8,9},{9,8},{10,11... | collective-permute-start | bytes 2727944 | tf_op jit(solution)/shard_map/ppermute | solution.py:203
  90.9 12.0 %collective-permute-start.9 = (bf16[1184,384]{1,0:T(8,128)(2,1)S(1)}, bf16[1184,384]{1,0:T(8,128)(2,1)}, u32[]{:S(2)}, u32[]{:S(2)}) collective-permute-start(bf16[1184,384]{1,0:T(8,128)(2,1)S(1)} %collective-permute-done.8.refs_2_), channel_id=1, source_target_pairs={{0,1},{1,0},{2,3},{3,2},{4,5},{5,4},{6,7},{7,6},{8,9},{9,8},{10,11... | collective-permute-start | bytes 2727944 | tf_op jit(solution)/shard_map/ppermute | solution.py:205
  121.8 17.3 %collective-permute-start.10 = (bf16[4,37,1536]{2,1,0:T(8,128)(2,1)S(1)}, bf16[4,37,1536]{2,1,0:T(8,128)(2,1)S(1)}, u32[]{:S(2)}, u32[]{:S(2)}) collective-permute-start(bf16[4,37,1536]{2,1,0:T(8,128)(2,1)S(1)} %get-tuple-element.31), channel_id=1, source_target_pairs={{4,0},{8,4},{12,8},{16,12},{20,16},{24,20},{28,24},{0,28},{5,1},{9... | collective-permute-start | bytes 1363976 | tf_op jit(solution)/shard_map/ppermute | solution.py:37
  128.8 45.7 %collective-permute-start.11 = (bf16[4,37,1536]{2,1,0:T(8,128)(2,1)S(1)}, bf16[4,37,1536]{2,1,0:T(8,128)(2,1)S(1)}, u32[]{:S(2)}, u32[]{:S(2)}) collective-permute-start(bf16[4,37,1536]{2,1,0:T(8,128)(2,1)S(1)} %get-tuple-element.32), channel_id=1, source_target_pairs={{8,0},{12,4},{16,8},{20,12},{24,16},{28,20},{0,24},{4,28},{9,1},{1... | collective-permute-start | bytes 1363976 | tf_op jit(solution)/shard_map/ppermute | solution.py:37
  133.1 41.6 %collective-permute-start.12 = (bf16[4,37,1536]{2,1,0:T(8,128)(2,1)S(1)}, bf16[4,37,1536]{2,1,0:T(8,128)(2,1)S(1)}, u32[]{:S(2)}, u32[]{:S(2)}) collective-permute-start(bf16[4,37,1536]{2,1,0:T(8,128)(2,1)S(1)} %get-tuple-element.33), channel_id=1, source_target_pairs={{12,0},{16,4},{20,8},{24,12},{28,16},{0,20},{4,24},{8,28},{13,1},{... | collective-permute-start | bytes 1363976 | tf_op jit(solution)/shard_map/ppermute | solution.py:37
  136.4 38.3 %collective-permute-start.13 = (bf16[4,37,1536]{2,1,0:T(8,128)(2,1)S(1)}, bf16[4,37,1536]{2,1,0:T(8,128)(2,1)S(1)}, u32[]{:S(2)}, u32[]{:S(2)}) collective-permute-start(bf16[4,37,1536]{2,1,0:T(8,128)(2,1)S(1)} %get-tuple-element.34), channel_id=1, source_target_pairs={{16,0},{20,4},{24,8},{28,12},{0,16},{4,20},{8,24},{12,28},{17,1},{... | collective-permute-start | bytes 1363976 | tf_op jit(solution)/shard_map/ppermute | solution.py:37
  136.8 37.9 %collective-permute-start.14 = (bf16[4,37,1536]{2,1,0:T(8,128)(2,1)S(1)}, bf16[4,37,1536]{2,1,0:T(8,128)(2,1)S(1)}, u32[]{:S(2)}, u32[]{:S(2)}) collective-permute-start(bf16[4,37,1536]{2,1,0:T(8,128)(2,1)S(1)} %get-tuple-element.35), channel_id=1, source_target_pairs={{20,0},{24,4},{28,8},{0,12},{4,16},{8,20},{12,24},{16,28},{21,1},{... | collective-permute-start | bytes 1363976 | tf_op jit(solution)/shard_map/ppermute | solution.py:37
  139.1 39.2 %collective-permute-start.15 = (bf16[4,37,1536]{2,1,0:T(8,128)(2,1)S(1)}, bf16[4,37,1536]{2,1,0:T(8,128)(2,1)S(1)}, u32[]{:S(2)}, u32[]{:S(2)}) collective-permute-start(bf16[4,37,1536]{2,1,0:T(8,128)(2,1)S(1)} %get-tuple-element.37), channel_id=1, source_target_pairs={{24,0},{28,4},{0,8},{4,12},{8,16},{12,20},{16,24},{20,28},{25,1},{... | collective-permute-start | bytes 1363976 | tf_op jit(solution)/shard_map/ppermute | solution.py:37
  174.5 14.7 %collective-permute-start.16 = (bf16[4,37,1536]{2,1,0:T(8,128)(2,1)S(1)}, bf16[4,37,1536]{2,1,0:T(8,128)(2,1)S(1)}, u32[]{:S(2)}, u32[]{:S(2)}) collective-permute-start(bf16[4,37,1536]{2,1,0:T(8,128)(2,1)S(1)} %get-tuple-element.36), channel_id=1, source_target_pairs={{28,0},{0,4},{4,8},{8,12},{12,16},{16,20},{20,24},{24,28},{29,1},{... | collective-permute-start | bytes 1363976 | tf_op jit(solution)/shard_map/ppermute | solution.py:37
  191.2 13.9 %collective-permute-start.17 = (bf16[4,37,1536]{2,1,0:T(8,128)(2,1)S(1)}, bf16[4,37,1536]{2,1,0:T(8,128)(2,1)S(1)}, u32[]{:S(2)}, u32[]{:S(2)}) collective-permute-start(bf16[4,37,1536]{2,1,0:T(8,128)(2,1)S(1)} %pad_maximum_fusion.5), channel_id=1, source_target_pairs={{0,4},{4,8},{8,12},{12,16},{16,20},{20,24},{24,28},{28,0},{1,5},{5... | collective-permute-start | bytes 1363976 | tf_op jit(solution)/shard_map/ppermute | solution.py:29
  191.3 33.1 %collective-permute-start.18 = (bf16[4,37,1536]{2,1,0:T(8,128)(2,1)S(1)}, bf16[4,37,1536]{2,1,0:T(8,128)(2,1)S(1)}, u32[]{:S(2)}, u32[]{:S(2)}) collective-permute-start(bf16[4,37,1536]{2,1,0:T(8,128)(2,1)S(1)} %pad_maximum_fusion.5), channel_id=1, source_target_pairs={{0,8},{4,12},{8,16},{12,20},{16,24},{20,28},{24,0},{28,4},{1,9},{5... | collective-permute-start | bytes 1363976 | tf_op jit(solution)/shard_map/ppermute | solution.py:29
  191.4 33.1 %collective-permute-start.19 = (bf16[4,37,1536]{2,1,0:T(8,128)(2,1)S(1)}, bf16[4,37,1536]{2,1,0:T(8,128)(2,1)S(1)}, u32[]{:S(2)}, u32[]{:S(2)}) collective-permute-start(bf16[4,37,1536]{2,1,0:T(8,128)(2,1)S(1)} %pad_maximum_fusion.5), channel_id=1, source_target_pairs={{0,12},{4,16},{8,20},{12,24},{16,28},{20,0},{24,4},{28,8},{1,13},{... | collective-permute-start | bytes 1363976 | tf_op jit(solution)/shard_map/ppermute | solution.py:29
  197.0 38.9 %collective-permute-start.20 = (bf16[4,37,1536]{2,1,0:T(8,128)(2,1)S(1)}, bf16[4,37,1536]{2,1,0:T(8,128)(2,1)S(1)}, u32[]{:S(2)}, u32[]{:S(2)}) collective-permute-start(bf16[4,37,1536]{2,1,0:T(8,128)(2,1)S(1)} %pad_maximum_fusion.5), channel_id=1, source_target_pairs={{0,16},{4,20},{8,24},{12,28},{16,0},{20,4},{24,8},{28,12},{1,17},{... | collective-permute-start | bytes 1363976 | tf_op jit(solution)/shard_map/ppermute | solution.py:29
  197.5 38.4 %collective-permute-start.21 = (bf16[4,37,1536]{2,1,0:T(8,128)(2,1)S(1)}, bf16[4,37,1536]{2,1,0:T(8,128)(2,1)S(1)}, u32[]{:S(2)}, u32[]{:S(2)}) collective-permute-start(bf16[4,37,1536]{2,1,0:T(8,128)(2,1)S(1)} %pad_maximum_fusion.5), channel_id=1, source_target_pairs={{0,20},{4,24},{8,28},{12,0},{16,4},{20,8},{24,12},{28,16},{1,21},{... | collective-permute-start | bytes 1363976 | tf_op jit(solution)/shard_map/ppermute | solution.py:29
  205.1 38.2 %collective-permute-start.22 = (bf16[4,37,1536]{2,1,0:T(8,128)(2,1)S(1)}, bf16[4,37,1536]{2,1,0:T(8,128)(2,1)S(1)}, u32[]{:S(2)}, u32[]{:S(2)}) collective-permute-start(bf16[4,37,1536]{2,1,0:T(8,128)(2,1)S(1)} %pad_maximum_fusion.5), channel_id=1, source_target_pairs={{0,24},{4,28},{8,0},{12,4},{16,8},{20,12},{24,16},{28,20},{1,25},{... | collective-permute-start | bytes 1363976 | tf_op jit(solution)/shard_map/ppermute | solution.py:29
  224.4 18.9 %collective-permute-start.23 = (bf16[4,37,1536]{2,1,0:T(8,128)(2,1)S(1)}, bf16[4,37,1536]{2,1,0:T(8,128)(2,1)S(1)}, u32[]{:S(2)}, u32[]{:S(2)}) collective-permute-start(bf16[4,37,1536]{2,1,0:T(8,128)(2,1)S(1)} %pad_maximum_fusion.5), channel_id=1, source_target_pairs={{0,28},{4,0},{8,4},{12,8},{16,12},{20,16},{24,20},{28,24},{1,29},{... | collective-permute-start | bytes 1363976 | tf_op jit(solution)/shard_map/ppermute | solution.py:29
  259.0 13.9 %collective-permute-start.24 = (bf16[4,37,1536]{2,1,0:T(8,128)(2,1)S(1)}, bf16[4,37,1536]{2,1,0:T(8,128)(2,1)S(1)}, u32[]{:S(2)}, u32[]{:S(2)}) collective-permute-start(bf16[4,37,1536]{2,1,0:T(8,128)(2,1)S(1)} %get-tuple-element.24), channel_id=1, source_target_pairs={{4,0},{8,4},{12,8},{16,12},{20,16},{24,20},{28,24},{0,28},{5,1},{9... | collective-permute-start | bytes 1363976 | tf_op jit(solution)/shard_map/ppermute | solution.py:37
  259.1 49.8 %collective-permute-start.25 = (bf16[4,37,1536]{2,1,0:T(8,128)(2,1)S(1)}, bf16[4,37,1536]{2,1,0:T(8,128)(2,1)S(1)}, u32[]{:S(2)}, u32[]{:S(2)}) collective-permute-start(bf16[4,37,1536]{2,1,0:T(8,128)(2,1)S(1)} %get-tuple-element.25), channel_id=1, source_target_pairs={{8,0},{12,4},{16,8},{20,12},{24,16},{28,20},{0,24},{4,28},{9,1},{1... | collective-permute-start | bytes 1363976 | tf_op jit(solution)/shard_map/ppermute | solution.py:37
  268.3 40.8 %collective-permute-start.26 = (bf16[4,37,1536]{2,1,0:T(8,128)(2,1)S(1)}, bf16[4,37,1536]{2,1,0:T(8,128)(2,1)S(1)}, u32[]{:S(2)}, u32[]{:S(2)}) collective-permute-start(bf16[4,37,1536]{2,1,0:T(8,128)(2,1)S(1)} %get-tuple-element.26), channel_id=1, source_target_pairs={{12,0},{16,4},{20,8},{24,12},{28,16},{0,20},{4,24},{8,28},{13,1},{... | collective-permute-start | bytes 1363976 | tf_op jit(solution)/shard_map/ppermute | solution.py:37
  268.4 40.7 %collective-permute-start.27 = (bf16[4,37,1536]{2,1,0:T(8,128)(2,1)S(1)}, bf16[4,37,1536]{2,1,0:T(8,128)(2,1)S(1)}, u32[]{:S(2)}, u32[]{:S(2)}) collective-permute-start(bf16[4,37,1536]{2,1,0:T(8,128)(2,1)S(1)} %get-tuple-element.27), channel_id=1, source_target_pairs={{16,0},{20,4},{24,8},{28,12},{0,16},{4,20},{8,24},{12,28},{17,1},{... | collective-permute-start | bytes 1363976 | tf_op jit(solution)/shard_map/ppermute | solution.py:37
  269.4 39.7 %collective-permute-start.28 = (bf16[4,37,1536]{2,1,0:T(8,128)(2,1)S(1)}, bf16[4,37,1536]{2,1,0:T(8,128)(2,1)S(1)}, u32[]{:S(2)}, u32[]{:S(2)}) collective-permute-start(bf16[4,37,1536]{2,1,0:T(8,128)(2,1)S(1)} %get-tuple-element.28), channel_id=1, source_target_pairs={{20,0},{24,4},{28,8},{0,12},{4,16},{8,20},{12,24},{16,28},{21,1},{... | collective-permute-start | bytes 1363976 | tf_op jit(solution)/shard_map/ppermute | solution.py:37
  272.9 36.2 %collective-permute-start.29 = (bf16[4,37,1536]{2,1,0:T(8,128)(2,1)S(1)}, bf16[4,37,1536]{2,1,0:T(8,128)(2,1)S(1)}, u32[]{:S(2)}, u32[]{:S(2)}) collective-permute-start(bf16[4,37,1536]{2,1,0:T(8,128)(2,1)S(1)} %get-tuple-element.30), channel_id=1, source_target_pairs={{24,0},{28,4},{0,8},{4,12},{8,16},{12,20},{16,24},{20,28},{25,1},{... | collective-permute-start | bytes 1363976 | tf_op jit(solution)/shard_map/ppermute | solution.py:37
  308.8 14.0 %collective-permute-start.30 = (bf16[4,37,1536]{2,1,0:T(8,128)(2,1)S(1)}, bf16[4,37,1536]{2,1,0:T(8,128)(2,1)S(1)}, u32[]{:S(2)}, u32[]{:S(2)}) collective-permute-start(bf16[4,37,1536]{2,1,0:T(8,128)(2,1)S(1)} %get-tuple-element.29), channel_id=1, source_target_pairs={{28,0},{0,4},{4,8},{8,12},{12,16},{16,20},{20,24},{24,28},{29,1},{... | collective-permute-start | bytes 1363976 | tf_op jit(solution)/shard_map/ppermute | solution.py:37
  335.0 7.8 %collective-permute-start.33 = (bf16[4,10,1,16]{3,2,1,0:T(2,128)(2,1)S(1)}, bf16[4,10,1,16]{3,2,1,0:T(2,128)(2,1)S(1)}, u32[]{:S(2)}, u32[]{:S(2)}) collective-permute-start(bf16[4,10,1,16]{3,2,1,0:T(2,128)(2,1)S(1)} %get-tuple-element.57), channel_id=1, source_target_pairs={{0,1},{1,2},{2,3},{4,5},{5,6},{6,7},{8,9},{9,10},{10,11},{12,13},{... | collective-permute-start | bytes 3848 | tf_op jit(solution)/shard_map/ppermute | solution.py:17
  (56 other events, 818.2 us)

commit v6 on v3

--- a/solution.py
+++ b/solution.py
@@ -22,11 +22,19 @@
     return block
 
 
+def moved(block, axis, shift):
+    count = lax.axis_size(axis)
+    if count == 8 and shift == count // 2:
+        step = [(i, (i + count - 2) % count) for i in range(count)]
+        return lax.ppermute(lax.ppermute(block, axis, step), axis, step)
+    return lax.ppermute(block, axis, [(i, (i + shift) % count) for i in range(count)])
+
+
 def gather_slots(block, axis):
     count = lax.axis_size(axis)
     parts = [block]
     for shift in range(1, count):
-        parts.append(lax.ppermute(block, axis, [(i, (i + shift) % count) for i in range(count)]))
+        parts.append(moved(block, axis, shift))
     return jnp.stack(parts)
 
 
@@ -34,9 +42,7 @@
     count = lax.axis_size(axis)
     total = partial[0].astype(jnp.float32)
     for shift in range(1, count):
-        total = total + lax.ppermute(
-            partial[shift], axis, [((i + shift) % count, i) for i in range(count)]
-        ).astype(jnp.float32)
+        total = total + moved(partial[shift], axis, count - shift).astype(jnp.float32)
     return total
 
 

time: 351 us -> 338 us (0.963)
  waiting for transfers between devices: 171 us -> 84.4 us
  starting transfers between devices: 75.3 us -> 149 us
    ppermute x28 -> x30, waiting for transfers between devices: 158 us -> 74 us  [the longest x8 45.7 us: moved(): return lax.ppermute(lax.ppermute(block, axis, step), axis, step)]
    ppermute x28 -> x30, starting transfers between devices: 60.1 us -> 122 us  [the longest x22 100 us: moved(): lax.ppermute(block, axis, [(i, (i + shift) % count) for i in range(count)])]
    ppermute x2, starting transfers between devices: 3.2 us -> 14.5 us  [extended(): lax.ppermute(lax.slice_in_dim(block, block.shape[dim] - width, None, axis...]
    ppermute x1, waiting for transfers between devices: 10.6 us -> 4.84 us  [body(): far = lax.ppermute(own_pairs, 'blk', flip_chip)]
    ppermute x2, starting transfers between devices: 7.59 us -> 3.21 us  [extended(): lax.ppermute(lax.slice_in_dim(block, 0, width, axis=dim), axis, backward)]
  transfers between devices with their start and end apart: 35 -> 37, of which waited for: 16 -> 18; matrix products, arithmetic and copies ran while one was open for 11% -> 11% of each run, Pallas kernels for 0% -> 0%
where the time goes in v6:
time: 338 us; the launch traced here: 333 us
  starting transfers between devices  149 us (44%)
  waiting for transfers between devices  84.4 us (25%)
  matrix products  36.5 us (11%)
  local copies, waits for them, and re-layouts  25 us (7%)
  other arithmetic  21.6 us (6%)
  Pallas kernels  14.2 us (4%)
    ppermute x22, starting transfers between devices, moved(): lax.ppermute(block, axis, [(i, (i + shift) % count) for i in range(count)])  100 us
    ppermute x8, waiting for transfers between devices, moved(): return lax.ppermute(lax.ppermute(block, axis, step), axis, step)  45.7 us
    ppermute x22, waiting for transfers between devices, moved(): lax.ppermute(block, axis, [(i, (i + shift) % count) for i in range(count)])  28.3 us
    ppermute x8, starting transfers between devices, moved(): return lax.ppermute(lax.ppermute(block, axis, step), axis, step)  21.3 us
    ppermute x2, starting transfers between devices, extended(): lax.ppermute(lax.slice_in_dim(block, block.shape[dim] - width, None, axis...  14.5 us
    pallas_call x1, Pallas kernels, attend(): pl.pallas_call(attention_kernel, grid=(requests, heads), in_specs=[pl.Blo...  14.2 us
    unnamed x131, local copies, waits for them, and re-layouts  11.1 us
    dot_general x4, matrix products, normalized(): jnp.dot(values * values, spread, precision=lax.Precision.HIGHEST)  8.49 us
  transfers between devices with their start and end apart: 37, of which 18 were waited for; matrix products, arithmetic and copies ran while one was open for 11% of the time, Pallas kernels for 0%

profile of v6, /device:TPU:1, one launch (start us, length us, event | category | flops | bytes accessed | tf_op | source)
XLA Modules:
  0.0 333.2 jit_solution(6169023273964835647)
XLA Ops:
  4.0 3.6 %collective-permute-start = (bf16[4,37,1536]{2,1,0:T(8,128)(2,1)}, bf16[4,37,1536]{2,1,0:T(8,128)(2,1)}, u32[]{:S(2)}, u32[]{:S(2)}) collective-permute-start(bf16[4,37,1536]{2,1,0:T(8,128)(2,1)} %get-tuple-element.47), channel_id=1, source_target_pairs={{0,4},{4,8},{8,12},{12,16},{16,20},{20,24},{24,28},{28,0},{1,5},{5... | collective-permute-start | bytes 1363976 | tf_op jit(solution)/shard_map/ppermute | solution.py:30
  29.2 14.7 %collective-permute-done.3 = bf16[4,37,1536]{2,1,0:T(8,128)(2,1)} collective-permute-done((bf16[4,37,1536]{2,1,0:T(8,128)(2,1)}, bf16[4,37,1536]{2,1,0:T(8,128)(2,1)}, u32[]{:S(2)}, u32[]{:S(2)}) %collective-permute-start.3) | collective-permute-done | bytes 454688 | tf_op jit(solution)/shard_map/ppermute | solution.py:29
  50.0 4.8 %collective-permute-done.4 = bf16[4,37,1536]{2,1,0:T(8,128)(2,1)S(1)} collective-permute-done((bf16[4,37,1536]{2,1,0:T(8,128)(2,1)}, bf16[4,37,1536]{2,1,0:T(8,128)(2,1)S(1)}, u32[]{:S(2)}, u32[]{:S(2)}) %collective-permute-start.4) | collective-permute-done | bytes 454688 | tf_op jit(solution)/shard_map/ppermute | solution.py:29
  74.7 4.2 %collective-permute-start.7 = (bf16[1184,384]{1,0:T(8,128)(2,1)S(1)}, bf16[1184,384]{1,0:T(8,128)(2,1)S(1)}, u32[]{:S(2)}, u32[]{:S(2)}) collective-permute-start(bf16[1184,384]{1,0:T(8,128)(2,1)S(1)} %copy-done.5), channel_id=1, source_target_pairs={{0,1},{1,0},{2,3},{3,2},{4,5},{5,4},{6,7},{7,6},{8,9},{9,8},{10,11... | collective-permute-start | bytes 2727944 | tf_op jit(solution)/shard_map/ppermute | solution.py:208
  82.3 4.8 %collective-permute-done.8.refs_2_ = bf16[1184,384]{1,0:T(8,128)(2,1)S(1)} collective-permute-done((bf16[1184,384]{1,0:T(8,128)(2,1)}, bf16[1184,384]{1,0:T(8,128)(2,1)S(1)}, u32[]{:S(2)}, u32[]{:S(2)}) %collective-permute-start.8) | collective-permute-done | bytes 909344 | tf_op jit(solution)/shard_map/ppermute | solution.py:205
  87.2 4.7 %collective-permute-start.9 = (bf16[1184,384]{1,0:T(8,128)(2,1)S(1)}, bf16[1184,384]{1,0:T(8,128)(2,1)}, u32[]{:S(2)}, u32[]{:S(2)}) collective-permute-start(bf16[1184,384]{1,0:T(8,128)(2,1)S(1)} %collective-permute-done.8.refs_2_), channel_id=1, source_target_pairs={{0,1},{1,0},{2,3},{3,2},{4,5},{5,4},{6,7},{7,6},{8,9},{9,8},{10,11... | collective-permute-start | bytes 2727944 | tf_op jit(solution)/shard_map/ppermute | solution.py:210
  91.8 4.0 %fusion.216 = f32[8,4,32,384]{3,2,1,0:T(8,128)S(1)} fusion(bf16[1536,384,1,1]{0,1,3,2:T(8,128)(2,1)S(1)} %bitcast.305, f32[8,4,37,1536]{3,2,1,0:T(8,128)} %copy-done.1, f32[4,1536]{1,0:T(4,128)S(1)} %copy-done.30, f32[4,1536]{1,0:T(4,128)S(1)} %bitcast.316, f32[8,4,32]{2,1,0:T(4,128)S(1)} %copy-done.37, f32[8,4,32]{2,1,0:T(4,128)S(1)} %broadcast_multiply_fusion.1), kind=kOutput, calls=%fused_computation.357 | convolution fusion | flops 1215823872 | bytes 9101312 | tf_op jit(solution)/shard_map/arnd,de->arne/dot_general | solution.py:135
  101.6 14.2 %shard_map.219 = bf16[4,296,384]{2,1,0:T(8,128)(2,1)} custom-call(bf16[4,296,384]{2,1,0:T(8,128)(2,1)} %copy.107.query_ref, bf16[1184,384]{1,0:T(8,128)(2,1)} %reshape.319.refs_0_, bf16[1184,384]{1,0:T(8,128)(2,1)} %copy-done.10, bf16[1184,384]{1,0:T(8,128)(2,1)} %copy-done.9, bf16[1184,384]{1,0:T(8,128)(2,1)} %collective-permute-done.9.refs_3_, ...), custom_call_target="tpu_custom_call" | custom-call | tf_op jit(solution)/shard_map/pallas_call | solution.py:78
  120.5 3.4 %collective-permute-start.13 = (bf16[4,37,1536]{2,1,0:T(8,128)(2,1)S(1)}, bf16[4,37,1536]{2,1,0:T(8,128)(2,1)S(1)}, u32[]{:S(2)}, u32[]{:S(2)}) collective-permute-start(bf16[4,37,1536]{2,1,0:T(8,128)(2,1)S(1)} %get-tuple-element.34), channel_id=1, source_target_pairs={{0,24},{4,28},{8,0},{12,4},{16,8},{20,12},{24,16},{28,20},{1,25},{... | collective-permute-start | bytes 1363976 | tf_op jit(solution)/shard_map/ppermute | solution.py:29
  123.9 10.2 %collective-permute-start.10 = (bf16[4,37,1536]{2,1,0:T(8,128)(2,1)S(1)}, bf16[4,37,1536]{2,1,0:T(8,128)(2,1)S(1)}, u32[]{:S(2)}, u32[]{:S(2)}) collective-permute-start(bf16[4,37,1536]{2,1,0:T(8,128)(2,1)S(1)} %get-tuple-element.31), channel_id=1, source_target_pairs={{0,28},{4,0},{8,4},{12,8},{16,12},{20,16},{24,20},{28,24},{1,29},{... | collective-permute-start | bytes 1363976 | tf_op jit(solution)/shard_map/ppermute | solution.py:30
  134.5 3.8 %collective-permute-start.15 = (bf16[4,37,1536]{2,1,0:T(8,128)(2,1)S(1)}, bf16[4,37,1536]{2,1,0:T(8,128)(2,1)S(1)}, u32[]{:S(2)}, u32[]{:S(2)}) collective-permute-start(bf16[4,37,1536]{2,1,0:T(8,128)(2,1)S(1)} %get-tuple-element.35), channel_id=1, source_target_pairs={{0,12},{4,16},{8,20},{12,24},{16,28},{20,0},{24,4},{28,8},{1,13},{... | collective-permute-start | bytes 1363976 | tf_op jit(solution)/shard_map/ppermute | solution.py:30
  139.8 5.5 %collective-permute-done.10 = bf16[4,37,1536]{2,1,0:T(8,128)(2,1)S(1)} collective-permute-done((bf16[4,37,1536]{2,1,0:T(8,128)(2,1)S(1)}, bf16[4,37,1536]{2,1,0:T(8,128)(2,1)S(1)}, u32[]{:S(2)}, u32[]{:S(2)}) %collective-permute-start.10) | collective-permute-done | bytes 454688 | tf_op jit(solution)/shard_map/ppermute | solution.py:30
  145.3 20.3 %collective-permute-start.17 = (bf16[4,37,1536]{2,1,0:T(8,128)(2,1)S(1)}, bf16[4,37,1536]{2,1,0:T(8,128)(2,1)S(1)}, u32[]{:S(2)}, u32[]{:S(2)}) collective-permute-start(bf16[4,37,1536]{2,1,0:T(8,128)(2,1)S(1)} %get-tuple-element.36), channel_id=1, source_target_pairs={{0,4},{4,8},{8,12},{12,16},{16,20},{20,24},{24,28},{28,0},{1,5},{5... | collective-permute-start | bytes 1363976 | tf_op jit(solution)/shard_map/ppermute | solution.py:30
  169.2 9.2 %collective-permute-done.17 = bf16[4,37,1536]{2,1,0:T(8,128)(2,1)S(1)} collective-permute-done((bf16[4,37,1536]{2,1,0:T(8,128)(2,1)S(1)}, bf16[4,37,1536]{2,1,0:T(8,128)(2,1)S(1)}, u32[]{:S(2)}, u32[]{:S(2)}) %collective-permute-start.17) | collective-permute-done | bytes 454688 | tf_op jit(solution)/shard_map/ppermute | solution.py:30
  180.6 10.4 %collective-permute-start.18 = (bf16[4,37,1536]{2,1,0:T(8,128)(2,1)S(1)}, bf16[4,37,1536]{2,1,0:T(8,128)(2,1)S(1)}, u32[]{:S(2)}, u32[]{:S(2)}) collective-permute-start(bf16[4,37,1536]{2,1,0:T(8,128)(2,1)S(1)} %pad_maximum_fusion.5), channel_id=1, source_target_pairs={{0,4},{4,8},{8,12},{12,16},{16,20},{20,24},{24,28},{28,0},{1,5},{5... | collective-permute-start | bytes 1363976 | tf_op jit(solution)/shard_map/ppermute | solution.py:30
  191.0 3.4 %collective-permute-start.21 = (bf16[4,37,1536]{2,1,0:T(8,128)(2,1)S(1)}, bf16[4,37,1536]{2,1,0:T(8,128)(2,1)S(1)}, u32[]{:S(2)}, u32[]{:S(2)}) collective-permute-start(bf16[4,37,1536]{2,1,0:T(8,128)(2,1)S(1)} %pad_maximum_fusion.5), channel_id=1, source_target_pairs={{0,24},{4,28},{8,0},{12,4},{16,8},{20,12},{24,16},{28,20},{1,25},{... | collective-permute-start | bytes 1363976 | tf_op jit(solution)/shard_map/ppermute | solution.py:29
  194.4 5.4 %collective-permute-start.23 = (bf16[4,37,1536]{2,1,0:T(8,128)(2,1)S(1)}, bf16[4,37,1536]{2,1,0:T(8,128)(2,1)S(1)}, u32[]{:S(2)}, u32[]{:S(2)}) collective-permute-start(bf16[4,37,1536]{2,1,0:T(8,128)(2,1)S(1)} %pad_maximum_fusion.5), channel_id=1, source_target_pairs={{0,20},{4,24},{8,28},{12,0},{16,4},{20,8},{24,12},{28,16},{1,21},{... | collective-permute-start | bytes 1363976 | tf_op jit(solution)/shard_map/ppermute | solution.py:30
  199.8 4.0 %collective-permute-done.18 = bf16[4,37,1536]{2,1,0:T(8,128)(2,1)S(1)} collective-permute-done((bf16[4,37,1536]{2,1,0:T(8,128)(2,1)S(1)}, bf16[4,37,1536]{2,1,0:T(8,128)(2,1)S(1)}, u32[]{:S(2)}, u32[]{:S(2)}) %collective-permute-start.18) | collective-permute-done | bytes 454688 | tf_op jit(solution)/shard_map/ppermute | solution.py:30
  206.3 15.3 %collective-permute-done.21 = bf16[4,37,1536]{2,1,0:T(8,128)(2,1)S(1)} collective-permute-done((bf16[4,37,1536]{2,1,0:T(8,128)(2,1)S(1)}, bf16[4,37,1536]{2,1,0:T(8,128)(2,1)S(1)}, u32[]{:S(2)}, u32[]{:S(2)}) %collective-permute-start.21) | collective-permute-done | bytes 454688 | tf_op jit(solution)/shard_map/ppermute | solution.py:29
  221.6 3.9 %collective-permute-start.22 = (bf16[4,37,1536]{2,1,0:T(8,128)(2,1)S(1)}, bf16[4,37,1536]{2,1,0:T(8,128)(2,1)S(1)}, u32[]{:S(2)}, u32[]{:S(2)}) collective-permute-start(bf16[4,37,1536]{2,1,0:T(8,128)(2,1)S(1)} %collective-permute-done.21), channel_id=1, source_target_pairs={{0,24},{4,28},{8,0},{12,4},{16,8},{20,12},{24,16},{28,20},{1,25},{... | collective-permute-start | bytes 1363976 | tf_op jit(solution)/shard_map/ppermute | solution.py:29
  227.0 4.8 %collective-permute-done.22 = bf16[4,37,1536]{2,1,0:T(8,128)(2,1)S(1)} collective-permute-done((bf16[4,37,1536]{2,1,0:T(8,128)(2,1)S(1)}, bf16[4,37,1536]{2,1,0:T(8,128)(2,1)S(1)}, u32[]{:S(2)}, u32[]{:S(2)}) %collective-permute-start.22) | collective-permute-done | bytes 454688 | tf_op jit(solution)/shard_map/ppermute | solution.py:29
  233.0 4.1 %fusion.8 = bf16[8,4,32,768]{3,2,1,0:T(8,128)(2,1)} fusion(bf16[1536,768]{1,0:T(8,128)(2,1)S(1)} %copy-done.49, bf16[8,4,37,1536]{3,2,1,0:T(8,128)(2,1)S(1)} %bitcast_dynamic-update-slice_fusion), kind=kOutput, calls=%fused_computation.43 | convolution fusion | flops 2422996992 | bytes 7077888 | tf_op jit(solution)/shard_map/arnd,df->arnf/dot_general | solution.py:244
  237.1 4.7 %convolution_convert_fusion.3 = bf16[8,4,5,1536]{3,0,2,1:T(8,128)(2,1)} fusion(bf16[768,1536]{1,0:T(8,128)(2,1)} %param.37, bf16[1536,768]{1,0:T(8,128)(2,1)} %param.35, bf16[8,4,5,1536]{3,2,1,0:T(8,128)(2,1)} %slice.333), kind=kOutput, calls=%fused_computation.47 | convolution fusion | flops 756326400 | bytes 5701632 | tf_op jit(solution)/shard_map/arnf,fd->arnd/dot_general | solution.py:252
  243.1 4.2 %convolution_convert_fusion = bf16[8,4,32,1536]{3,2,1,0:T(8,128)(2,1)S(1)} fusion(bf16[8,4,32,768]{3,2,1,0:T(8,128)(2,1)} %fusion.8, bf16[768,1536]{1,0:T(8,128)(2,1)S(1)} %copy-done), kind=kOutput, calls=%fused_computation.19 | convolution fusion | flops 2417491968 | bytes 7077888 | tf_op jit(solution)/shard_map/arnf,fd->arnd/dot_general | solution.py:251
  247.8 3.5 %collective-permute-start.28 = (bf16[4,37,1536]{2,1,0:T(8,128)(2,1)S(1)}, bf16[4,37,1536]{2,1,0:T(8,128)(2,1)S(1)}, u32[]{:S(2)}, u32[]{:S(2)}) collective-permute-start(bf16[4,37,1536]{2,1,0:T(8,128)(2,1)S(1)} %get-tuple-element.27), channel_id=1, source_target_pairs={{0,24},{4,28},{8,0},{12,4},{16,8},{20,12},{24,16},{28,20},{1,25},{... | collective-permute-start | bytes 1363976 | tf_op jit(solution)/shard_map/ppermute | solution.py:29
  251.3 3.6 %collective-permute-start.25 = (bf16[4,37,1536]{2,1,0:T(8,128)(2,1)S(1)}, bf16[4,37,1536]{2,1,0:T(8,128)(2,1)S(1)}, u32[]{:S(2)}, u32[]{:S(2)}) collective-permute-start(bf16[4,37,1536]{2,1,0:T(8,128)(2,1)S(1)} %get-tuple-element.24), channel_id=1, source_target_pairs={{0,28},{4,0},{8,4},{12,8},{16,12},{20,16},{24,20},{28,24},{1,29},{... | collective-permute-start | bytes 1363976 | tf_op jit(solution)/shard_map/ppermute | solution.py:30
  256.4 3.9 %collective-permute-start.30 = (bf16[4,37,1536]{2,1,0:T(8,128)(2,1)S(1)}, bf16[4,37,1536]{2,1,0:T(8,128)(2,1)S(1)}, u32[]{:S(2)}, u32[]{:S(2)}) collective-permute-start(bf16[4,37,1536]{2,1,0:T(8,128)(2,1)S(1)} %get-tuple-element.28), channel_id=1, source_target_pairs={{0,12},{4,16},{8,20},{12,24},{16,28},{20,0},{24,4},{28,8},{1,13},{... | collective-permute-start | bytes 1363976 | tf_op jit(solution)/shard_map/ppermute | solution.py:30
  261.1 25.2 %collective-permute-start.32 = (bf16[4,37,1536]{2,1,0:T(8,128)(2,1)S(1)}, bf16[4,37,1536]{2,1,0:T(8,128)(2,1)S(1)}, u32[]{:S(2)}, u32[]{:S(2)}) collective-permute-start(bf16[4,37,1536]{2,1,0:T(8,128)(2,1)S(1)} %get-tuple-element.29), channel_id=1, source_target_pairs={{0,4},{4,8},{8,12},{12,16},{16,20},{20,24},{24,28},{28,0},{1,5},{5... | collective-permute-start | bytes 1363976 | tf_op jit(solution)/shard_map/ppermute | solution.py:30
  286.2 3.8 %collective-permute-done.26 = bf16[4,37,1536]{2,1,0:T(8,128)(2,1)S(1)} collective-permute-done((bf16[4,37,1536]{2,1,0:T(8,128)(2,1)S(1)}, bf16[4,37,1536]{2,1,0:T(8,128)(2,1)S(1)}, u32[]{:S(2)}, u32[]{:S(2)}) %collective-permute-start.26) | collective-permute-done | bytes 454688 | tf_op jit(solution)/shard_map/ppermute | solution.py:30
  293.8 5.9 %collective-permute-done.29 = bf16[4,37,1536]{2,1,0:T(8,128)(2,1)S(1)} collective-permute-done((bf16[4,37,1536]{2,1,0:T(8,128)(2,1)S(1)}, bf16[4,37,1536]{2,1,0:T(8,128)(2,1)S(1)}, u32[]{:S(2)}, u32[]{:S(2)}) %collective-permute-start.29) | collective-permute-done | bytes 454688 | tf_op jit(solution)/shard_map/ppermute | solution.py:29
  304.6 7.3 %collective-permute-start.33 = (bf16[4,1,16,16]{3,2,1,0:T(8,128)(2,1)S(1)}, bf16[4,1,16,16]{3,2,1,0:T(8,128)(2,1)S(1)}, u32[]{:S(2)}, u32[]{:S(2)}) collective-permute-start(bf16[4,1,16,16]{3,2,1,0:T(8,128)(2,1)S(1)} %get-tuple-element.64), channel_id=1, source_target_pairs={{0,4},{4,8},{8,12},{12,16},{16,20},{20,24},{24,28},{1,5},{5,9},{9,... | collective-permute-start | bytes 6152 | tf_op jit(solution)/shard_map/ppermute | solution.py:17
  318.0 7.2 %collective-permute-start.35 = (bf16[4,10,1,16]{3,2,1,0:T(2,128)(2,1)S(1)}, bf16[4,10,1,16]{3,2,1,0:T(2,128)(2,1)S(1)}, u32[]{:S(2)}, u32[]{:S(2)}) collective-permute-start(bf16[4,10,1,16]{3,2,1,0:T(2,128)(2,1)S(1)} %get-tuple-element.50), channel_id=1, source_target_pairs={{0,1},{1,2},{2,3},{4,5},{5,6},{6,7},{8,9},{9,10},{10,11},{12,13},{... | collective-permute-start | bytes 3848 | tf_op jit(solution)/shard_map/ppermute | solution.py:17
  (278 shorter events, 103.1 us)
Async XLA Ops:
  4.0 24.9 %collective-permute-start = (bf16[4,37,1536]{2,1,0:T(8,128)(2,1)}, bf16[4,37,1536]{2,1,0:T(8,128)(2,1)}, u32[]{:S(2)}, u32[]{:S(2)}) collective-permute-start(bf16[4,37,1536]{2,1,0:T(8,128)(2,1)} %get-tuple-element.47), channel_id=1, source_target_pairs={{0,4},{4,8},{8,12},{12,16},{16,20},{20,24},{24,28},{28,0},{1,5},{5... | collective-permute-start | bytes 1363976 | tf_op jit(solution)/shard_map/ppermute | solution.py:30
  7.6 40.2 %collective-permute-start.1 = (bf16[4,37,1536]{2,1,0:T(8,128)(2,1)}, bf16[4,37,1536]{2,1,0:T(8,128)(2,1)}, u32[]{:S(2)}, u32[]{:S(2)}) collective-permute-start(bf16[4,37,1536]{2,1,0:T(8,128)(2,1)} %get-tuple-element.47), channel_id=1, source_target_pairs={{0,8},{4,12},{8,16},{12,20},{16,24},{20,28},{24,0},{28,4},{1,9},{5... | collective-permute-start | bytes 1363976 | tf_op jit(solution)/shard_map/ppermute | solution.py:30
  9.2 39.7 %collective-permute-start.2 = (bf16[4,37,1536]{2,1,0:T(8,128)(2,1)}, bf16[4,37,1536]{2,1,0:T(8,128)(2,1)}, u32[]{:S(2)}, u32[]{:S(2)}) collective-permute-start(bf16[4,37,1536]{2,1,0:T(8,128)(2,1)} %get-tuple-element.47), channel_id=1, source_target_pairs={{0,12},{4,16},{8,20},{12,24},{16,28},{20,0},{24,4},{28,8},{1,13},{... | collective-permute-start | bytes 1363976 | tf_op jit(solution)/shard_map/ppermute | solution.py:30
  11.9 32.1 %collective-permute-start.3 = (bf16[4,37,1536]{2,1,0:T(8,128)(2,1)}, bf16[4,37,1536]{2,1,0:T(8,128)(2,1)}, u32[]{:S(2)}, u32[]{:S(2)}) collective-permute-start(bf16[4,37,1536]{2,1,0:T(8,128)(2,1)} %get-tuple-element.47), channel_id=1, source_target_pairs={{0,24},{4,28},{8,0},{12,4},{16,8},{20,12},{24,16},{28,20},{1,25},{... | collective-permute-start | bytes 1363976 | tf_op jit(solution)/shard_map/ppermute | solution.py:29
  13.2 41.6 %collective-permute-start.5 = (bf16[4,37,1536]{2,1,0:T(8,128)(2,1)}, bf16[4,37,1536]{2,1,0:T(8,128)(2,1)}, u32[]{:S(2)}, u32[]{:S(2)}) collective-permute-start(bf16[4,37,1536]{2,1,0:T(8,128)(2,1)} %get-tuple-element.47), channel_id=1, source_target_pairs={{0,20},{4,24},{8,28},{12,0},{16,4},{20,8},{24,12},{28,16},{1,21},{... | collective-permute-start | bytes 1363976 | tf_op jit(solution)/shard_map/ppermute | solution.py:30
  28.9 28.1 %collective-permute-start.6 = (bf16[4,37,1536]{2,1,0:T(8,128)(2,1)}, bf16[4,37,1536]{2,1,0:T(8,128)(2,1)S(1)}, u32[]{:S(2)}, u32[]{:S(2)}) collective-permute-start(bf16[4,37,1536]{2,1,0:T(8,128)(2,1)} %get-tuple-element.47), channel_id=1, source_target_pairs={{0,28},{4,0},{8,4},{12,8},{16,12},{20,16},{24,20},{28,24},{1,29},{... | collective-permute-start | bytes 1363976 | tf_op jit(solution)/shard_map/ppermute | solution.py:30
  43.9 10.8 %collective-permute-start.4 = (bf16[4,37,1536]{2,1,0:T(8,128)(2,1)}, bf16[4,37,1536]{2,1,0:T(8,128)(2,1)S(1)}, u32[]{:S(2)}, u32[]{:S(2)}) collective-permute-start(bf16[4,37,1536]{2,1,0:T(8,128)(2,1)} %collective-permute-done.3), channel_id=1, source_target_pairs={{0,24},{4,28},{8,0},{12,4},{16,8},{20,12},{24,16},{28,20},{1,25},{... | collective-permute-start | bytes 1363976 | tf_op jit(solution)/shard_map/ppermute | solution.py:29
  69.0 18.1 %collective-permute-start.8 = (bf16[1184,384]{1,0:T(8,128)(2,1)}, bf16[1184,384]{1,0:T(8,128)(2,1)S(1)}, u32[]{:S(2)}, u32[]{:S(2)}) collective-permute-start(bf16[1184,384]{1,0:T(8,128)(2,1)} %reshape.319.refs_0_), channel_id=1, source_target_pairs={{0,2},{1,3},{2,0},{3,1},{4,6},{5,7},{6,4},{7,5},{8,10},{9,11},{10,... | collective-permute-start | bytes 2727944 | tf_op jit(solution)/shard_map/ppermute | solution.py:205
  74.7 26.0 %collective-permute-start.7 = (bf16[1184,384]{1,0:T(8,128)(2,1)S(1)}, bf16[1184,384]{1,0:T(8,128)(2,1)S(1)}, u32[]{:S(2)}, u32[]{:S(2)}) collective-permute-start(bf16[1184,384]{1,0:T(8,128)(2,1)S(1)} %copy-done.5), channel_id=1, source_target_pairs={{0,1},{1,0},{2,3},{3,2},{4,5},{5,4},{6,7},{7,6},{8,9},{9,8},{10,11... | collective-permute-start | bytes 2727944 | tf_op jit(solution)/shard_map/ppermute | solution.py:208
  87.2 14.4 %collective-permute-start.9 = (bf16[1184,384]{1,0:T(8,128)(2,1)S(1)}, bf16[1184,384]{1,0:T(8,128)(2,1)}, u32[]{:S(2)}, u32[]{:S(2)}) collective-permute-start(bf16[1184,384]{1,0:T(8,128)(2,1)S(1)} %collective-permute-done.8.refs_2_), channel_id=1, source_target_pairs={{0,1},{1,0},{2,3},{3,2},{4,5},{5,4},{6,7},{7,6},{8,9},{9,8},{10,11... | collective-permute-start | bytes 2727944 | tf_op jit(solution)/shard_map/ppermute | solution.py:210
  120.5 17.8 %collective-permute-start.13 = (bf16[4,37,1536]{2,1,0:T(8,128)(2,1)S(1)}, bf16[4,37,1536]{2,1,0:T(8,128)(2,1)S(1)}, u32[]{:S(2)}, u32[]{:S(2)}) collective-permute-start(bf16[4,37,1536]{2,1,0:T(8,128)(2,1)S(1)} %get-tuple-element.34), channel_id=1, source_target_pairs={{0,24},{4,28},{8,0},{12,4},{16,8},{20,12},{24,16},{28,20},{1,25},{... | collective-permute-start | bytes 1363976 | tf_op jit(solution)/shard_map/ppermute | solution.py:29
  123.9 21.4 %collective-permute-start.10 = (bf16[4,37,1536]{2,1,0:T(8,128)(2,1)S(1)}, bf16[4,37,1536]{2,1,0:T(8,128)(2,1)S(1)}, u32[]{:S(2)}, u32[]{:S(2)}) collective-permute-start(bf16[4,37,1536]{2,1,0:T(8,128)(2,1)S(1)} %get-tuple-element.31), channel_id=1, source_target_pairs={{0,28},{4,0},{8,4},{12,8},{16,12},{20,16},{24,20},{28,24},{1,29},{... | collective-permute-start | bytes 1363976 | tf_op jit(solution)/shard_map/ppermute | solution.py:30
  134.1 33.2 %collective-permute-start.11 = (bf16[4,37,1536]{2,1,0:T(8,128)(2,1)S(1)}, bf16[4,37,1536]{2,1,0:T(8,128)(2,1)S(1)}, u32[]{:S(2)}, u32[]{:S(2)}) collective-permute-start(bf16[4,37,1536]{2,1,0:T(8,128)(2,1)S(1)} %get-tuple-element.32), channel_id=1, source_target_pairs={{0,24},{4,28},{8,0},{12,4},{16,8},{20,12},{24,16},{28,20},{1,25},{... | collective-permute-start | bytes 1363976 | tf_op jit(solution)/shard_map/ppermute | solution.py:30
  134.1 35.1 %collective-permute-start.12 = (bf16[4,37,1536]{2,1,0:T(8,128)(2,1)S(1)}, bf16[4,37,1536]{2,1,0:T(8,128)(2,1)S(1)}, u32[]{:S(2)}, u32[]{:S(2)}) collective-permute-start(bf16[4,37,1536]{2,1,0:T(8,128)(2,1)S(1)} %get-tuple-element.33), channel_id=1, source_target_pairs={{0,20},{4,24},{8,28},{12,0},{16,4},{20,8},{24,12},{28,16},{1,21},{... | collective-permute-start | bytes 1363976 | tf_op jit(solution)/shard_map/ppermute | solution.py:30
  134.5 34.7 %collective-permute-start.15 = (bf16[4,37,1536]{2,1,0:T(8,128)(2,1)S(1)}, bf16[4,37,1536]{2,1,0:T(8,128)(2,1)S(1)}, u32[]{:S(2)}, u32[]{:S(2)}) collective-permute-start(bf16[4,37,1536]{2,1,0:T(8,128)(2,1)S(1)} %get-tuple-element.35), channel_id=1, source_target_pairs={{0,12},{4,16},{8,20},{12,24},{16,28},{20,0},{24,4},{28,8},{1,13},{... | collective-permute-start | bytes 1363976 | tf_op jit(solution)/shard_map/ppermute | solution.py:30
  138.4 30.9 %collective-permute-start.16 = (bf16[4,37,1536]{2,1,0:T(8,128)(2,1)S(1)}, bf16[4,37,1536]{2,1,0:T(8,128)(2,1)S(1)}, u32[]{:S(2)}, u32[]{:S(2)}) collective-permute-start(bf16[4,37,1536]{2,1,0:T(8,128)(2,1)S(1)} %get-tuple-element.37), channel_id=1, source_target_pairs={{0,8},{4,12},{8,16},{12,20},{16,24},{20,28},{24,0},{28,4},{1,9},{5... | collective-permute-start | bytes 1363976 | tf_op jit(solution)/shard_map/ppermute | solution.py:30
  145.3 33.1 %collective-permute-start.17 = (bf16[4,37,1536]{2,1,0:T(8,128)(2,1)S(1)}, bf16[4,37,1536]{2,1,0:T(8,128)(2,1)S(1)}, u32[]{:S(2)}, u32[]{:S(2)}) collective-permute-start(bf16[4,37,1536]{2,1,0:T(8,128)(2,1)S(1)} %get-tuple-element.36), channel_id=1, source_target_pairs={{0,4},{4,8},{8,12},{12,16},{16,20},{20,24},{24,28},{28,0},{1,5},{5... | collective-permute-start | bytes 1363976 | tf_op jit(solution)/shard_map/ppermute | solution.py:30
  167.3 11.3 %collective-permute-start.14 = (bf16[4,37,1536]{2,1,0:T(8,128)(2,1)S(1)}, bf16[4,37,1536]{2,1,0:T(8,128)(2,1)S(1)}, u32[]{:S(2)}, u32[]{:S(2)}) collective-permute-start(bf16[4,37,1536]{2,1,0:T(8,128)(2,1)S(1)} %collective-permute-done.13), channel_id=1, source_target_pairs={{0,24},{4,28},{8,0},{12,4},{16,8},{20,12},{24,16},{28,20},{1,25},{... | collective-permute-start | bytes 1363976 | tf_op jit(solution)/shard_map/ppermute | solution.py:29
  180.6 23.3 %collective-permute-start.18 = (bf16[4,37,1536]{2,1,0:T(8,128)(2,1)S(1)}, bf16[4,37,1536]{2,1,0:T(8,128)(2,1)S(1)}, u32[]{:S(2)}, u32[]{:S(2)}) collective-permute-start(bf16[4,37,1536]{2,1,0:T(8,128)(2,1)S(1)} %pad_maximum_fusion.5), channel_id=1, source_target_pairs={{0,4},{4,8},{8,12},{12,16},{16,20},{20,24},{24,28},{28,0},{1,5},{5... | collective-permute-start | bytes 1363976 | tf_op jit(solution)/shard_map/ppermute | solution.py:30
  191.0 30.6 %collective-permute-start.21 = (bf16[4,37,1536]{2,1,0:T(8,128)(2,1)S(1)}, bf16[4,37,1536]{2,1,0:T(8,128)(2,1)S(1)}, u32[]{:S(2)}, u32[]{:S(2)}) collective-permute-start(bf16[4,37,1536]{2,1,0:T(8,128)(2,1)S(1)} %pad_maximum_fusion.5), channel_id=1, source_target_pairs={{0,24},{4,28},{8,0},{12,4},{16,8},{20,12},{24,16},{28,20},{1,25},{... | collective-permute-start | bytes 1363976 | tf_op jit(solution)/shard_map/ppermute | solution.py:29
  194.4 32.5 %collective-permute-start.19 = (bf16[4,37,1536]{2,1,0:T(8,128)(2,1)S(1)}, bf16[4,37,1536]{2,1,0:T(8,128)(2,1)S(1)}, u32[]{:S(2)}, u32[]{:S(2)}) collective-permute-start(bf16[4,37,1536]{2,1,0:T(8,128)(2,1)S(1)} %pad_maximum_fusion.5), channel_id=1, source_target_pairs={{0,8},{4,12},{8,16},{12,20},{16,24},{20,28},{24,0},{28,4},{1,9},{5... | collective-permute-start | bytes 1363976 | tf_op jit(solution)/shard_map/ppermute | solution.py:30
  194.4 32.5 %collective-permute-start.20 = (bf16[4,37,1536]{2,1,0:T(8,128)(2,1)S(1)}, bf16[4,37,1536]{2,1,0:T(8,128)(2,1)S(1)}, u32[]{:S(2)}, u32[]{:S(2)}) collective-permute-start(bf16[4,37,1536]{2,1,0:T(8,128)(2,1)S(1)} %pad_maximum_fusion.5), channel_id=1, source_target_pairs={{0,12},{4,16},{8,20},{12,24},{16,28},{20,0},{24,4},{28,8},{1,13},{... | collective-permute-start | bytes 1363976 | tf_op jit(solution)/shard_map/ppermute | solution.py:30
  194.4 37.4 %collective-permute-start.23 = (bf16[4,37,1536]{2,1,0:T(8,128)(2,1)S(1)}, bf16[4,37,1536]{2,1,0:T(8,128)(2,1)S(1)}, u32[]{:S(2)}, u32[]{:S(2)}) collective-permute-start(bf16[4,37,1536]{2,1,0:T(8,128)(2,1)S(1)} %pad_maximum_fusion.5), channel_id=1, source_target_pairs={{0,20},{4,24},{8,28},{12,0},{16,4},{20,8},{24,12},{28,16},{1,21},{... | collective-permute-start | bytes 1363976 | tf_op jit(solution)/shard_map/ppermute | solution.py:30
  203.8 28.2 %collective-permute-start.24 = (bf16[4,37,1536]{2,1,0:T(8,128)(2,1)S(1)}, bf16[4,37,1536]{2,1,0:T(8,128)(2,1)S(1)}, u32[]{:S(2)}, u32[]{:S(2)}) collective-permute-start(bf16[4,37,1536]{2,1,0:T(8,128)(2,1)S(1)} %pad_maximum_fusion.5), channel_id=1, source_target_pairs={{0,28},{4,0},{8,4},{12,8},{16,12},{20,16},{24,20},{28,24},{1,29},{... | collective-permute-start | bytes 1363976 | tf_op jit(solution)/shard_map/ppermute | solution.py:30
  221.6 10.2 %collective-permute-start.22 = (bf16[4,37,1536]{2,1,0:T(8,128)(2,1)S(1)}, bf16[4,37,1536]{2,1,0:T(8,128)(2,1)S(1)}, u32[]{:S(2)}, u32[]{:S(2)}) collective-permute-start(bf16[4,37,1536]{2,1,0:T(8,128)(2,1)S(1)} %collective-permute-done.21), channel_id=1, source_target_pairs={{0,24},{4,28},{8,0},{12,4},{16,8},{20,12},{24,16},{28,20},{1,25},{... | collective-permute-start | bytes 1363976 | tf_op jit(solution)/shard_map/ppermute | solution.py:29
  247.8 12.4 %collective-permute-start.28 = (bf16[4,37,1536]{2,1,0:T(8,128)(2,1)S(1)}, bf16[4,37,1536]{2,1,0:T(8,128)(2,1)S(1)}, u32[]{:S(2)}, u32[]{:S(2)}) collective-permute-start(bf16[4,37,1536]{2,1,0:T(8,128)(2,1)S(1)} %get-tuple-element.27), channel_id=1, source_target_pairs={{0,24},{4,28},{8,0},{12,4},{16,8},{20,12},{24,16},{28,20},{1,25},{... | collective-permute-start | bytes 1363976 | tf_op jit(solution)/shard_map/ppermute | solution.py:29
  254.8 35.2 %collective-permute-start.26 = (bf16[4,37,1536]{2,1,0:T(8,128)(2,1)S(1)}, bf16[4,37,1536]{2,1,0:T(8,128)(2,1)S(1)}, u32[]{:S(2)}, u32[]{:S(2)}) collective-permute-start(bf16[4,37,1536]{2,1,0:T(8,128)(2,1)S(1)} %get-tuple-element.25), channel_id=1, source_target_pairs={{0,24},{4,28},{8,0},{12,4},{16,8},{20,12},{24,16},{28,20},{1,25},{... | collective-permute-start | bytes 1363976 | tf_op jit(solution)/shard_map/ppermute | solution.py:30
  256.3 35.1 %collective-permute-start.27 = (bf16[4,37,1536]{2,1,0:T(8,128)(2,1)S(1)}, bf16[4,37,1536]{2,1,0:T(8,128)(2,1)S(1)}, u32[]{:S(2)}, u32[]{:S(2)}) collective-permute-start(bf16[4,37,1536]{2,1,0:T(8,128)(2,1)S(1)} %get-tuple-element.26), channel_id=1, source_target_pairs={{0,20},{4,24},{8,28},{12,0},{16,4},{20,8},{24,12},{28,16},{1,21},{... | collective-permute-start | bytes 1363976 | tf_op jit(solution)/shard_map/ppermute | solution.py:30
  256.4 35.0 %collective-permute-start.30 = (bf16[4,37,1536]{2,1,0:T(8,128)(2,1)S(1)}, bf16[4,37,1536]{2,1,0:T(8,128)(2,1)S(1)}, u32[]{:S(2)}, u32[]{:S(2)}) collective-permute-start(bf16[4,37,1536]{2,1,0:T(8,128)(2,1)S(1)} %get-tuple-element.28), channel_id=1, source_target_pairs={{0,12},{4,16},{8,20},{12,24},{16,28},{20,0},{24,4},{28,8},{1,13},{... | collective-permute-start | bytes 1363976 | tf_op jit(solution)/shard_map/ppermute | solution.py:30
  260.2 31.2 %collective-permute-start.31 = (bf16[4,37,1536]{2,1,0:T(8,128)(2,1)S(1)}, bf16[4,37,1536]{2,1,0:T(8,128)(2,1)S(1)}, u32[]{:S(2)}, u32[]{:S(2)}) collective-permute-start(bf16[4,37,1536]{2,1,0:T(8,128)(2,1)S(1)} %get-tuple-element.30), channel_id=1, source_target_pairs={{0,8},{4,12},{8,16},{12,20},{16,24},{20,28},{24,0},{28,4},{1,9},{5... | collective-permute-start | bytes 1363976 | tf_op jit(solution)/shard_map/ppermute | solution.py:30
  261.1 32.7 %collective-permute-start.32 = (bf16[4,37,1536]{2,1,0:T(8,128)(2,1)S(1)}, bf16[4,37,1536]{2,1,0:T(8,128)(2,1)S(1)}, u32[]{:S(2)}, u32[]{:S(2)}) collective-permute-start(bf16[4,37,1536]{2,1,0:T(8,128)(2,1)S(1)} %get-tuple-element.29), channel_id=1, source_target_pairs={{0,4},{4,8},{8,12},{12,16},{16,20},{20,24},{24,28},{28,0},{1,5},{5... | collective-permute-start | bytes 1363976 | tf_op jit(solution)/shard_map/ppermute | solution.py:30
  304.6 10.5 %collective-permute-start.33 = (bf16[4,1,16,16]{3,2,1,0:T(8,128)(2,1)S(1)}, bf16[4,1,16,16]{3,2,1,0:T(8,128)(2,1)S(1)}, u32[]{:S(2)}, u32[]{:S(2)}) collective-permute-start(bf16[4,1,16,16]{3,2,1,0:T(8,128)(2,1)S(1)} %get-tuple-element.64), channel_id=1, source_target_pairs={{0,4},{4,8},{8,12},{12,16},{16,20},{20,24},{24,28},{1,5},{5,9},{9,... | collective-permute-start | bytes 6152 | tf_op jit(solution)/shard_map/ppermute | solution.py:17
  (59 other events, 833.1 us)

commit v7 on v6

--- a/solution.py
+++ b/solution.py
@@ -28,6 +28,37 @@
         step = [(i, (i + count - 2) % count) for i in range(count)]
         return lax.ppermute(lax.ppermute(block, axis, step), axis, step)
     return lax.ppermute(block, axis, [(i, (i + shift) % count) for i in range(count)])
+
+
+def bordered(block):
+    rows = lax.axis_size("head")
+    cols = lax.axis_size("blk")
+
+    def along(piece, axis, count, step):
+        pairs = [(i, i + step) for i in range(count) if 0 <= i + step < count]
+        return lax.ppermute(piece, axis, pairs)
+
+    def diagonal(piece, row_step, col_step):
+        pairs = [
+            (i * cols + j, (i + row_step) * cols + j + col_step)
+            for i in range(rows)
+            for j in range(cols)
+            if 0 <= i + row_step < rows and 0 <= j + col_step < cols
+        ]
+        return lax.ppermute(piece, ("head", "blk"), pairs)
+
+    above = along(block[:, -1:], "head", rows, 1)
+    below = along(block[:, :1], "head", rows, -1)
+    left = along(block[:, :, -1:], "blk", cols, 1)
+    right = along(block[:, :, :1], "blk", cols, -1)
+    above_left = diagonal(block[:, -1:, -1:], 1, 1)
+    above_right = diagonal(block[:, -1:, :1], 1, -1)
+    below_left = diagonal(block[:, :1, -1:], -1, 1)
+    below_right = diagonal(block[:, :1, :1], -1, -1)
+    top = jnp.concatenate([above_left, above, above_right], 2)
+    middle = jnp.concatenate([left, block, right], 2)
+    bottom = jnp.concatenate([below_left, below, below_right], 2)
+    return jnp.concatenate([top, middle, bottom], 1)
 
 
 def gather_slots(block, axis):
@@ -268,7 +299,7 @@
     step_size = noise_level(following) - noise_level(current)
     latent_next = latent_grid + step_size[:, None, None, None] * velocity
     decoded_in = (latent_next / 1.5305 + 0.0609).astype(jnp.bfloat16)
-    padded = extended(decoded_in, (("head", 1), ("blk", 2)), 1)
+    padded = bordered(decoded_in)
     features = convolve(padded, conv_kernel)
     return (image_states, text_states, latent_next, features)
 

time: 338 us -> 350 us (1.036)
  starting transfers between devices: 149 us -> 159 us
    ppermute x4 -> x8, starting transfers between devices: 17.7 us -> 27.4 us  [the longest x4 16.7 us: along(): return lax.ppermute(piece, axis, pairs)]
    ppermute x4 -> x8, waiting for transfers between devices: 5.52 us -> 7.69 us  [the longest x4 7.68 us: diagonal(): return lax.ppermute(piece, ('head', 'blk'), pairs)]
  transfers between devices with their start and end apart: 37 -> 41, of which waited for: 18 -> 18; matrix products, arithmetic and copies ran while one was open for 11% -> 11% of each run, Pallas kernels for 0% -> 0%
where the time goes in v7:
time: 350 us; the launch traced here: 345 us
  starting transfers between devices  159 us (45%)
  waiting for transfers between devices  86.6 us (25%)
  matrix products  36.4 us (10%)
  local copies, waits for them, and re-layouts  24.9 us (7%)
  other arithmetic  21.6 us (6%)
  Pallas kernels  14.2 us (4%)
    ppermute x22, starting transfers between devices, moved(): lax.ppermute(block, axis, [(i, (i + shift) % count) for i in range(count)])  100 us
    ppermute x8, waiting for transfers between devices, moved(): return lax.ppermute(lax.ppermute(block, axis, step), axis, step)  45.8 us
    ppermute x22, waiting for transfers between devices, moved(): lax.ppermute(block, axis, [(i, (i + shift) % count) for i in range(count)])  28.3 us
    ppermute x8, starting transfers between devices, moved(): return lax.ppermute(lax.ppermute(block, axis, step), axis, step)  21.4 us
    ppermute x4, starting transfers between devices, along(): return lax.ppermute(piece, axis, pairs)  16.7 us
    pallas_call x1, Pallas kernels, attend(): pl.pallas_call(attention_kernel, grid=(requests, heads), in_specs=[pl.Blo...  14.2 us
    unnamed x131, local copies, waits for them, and re-layouts  11.1 us
    ppermute x4, starting transfers between devices, diagonal(): return lax.ppermute(piece, ('head', 'blk'), pairs)  10.7 us
  transfers between devices with their start and end apart: 41, of which 18 were waited for; matrix products, arithmetic and copies ran while one was open for 11% of the time, Pallas kernels for 0%

profile of v7, /device:TPU:1, one launch (start us, length us, event | category | flops | bytes accessed | tf_op | source)
XLA Modules:
  0.0 345.1 jit_solution(5500901788537120614)
XLA Ops:
  4.0 3.6 %collective-permute-start = (bf16[4,37,1536]{2,1,0:T(8,128)(2,1)}, bf16[4,37,1536]{2,1,0:T(8,128)(2,1)}, u32[]{:S(2)}, u32[]{:S(2)}) collective-permute-start(bf16[4,37,1536]{2,1,0:T(8,128)(2,1)} %get-tuple-element.47), channel_id=1, source_target_pairs={{0,4},{4,8},{8,12},{12,16},{16,20},{20,24},{24,28},{28,0},{1,5},{5... | collective-permute-start | bytes 1363976 | tf_op jit(solution)/shard_map/ppermute | solution.py:30
  29.2 14.8 %collective-permute-done.3 = bf16[4,37,1536]{2,1,0:T(8,128)(2,1)} collective-permute-done((bf16[4,37,1536]{2,1,0:T(8,128)(2,1)}, bf16[4,37,1536]{2,1,0:T(8,128)(2,1)}, u32[]{:S(2)}, u32[]{:S(2)}) %collective-permute-start.3) | collective-permute-done | bytes 454688 | tf_op jit(solution)/shard_map/ppermute | solution.py:29
  50.0 4.8 %collective-permute-done.4 = bf16[4,37,1536]{2,1,0:T(8,128)(2,1)S(1)} collective-permute-done((bf16[4,37,1536]{2,1,0:T(8,128)(2,1)}, bf16[4,37,1536]{2,1,0:T(8,128)(2,1)S(1)}, u32[]{:S(2)}, u32[]{:S(2)}) %collective-permute-start.4) | collective-permute-done | bytes 454688 | tf_op jit(solution)/shard_map/ppermute | solution.py:29
  74.7 4.2 %collective-permute-start.7 = (bf16[1184,384]{1,0:T(8,128)(2,1)S(1)}, bf16[1184,384]{1,0:T(8,128)(2,1)S(1)}, u32[]{:S(2)}, u32[]{:S(2)}) collective-permute-start(bf16[1184,384]{1,0:T(8,128)(2,1)S(1)} %copy-done.5), channel_id=1, source_target_pairs={{0,1},{1,0},{2,3},{3,2},{4,5},{5,4},{6,7},{7,6},{8,9},{9,8},{10,11... | collective-permute-start | bytes 2727944 | tf_op jit(solution)/shard_map/ppermute | solution.py:239
  82.3 4.9 %collective-permute-done.8.refs_2_ = bf16[1184,384]{1,0:T(8,128)(2,1)S(1)} collective-permute-done((bf16[1184,384]{1,0:T(8,128)(2,1)}, bf16[1184,384]{1,0:T(8,128)(2,1)S(1)}, u32[]{:S(2)}, u32[]{:S(2)}) %collective-permute-start.8) | collective-permute-done | bytes 909344 | tf_op jit(solution)/shard_map/ppermute | solution.py:236
  87.1 4.7 %collective-permute-start.9 = (bf16[1184,384]{1,0:T(8,128)(2,1)S(1)}, bf16[1184,384]{1,0:T(8,128)(2,1)}, u32[]{:S(2)}, u32[]{:S(2)}) collective-permute-start(bf16[1184,384]{1,0:T(8,128)(2,1)S(1)} %collective-permute-done.8.refs_2_), channel_id=1, source_target_pairs={{0,1},{1,0},{2,3},{3,2},{4,5},{5,4},{6,7},{7,6},{8,9},{9,8},{10,11... | collective-permute-start | bytes 2727944 | tf_op jit(solution)/shard_map/ppermute | solution.py:241
  91.8 4.0 %fusion.204 = f32[8,4,32,384]{3,2,1,0:T(8,128)S(1)} fusion(bf16[1536,384,1,1]{0,1,3,2:T(8,128)(2,1)S(1)} %bitcast.305, f32[8,4,37,1536]{3,2,1,0:T(8,128)} %copy-done.1, f32[4,1536]{1,0:T(4,128)S(1)} %copy-done.30, f32[4,1536]{1,0:T(4,128)S(1)} %bitcast.316, f32[8,4,32]{2,1,0:T(4,128)S(1)} %copy-done.37, f32[8,4,32]{2,1,0:T(4,128)S(1)} %broadcast_multiply_fusion.1), kind=kOutput, calls=%fused_computation.348 | convolution fusion | flops 1215823872 | bytes 9101312 | tf_op jit(solution)/shard_map/arnd,de->arne/dot_general | solution.py:166
  101.6 14.2 %shard_map.219 = bf16[4,296,384]{2,1,0:T(8,128)(2,1)} custom-call(bf16[4,296,384]{2,1,0:T(8,128)(2,1)} %copy.107.query_ref, bf16[1184,384]{1,0:T(8,128)(2,1)} %reshape.319.refs_0_, bf16[1184,384]{1,0:T(8,128)(2,1)} %copy-done.10, bf16[1184,384]{1,0:T(8,128)(2,1)} %copy-done.9, bf16[1184,384]{1,0:T(8,128)(2,1)} %collective-permute-done.9.refs_3_, ...), custom_call_target="tpu_custom_call" | custom-call | tf_op jit(solution)/shard_map/pallas_call | solution.py:109
  123.9 10.2 %collective-permute-start.10 = (bf16[4,37,1536]{2,1,0:T(8,128)(2,1)S(1)}, bf16[4,37,1536]{2,1,0:T(8,128)(2,1)S(1)}, u32[]{:S(2)}, u32[]{:S(2)}) collective-permute-start(bf16[4,37,1536]{2,1,0:T(8,128)(2,1)S(1)} %get-tuple-element.31), channel_id=1, source_target_pairs={{0,28},{4,0},{8,4},{12,8},{16,12},{20,16},{24,20},{28,24},{1,29},{... | collective-permute-start | bytes 1363976 | tf_op jit(solution)/shard_map/ppermute | solution.py:30
  134.5 3.9 %collective-permute-start.15 = (bf16[4,37,1536]{2,1,0:T(8,128)(2,1)S(1)}, bf16[4,37,1536]{2,1,0:T(8,128)(2,1)S(1)}, u32[]{:S(2)}, u32[]{:S(2)}) collective-permute-start(bf16[4,37,1536]{2,1,0:T(8,128)(2,1)S(1)} %get-tuple-element.35), channel_id=1, source_target_pairs={{0,12},{4,16},{8,20},{12,24},{16,28},{20,0},{24,4},{28,8},{1,13},{... | collective-permute-start | bytes 1363976 | tf_op jit(solution)/shard_map/ppermute | solution.py:30
  139.8 5.5 %collective-permute-done.10 = bf16[4,37,1536]{2,1,0:T(8,128)(2,1)S(1)} collective-permute-done((bf16[4,37,1536]{2,1,0:T(8,128)(2,1)S(1)}, bf16[4,37,1536]{2,1,0:T(8,128)(2,1)S(1)}, u32[]{:S(2)}, u32[]{:S(2)}) %collective-permute-start.10) | collective-permute-done | bytes 454688 | tf_op jit(solution)/shard_map/ppermute | solution.py:30
  145.3 20.3 %collective-permute-start.17 = (bf16[4,37,1536]{2,1,0:T(8,128)(2,1)S(1)}, bf16[4,37,1536]{2,1,0:T(8,128)(2,1)S(1)}, u32[]{:S(2)}, u32[]{:S(2)}) collective-permute-start(bf16[4,37,1536]{2,1,0:T(8,128)(2,1)S(1)} %get-tuple-element.36), channel_id=1, source_target_pairs={{0,4},{4,8},{8,12},{12,16},{16,20},{20,24},{24,28},{28,0},{1,5},{5... | collective-permute-start | bytes 1363976 | tf_op jit(solution)/shard_map/ppermute | solution.py:30
  169.2 9.2 %collective-permute-done.17 = bf16[4,37,1536]{2,1,0:T(8,128)(2,1)S(1)} collective-permute-done((bf16[4,37,1536]{2,1,0:T(8,128)(2,1)S(1)}, bf16[4,37,1536]{2,1,0:T(8,128)(2,1)S(1)}, u32[]{:S(2)}, u32[]{:S(2)}) %collective-permute-start.17) | collective-permute-done | bytes 454688 | tf_op jit(solution)/shard_map/ppermute | solution.py:30
  180.5 10.4 %collective-permute-start.18 = (bf16[4,37,1536]{2,1,0:T(8,128)(2,1)S(1)}, bf16[4,37,1536]{2,1,0:T(8,128)(2,1)S(1)}, u32[]{:S(2)}, u32[]{:S(2)}) collective-permute-start(bf16[4,37,1536]{2,1,0:T(8,128)(2,1)S(1)} %pad_maximum_fusion.5), channel_id=1, source_target_pairs={{0,4},{4,8},{8,12},{12,16},{16,20},{20,24},{24,28},{28,0},{1,5},{5... | collective-permute-start | bytes 1363976 | tf_op jit(solution)/shard_map/ppermute | solution.py:30
  194.4 5.4 %collective-permute-start.23 = (bf16[4,37,1536]{2,1,0:T(8,128)(2,1)S(1)}, bf16[4,37,1536]{2,1,0:T(8,128)(2,1)S(1)}, u32[]{:S(2)}, u32[]{:S(2)}) collective-permute-start(bf16[4,37,1536]{2,1,0:T(8,128)(2,1)S(1)} %pad_maximum_fusion.5), channel_id=1, source_target_pairs={{0,20},{4,24},{8,28},{12,0},{16,4},{20,8},{24,12},{28,16},{1,21},{... | collective-permute-start | bytes 1363976 | tf_op jit(solution)/shard_map/ppermute | solution.py:30
  199.8 4.0 %collective-permute-done.18 = bf16[4,37,1536]{2,1,0:T(8,128)(2,1)S(1)} collective-permute-done((bf16[4,37,1536]{2,1,0:T(8,128)(2,1)S(1)}, bf16[4,37,1536]{2,1,0:T(8,128)(2,1)S(1)}, u32[]{:S(2)}, u32[]{:S(2)}) %collective-permute-start.18) | collective-permute-done | bytes 454688 | tf_op jit(solution)/shard_map/ppermute | solution.py:30
  206.3 15.3 %collective-permute-done.21 = bf16[4,37,1536]{2,1,0:T(8,128)(2,1)S(1)} collective-permute-done((bf16[4,37,1536]{2,1,0:T(8,128)(2,1)S(1)}, bf16[4,37,1536]{2,1,0:T(8,128)(2,1)S(1)}, u32[]{:S(2)}, u32[]{:S(2)}) %collective-permute-start.21) | collective-permute-done | bytes 454688 | tf_op jit(solution)/shard_map/ppermute | solution.py:29
  221.6 3.9 %collective-permute-start.22 = (bf16[4,37,1536]{2,1,0:T(8,128)(2,1)S(1)}, bf16[4,37,1536]{2,1,0:T(8,128)(2,1)S(1)}, u32[]{:S(2)}, u32[]{:S(2)}) collective-permute-start(bf16[4,37,1536]{2,1,0:T(8,128)(2,1)S(1)} %collective-permute-done.21), channel_id=1, source_target_pairs={{0,24},{4,28},{8,0},{12,4},{16,8},{20,12},{24,16},{28,20},{1,25},{... | collective-permute-start | bytes 1363976 | tf_op jit(solution)/shard_map/ppermute | solution.py:29
  227.0 4.8 %collective-permute-done.22 = bf16[4,37,1536]{2,1,0:T(8,128)(2,1)S(1)} collective-permute-done((bf16[4,37,1536]{2,1,0:T(8,128)(2,1)S(1)}, bf16[4,37,1536]{2,1,0:T(8,128)(2,1)S(1)}, u32[]{:S(2)}, u32[]{:S(2)}) %collective-permute-start.22) | collective-permute-done | bytes 454688 | tf_op jit(solution)/shard_map/ppermute | solution.py:29
  233.0 4.1 %fusion.8 = bf16[8,4,32,768]{3,2,1,0:T(8,128)(2,1)} fusion(bf16[1536,768]{1,0:T(8,128)(2,1)S(1)} %copy-done.49, bf16[8,4,37,1536]{3,2,1,0:T(8,128)(2,1)S(1)} %bitcast_dynamic-update-slice_fusion), kind=kOutput, calls=%fused_computation.43 | convolution fusion | flops 2422996992 | bytes 7077888 | tf_op jit(solution)/shard_map/arnd,df->arnf/dot_general | solution.py:275
  237.1 4.7 %convolution_convert_fusion.3 = bf16[8,4,5,1536]{3,0,2,1:T(8,128)(2,1)} fusion(bf16[768,1536]{1,0:T(8,128)(2,1)} %param.37, bf16[1536,768]{1,0:T(8,128)(2,1)} %param.35, bf16[8,4,5,1536]{3,2,1,0:T(8,128)(2,1)} %slice.349), kind=kOutput, calls=%fused_computation.47 | convolution fusion | flops 756326400 | bytes 5701632 | tf_op jit(solution)/shard_map/arnf,fd->arnd/dot_general | solution.py:283
  243.0 4.2 %convolution_convert_fusion = bf16[8,4,32,1536]{3,2,1,0:T(8,128)(2,1)S(1)} fusion(bf16[8,4,32,768]{3,2,1,0:T(8,128)(2,1)} %fusion.8, bf16[768,1536]{1,0:T(8,128)(2,1)S(1)} %copy-done), kind=kOutput, calls=%fused_computation.19 | convolution fusion | flops 2417491968 | bytes 7077888 | tf_op jit(solution)/shard_map/arnf,fd->arnd/dot_general | solution.py:282
  256.3 3.9 %collective-permute-start.30 = (bf16[4,37,1536]{2,1,0:T(8,128)(2,1)S(1)}, bf16[4,37,1536]{2,1,0:T(8,128)(2,1)S(1)}, u32[]{:S(2)}, u32[]{:S(2)}) collective-permute-start(bf16[4,37,1536]{2,1,0:T(8,128)(2,1)S(1)} %get-tuple-element.28), channel_id=1, source_target_pairs={{0,12},{4,16},{8,20},{12,24},{16,28},{20,0},{24,4},{28,8},{1,13},{... | collective-permute-start | bytes 1363976 | tf_op jit(solution)/shard_map/ppermute | solution.py:30
  261.0 25.2 %collective-permute-start.32 = (bf16[4,37,1536]{2,1,0:T(8,128)(2,1)S(1)}, bf16[4,37,1536]{2,1,0:T(8,128)(2,1)S(1)}, u32[]{:S(2)}, u32[]{:S(2)}) collective-permute-start(bf16[4,37,1536]{2,1,0:T(8,128)(2,1)S(1)} %get-tuple-element.29), channel_id=1, source_target_pairs={{0,4},{4,8},{8,12},{12,16},{16,20},{20,24},{24,28},{28,0},{1,5},{5... | collective-permute-start | bytes 1363976 | tf_op jit(solution)/shard_map/ppermute | solution.py:30
  286.2 3.8 %collective-permute-done.26 = bf16[4,37,1536]{2,1,0:T(8,128)(2,1)S(1)} collective-permute-done((bf16[4,37,1536]{2,1,0:T(8,128)(2,1)S(1)}, bf16[4,37,1536]{2,1,0:T(8,128)(2,1)S(1)}, u32[]{:S(2)}, u32[]{:S(2)}) %collective-permute-start.26) | collective-permute-done | bytes 454688 | tf_op jit(solution)/shard_map/ppermute | solution.py:30
  293.8 5.9 %collective-permute-done.29 = bf16[4,37,1536]{2,1,0:T(8,128)(2,1)S(1)} collective-permute-done((bf16[4,37,1536]{2,1,0:T(8,128)(2,1)S(1)}, bf16[4,37,1536]{2,1,0:T(8,128)(2,1)S(1)}, u32[]{:S(2)}, u32[]{:S(2)}) %collective-permute-start.29) | collective-permute-done | bytes 454688 | tf_op jit(solution)/shard_map/ppermute | solution.py:29
  304.6 7.3 %collective-permute-start.34 = (bf16[4,1,16,16]{3,2,1,0:T(8,128)(2,1)S(1)}, bf16[4,1,16,16]{3,2,1,0:T(8,128)(2,1)S(1)}, u32[]{:S(2)}, u32[]{:S(2)}) collective-permute-start(bf16[4,1,16,16]{3,2,1,0:T(8,128)(2,1)S(1)} %get-tuple-element.66), channel_id=1, source_target_pairs={{0,4},{4,8},{8,12},{12,16},{16,20},{20,24},{24,28},{1,5},{5,9},{9,... | collective-permute-start | bytes 6152 | tf_op jit(solution)/shard_map/ppermute | solution.py:39
  311.9 6.2 %collective-permute-start.36 = (bf16[4,8,1,16]{3,2,1,0:T(2,128)(2,1)S(1)}, bf16[4,8,1,16]{3,2,1,0:T(2,128)(2,1)S(1)}, u32[]{:S(2)}, u32[]{:S(2)}) collective-permute-start(bf16[4,8,1,16]{3,2,1,0:T(2,128)(2,1)S(1)} %get-tuple-element.68), channel_id=1, source_target_pairs={{0,1},{1,2},{2,3},{4,5},{5,6},{6,7},{8,9},{9,10},{10,11},{12,13},{... | collective-permute-start | bytes 3080 | tf_op jit(solution)/shard_map/ppermute | solution.py:39
  320.0 3.6 %collective-permute-start.33 = (bf16[4,1,1,16]{3,2,1,0:T(2,128)(2,1)S(1)}, bf16[4,1,1,16]{3,2,1,0:T(2,128)(2,1)S(1)}, u32[]{:S(2)}, u32[]{:S(2)}) collective-permute-start(bf16[4,1,1,16]{3,2,1,0:T(2,128)(2,1)S(1)} %get-tuple-element.62), channel_id=1, source_target_pairs={{0,5},{1,6},{2,7},{4,9},{5,10},{6,11},{8,13},{9,14},{10,15},{12,17... | collective-permute-start | bytes 392 | tf_op jit(solution)/shard_map/ppermute | solution.py:48
  323.7 4.5 %collective-permute-start.35 = (bf16[4,1,1,16]{3,2,1,0:T(2,128)(2,1)S(1)}, bf16[4,1,1,16]{3,2,1,0:T(2,128)(2,1)S(1)}, u32[]{:S(2)}, u32[]{:S(2)}) collective-permute-start(bf16[4,1,1,16]{3,2,1,0:T(2,128)(2,1)S(1)} %get-tuple-element.65), channel_id=1, source_target_pairs={{1,4},{2,5},{3,6},{5,8},{6,9},{7,10},{9,12},{10,13},{11,14},{13,16... | collective-permute-start | bytes 392 | tf_op jit(solution)/shard_map/ppermute | solution.py:48
  331.8 3.8 %collective-permute-done.38 = bf16[4,1,1,16]{3,2,1,0:T(2,128)(2,1)S(1)} collective-permute-done((bf16[4,1,1,16]{3,2,1,0:T(2,128)(2,1)S(1)}, bf16[4,1,1,16]{3,2,1,0:T(2,128)(2,1)S(1)}, u32[]{:S(2)}, u32[]{:S(2)}) %collective-permute-start.38) | collective-permute-done | bytes 160 | tf_op jit(solution)/shard_map/ppermute | solution.py:48
  337.8 3.9 %collective-permute-done.40 = bf16[4,1,1,16]{3,2,1,0:T(2,128)(2,1)S(1)} collective-permute-done((bf16[4,1,1,16]{3,2,1,0:T(2,128)(2,1)S(1)}, bf16[4,1,1,16]{3,2,1,0:T(2,128)(2,1)S(1)}, u32[]{:S(2)}, u32[]{:S(2)}) %collective-permute-start.40) | collective-permute-done | bytes 160 | tf_op jit(solution)/shard_map/ppermute | solution.py:48
  (287 shorter events, 113.9 us)
Async XLA Ops:
  4.0 24.8 %collective-permute-start = (bf16[4,37,1536]{2,1,0:T(8,128)(2,1)}, bf16[4,37,1536]{2,1,0:T(8,128)(2,1)}, u32[]{:S(2)}, u32[]{:S(2)}) collective-permute-start(bf16[4,37,1536]{2,1,0:T(8,128)(2,1)} %get-tuple-element.47), channel_id=1, source_target_pairs={{0,4},{4,8},{8,12},{12,16},{16,20},{20,24},{24,28},{28,0},{1,5},{5... | collective-permute-start | bytes 1363976 | tf_op jit(solution)/shard_map/ppermute | solution.py:30
  7.6 40.2 %collective-permute-start.1 = (bf16[4,37,1536]{2,1,0:T(8,128)(2,1)}, bf16[4,37,1536]{2,1,0:T(8,128)(2,1)}, u32[]{:S(2)}, u32[]{:S(2)}) collective-permute-start(bf16[4,37,1536]{2,1,0:T(8,128)(2,1)} %get-tuple-element.47), channel_id=1, source_target_pairs={{0,8},{4,12},{8,16},{12,20},{16,24},{20,28},{24,0},{28,4},{1,9},{5... | collective-permute-start | bytes 1363976 | tf_op jit(solution)/shard_map/ppermute | solution.py:30
  9.2 39.7 %collective-permute-start.2 = (bf16[4,37,1536]{2,1,0:T(8,128)(2,1)}, bf16[4,37,1536]{2,1,0:T(8,128)(2,1)}, u32[]{:S(2)}, u32[]{:S(2)}) collective-permute-start(bf16[4,37,1536]{2,1,0:T(8,128)(2,1)} %get-tuple-element.47), channel_id=1, source_target_pairs={{0,12},{4,16},{8,20},{12,24},{16,28},{20,0},{24,4},{28,8},{1,13},{... | collective-permute-start | bytes 1363976 | tf_op jit(solution)/shard_map/ppermute | solution.py:30
  11.9 32.1 %collective-permute-start.3 = (bf16[4,37,1536]{2,1,0:T(8,128)(2,1)}, bf16[4,37,1536]{2,1,0:T(8,128)(2,1)}, u32[]{:S(2)}, u32[]{:S(2)}) collective-permute-start(bf16[4,37,1536]{2,1,0:T(8,128)(2,1)} %get-tuple-element.47), channel_id=1, source_target_pairs={{0,24},{4,28},{8,0},{12,4},{16,8},{20,12},{24,16},{28,20},{1,25},{... | collective-permute-start | bytes 1363976 | tf_op jit(solution)/shard_map/ppermute | solution.py:29
  13.2 41.6 %collective-permute-start.5 = (bf16[4,37,1536]{2,1,0:T(8,128)(2,1)}, bf16[4,37,1536]{2,1,0:T(8,128)(2,1)}, u32[]{:S(2)}, u32[]{:S(2)}) collective-permute-start(bf16[4,37,1536]{2,1,0:T(8,128)(2,1)} %get-tuple-element.47), channel_id=1, source_target_pairs={{0,20},{4,24},{8,28},{12,0},{16,4},{20,8},{24,12},{28,16},{1,21},{... | collective-permute-start | bytes 1363976 | tf_op jit(solution)/shard_map/ppermute | solution.py:30
  28.8 28.2 %collective-permute-start.6 = (bf16[4,37,1536]{2,1,0:T(8,128)(2,1)}, bf16[4,37,1536]{2,1,0:T(8,128)(2,1)S(1)}, u32[]{:S(2)}, u32[]{:S(2)}) collective-permute-start(bf16[4,37,1536]{2,1,0:T(8,128)(2,1)} %get-tuple-element.47), channel_id=1, source_target_pairs={{0,28},{4,0},{8,4},{12,8},{16,12},{20,16},{24,20},{28,24},{1,29},{... | collective-permute-start | bytes 1363976 | tf_op jit(solution)/shard_map/ppermute | solution.py:30
  69.0 18.1 %collective-permute-start.8 = (bf16[1184,384]{1,0:T(8,128)(2,1)}, bf16[1184,384]{1,0:T(8,128)(2,1)S(1)}, u32[]{:S(2)}, u32[]{:S(2)}) collective-permute-start(bf16[1184,384]{1,0:T(8,128)(2,1)} %reshape.319.refs_0_), channel_id=1, source_target_pairs={{0,2},{1,3},{2,0},{3,1},{4,6},{5,7},{6,4},{7,5},{8,10},{9,11},{10,... | collective-permute-start | bytes 2727944 | tf_op jit(solution)/shard_map/ppermute | solution.py:236
  74.7 26.0 %collective-permute-start.7 = (bf16[1184,384]{1,0:T(8,128)(2,1)S(1)}, bf16[1184,384]{1,0:T(8,128)(2,1)S(1)}, u32[]{:S(2)}, u32[]{:S(2)}) collective-permute-start(bf16[1184,384]{1,0:T(8,128)(2,1)S(1)} %copy-done.5), channel_id=1, source_target_pairs={{0,1},{1,0},{2,3},{3,2},{4,5},{5,4},{6,7},{7,6},{8,9},{9,8},{10,11... | collective-permute-start | bytes 2727944 | tf_op jit(solution)/shard_map/ppermute | solution.py:239
  87.1 14.4 %collective-permute-start.9 = (bf16[1184,384]{1,0:T(8,128)(2,1)S(1)}, bf16[1184,384]{1,0:T(8,128)(2,1)}, u32[]{:S(2)}, u32[]{:S(2)}) collective-permute-start(bf16[1184,384]{1,0:T(8,128)(2,1)S(1)} %collective-permute-done.8.refs_2_), channel_id=1, source_target_pairs={{0,1},{1,0},{2,3},{3,2},{4,5},{5,4},{6,7},{7,6},{8,9},{9,8},{10,11... | collective-permute-start | bytes 2727944 | tf_op jit(solution)/shard_map/ppermute | solution.py:241
  120.5 17.8 %collective-permute-start.13 = (bf16[4,37,1536]{2,1,0:T(8,128)(2,1)S(1)}, bf16[4,37,1536]{2,1,0:T(8,128)(2,1)S(1)}, u32[]{:S(2)}, u32[]{:S(2)}) collective-permute-start(bf16[4,37,1536]{2,1,0:T(8,128)(2,1)S(1)} %get-tuple-element.34), channel_id=1, source_target_pairs={{0,24},{4,28},{8,0},{12,4},{16,8},{20,12},{24,16},{28,20},{1,25},{... | collective-permute-start | bytes 1363976 | tf_op jit(solution)/shard_map/ppermute | solution.py:29
  123.9 21.4 %collective-permute-start.10 = (bf16[4,37,1536]{2,1,0:T(8,128)(2,1)S(1)}, bf16[4,37,1536]{2,1,0:T(8,128)(2,1)S(1)}, u32[]{:S(2)}, u32[]{:S(2)}) collective-permute-start(bf16[4,37,1536]{2,1,0:T(8,128)(2,1)S(1)} %get-tuple-element.31), channel_id=1, source_target_pairs={{0,28},{4,0},{8,4},{12,8},{16,12},{20,16},{24,20},{28,24},{1,29},{... | collective-permute-start | bytes 1363976 | tf_op jit(solution)/shard_map/ppermute | solution.py:30
  134.1 33.2 %collective-permute-start.11 = (bf16[4,37,1536]{2,1,0:T(8,128)(2,1)S(1)}, bf16[4,37,1536]{2,1,0:T(8,128)(2,1)S(1)}, u32[]{:S(2)}, u32[]{:S(2)}) collective-permute-start(bf16[4,37,1536]{2,1,0:T(8,128)(2,1)S(1)} %get-tuple-element.32), channel_id=1, source_target_pairs={{0,24},{4,28},{8,0},{12,4},{16,8},{20,12},{24,16},{28,20},{1,25},{... | collective-permute-start | bytes 1363976 | tf_op jit(solution)/shard_map/ppermute | solution.py:30
  134.1 35.1 %collective-permute-start.12 = (bf16[4,37,1536]{2,1,0:T(8,128)(2,1)S(1)}, bf16[4,37,1536]{2,1,0:T(8,128)(2,1)S(1)}, u32[]{:S(2)}, u32[]{:S(2)}) collective-permute-start(bf16[4,37,1536]{2,1,0:T(8,128)(2,1)S(1)} %get-tuple-element.33), channel_id=1, source_target_pairs={{0,20},{4,24},{8,28},{12,0},{16,4},{20,8},{24,12},{28,16},{1,21},{... | collective-permute-start | bytes 1363976 | tf_op jit(solution)/shard_map/ppermute | solution.py:30
  134.5 34.7 %collective-permute-start.15 = (bf16[4,37,1536]{2,1,0:T(8,128)(2,1)S(1)}, bf16[4,37,1536]{2,1,0:T(8,128)(2,1)S(1)}, u32[]{:S(2)}, u32[]{:S(2)}) collective-permute-start(bf16[4,37,1536]{2,1,0:T(8,128)(2,1)S(1)} %get-tuple-element.35), channel_id=1, source_target_pairs={{0,12},{4,16},{8,20},{12,24},{16,28},{20,0},{24,4},{28,8},{1,13},{... | collective-permute-start | bytes 1363976 | tf_op jit(solution)/shard_map/ppermute | solution.py:30
  138.3 30.9 %collective-permute-start.16 = (bf16[4,37,1536]{2,1,0:T(8,128)(2,1)S(1)}, bf16[4,37,1536]{2,1,0:T(8,128)(2,1)S(1)}, u32[]{:S(2)}, u32[]{:S(2)}) collective-permute-start(bf16[4,37,1536]{2,1,0:T(8,128)(2,1)S(1)} %get-tuple-element.37), channel_id=1, source_target_pairs={{0,8},{4,12},{8,16},{12,20},{16,24},{20,28},{24,0},{28,4},{1,9},{5... | collective-permute-start | bytes 1363976 | tf_op jit(solution)/shard_map/ppermute | solution.py:30
  145.3 33.1 %collective-permute-start.17 = (bf16[4,37,1536]{2,1,0:T(8,128)(2,1)S(1)}, bf16[4,37,1536]{2,1,0:T(8,128)(2,1)S(1)}, u32[]{:S(2)}, u32[]{:S(2)}) collective-permute-start(bf16[4,37,1536]{2,1,0:T(8,128)(2,1)S(1)} %get-tuple-element.36), channel_id=1, source_target_pairs={{0,4},{4,8},{8,12},{12,16},{16,20},{20,24},{24,28},{28,0},{1,5},{5... | collective-permute-start | bytes 1363976 | tf_op jit(solution)/shard_map/ppermute | solution.py:30
  167.3 11.2 %collective-permute-start.14 = (bf16[4,37,1536]{2,1,0:T(8,128)(2,1)S(1)}, bf16[4,37,1536]{2,1,0:T(8,128)(2,1)S(1)}, u32[]{:S(2)}, u32[]{:S(2)}) collective-permute-start(bf16[4,37,1536]{2,1,0:T(8,128)(2,1)S(1)} %collective-permute-done.13), channel_id=1, source_target_pairs={{0,24},{4,28},{8,0},{12,4},{16,8},{20,12},{24,16},{28,20},{1,25},{... | collective-permute-start | bytes 1363976 | tf_op jit(solution)/shard_map/ppermute | solution.py:29
  180.5 23.3 %collective-permute-start.18 = (bf16[4,37,1536]{2,1,0:T(8,128)(2,1)S(1)}, bf16[4,37,1536]{2,1,0:T(8,128)(2,1)S(1)}, u32[]{:S(2)}, u32[]{:S(2)}) collective-permute-start(bf16[4,37,1536]{2,1,0:T(8,128)(2,1)S(1)} %pad_maximum_fusion.5), channel_id=1, source_target_pairs={{0,4},{4,8},{8,12},{12,16},{16,20},{20,24},{24,28},{28,0},{1,5},{5... | collective-permute-start | bytes 1363976 | tf_op jit(solution)/shard_map/ppermute | solution.py:30
  191.0 30.6 %collective-permute-start.21 = (bf16[4,37,1536]{2,1,0:T(8,128)(2,1)S(1)}, bf16[4,37,1536]{2,1,0:T(8,128)(2,1)S(1)}, u32[]{:S(2)}, u32[]{:S(2)}) collective-permute-start(bf16[4,37,1536]{2,1,0:T(8,128)(2,1)S(1)} %pad_maximum_fusion.5), channel_id=1, source_target_pairs={{0,24},{4,28},{8,0},{12,4},{16,8},{20,12},{24,16},{28,20},{1,25},{... | collective-permute-start | bytes 1363976 | tf_op jit(solution)/shard_map/ppermute | solution.py:29
  194.4 32.5 %collective-permute-start.19 = (bf16[4,37,1536]{2,1,0:T(8,128)(2,1)S(1)}, bf16[4,37,1536]{2,1,0:T(8,128)(2,1)S(1)}, u32[]{:S(2)}, u32[]{:S(2)}) collective-permute-start(bf16[4,37,1536]{2,1,0:T(8,128)(2,1)S(1)} %pad_maximum_fusion.5), channel_id=1, source_target_pairs={{0,8},{4,12},{8,16},{12,20},{16,24},{20,28},{24,0},{28,4},{1,9},{5... | collective-permute-start | bytes 1363976 | tf_op jit(solution)/shard_map/ppermute | solution.py:30
  194.4 32.5 %collective-permute-start.20 = (bf16[4,37,1536]{2,1,0:T(8,128)(2,1)S(1)}, bf16[4,37,1536]{2,1,0:T(8,128)(2,1)S(1)}, u32[]{:S(2)}, u32[]{:S(2)}) collective-permute-start(bf16[4,37,1536]{2,1,0:T(8,128)(2,1)S(1)} %pad_maximum_fusion.5), channel_id=1, source_target_pairs={{0,12},{4,16},{8,20},{12,24},{16,28},{20,0},{24,4},{28,8},{1,13},{... | collective-permute-start | bytes 1363976 | tf_op jit(solution)/shard_map/ppermute | solution.py:30
  194.4 37.4 %collective-permute-start.23 = (bf16[4,37,1536]{2,1,0:T(8,128)(2,1)S(1)}, bf16[4,37,1536]{2,1,0:T(8,128)(2,1)S(1)}, u32[]{:S(2)}, u32[]{:S(2)}) collective-permute-start(bf16[4,37,1536]{2,1,0:T(8,128)(2,1)S(1)} %pad_maximum_fusion.5), channel_id=1, source_target_pairs={{0,20},{4,24},{8,28},{12,0},{16,4},{20,8},{24,12},{28,16},{1,21},{... | collective-permute-start | bytes 1363976 | tf_op jit(solution)/shard_map/ppermute | solution.py:30
  203.8 28.2 %collective-permute-start.24 = (bf16[4,37,1536]{2,1,0:T(8,128)(2,1)S(1)}, bf16[4,37,1536]{2,1,0:T(8,128)(2,1)S(1)}, u32[]{:S(2)}, u32[]{:S(2)}) collective-permute-start(bf16[4,37,1536]{2,1,0:T(8,128)(2,1)S(1)} %pad_maximum_fusion.5), channel_id=1, source_target_pairs={{0,28},{4,0},{8,4},{12,8},{16,12},{20,16},{24,20},{28,24},{1,29},{... | collective-permute-start | bytes 1363976 | tf_op jit(solution)/shard_map/ppermute | solution.py:30
  247.7 12.4 %collective-permute-start.28 = (bf16[4,37,1536]{2,1,0:T(8,128)(2,1)S(1)}, bf16[4,37,1536]{2,1,0:T(8,128)(2,1)S(1)}, u32[]{:S(2)}, u32[]{:S(2)}) collective-permute-start(bf16[4,37,1536]{2,1,0:T(8,128)(2,1)S(1)} %get-tuple-element.27), channel_id=1, source_target_pairs={{0,24},{4,28},{8,0},{12,4},{16,8},{20,12},{24,16},{28,20},{1,25},{... | collective-permute-start | bytes 1363976 | tf_op jit(solution)/shard_map/ppermute | solution.py:29
  254.8 35.2 %collective-permute-start.26 = (bf16[4,37,1536]{2,1,0:T(8,128)(2,1)S(1)}, bf16[4,37,1536]{2,1,0:T(8,128)(2,1)S(1)}, u32[]{:S(2)}, u32[]{:S(2)}) collective-permute-start(bf16[4,37,1536]{2,1,0:T(8,128)(2,1)S(1)} %get-tuple-element.25), channel_id=1, source_target_pairs={{0,24},{4,28},{8,0},{12,4},{16,8},{20,12},{24,16},{28,20},{1,25},{... | collective-permute-start | bytes 1363976 | tf_op jit(solution)/shard_map/ppermute | solution.py:30
  256.2 35.1 %collective-permute-start.27 = (bf16[4,37,1536]{2,1,0:T(8,128)(2,1)S(1)}, bf16[4,37,1536]{2,1,0:T(8,128)(2,1)S(1)}, u32[]{:S(2)}, u32[]{:S(2)}) collective-permute-start(bf16[4,37,1536]{2,1,0:T(8,128)(2,1)S(1)} %get-tuple-element.26), channel_id=1, source_target_pairs={{0,20},{4,24},{8,28},{12,0},{16,4},{20,8},{24,12},{28,16},{1,21},{... | collective-permute-start | bytes 1363976 | tf_op jit(solution)/shard_map/ppermute | solution.py:30
  256.3 35.0 %collective-permute-start.30 = (bf16[4,37,1536]{2,1,0:T(8,128)(2,1)S(1)}, bf16[4,37,1536]{2,1,0:T(8,128)(2,1)S(1)}, u32[]{:S(2)}, u32[]{:S(2)}) collective-permute-start(bf16[4,37,1536]{2,1,0:T(8,128)(2,1)S(1)} %get-tuple-element.28), channel_id=1, source_target_pairs={{0,12},{4,16},{8,20},{12,24},{16,28},{20,0},{24,4},{28,8},{1,13},{... | collective-permute-start | bytes 1363976 | tf_op jit(solution)/shard_map/ppermute | solution.py:30
  260.2 31.2 %collective-permute-start.31 = (bf16[4,37,1536]{2,1,0:T(8,128)(2,1)S(1)}, bf16[4,37,1536]{2,1,0:T(8,128)(2,1)S(1)}, u32[]{:S(2)}, u32[]{:S(2)}) collective-permute-start(bf16[4,37,1536]{2,1,0:T(8,128)(2,1)S(1)} %get-tuple-element.30), channel_id=1, source_target_pairs={{0,8},{4,12},{8,16},{12,20},{16,24},{20,28},{24,0},{28,4},{1,9},{5... | collective-permute-start | bytes 1363976 | tf_op jit(solution)/shard_map/ppermute | solution.py:30
  261.0 32.7 %collective-permute-start.32 = (bf16[4,37,1536]{2,1,0:T(8,128)(2,1)S(1)}, bf16[4,37,1536]{2,1,0:T(8,128)(2,1)S(1)}, u32[]{:S(2)}, u32[]{:S(2)}) collective-permute-start(bf16[4,37,1536]{2,1,0:T(8,128)(2,1)S(1)} %get-tuple-element.29), channel_id=1, source_target_pairs={{0,4},{4,8},{8,12},{12,16},{16,20},{20,24},{24,28},{28,0},{1,5},{5... | collective-permute-start | bytes 1363976 | tf_op jit(solution)/shard_map/ppermute | solution.py:30
  304.6 37.1 %collective-permute-start.34 = (bf16[4,1,16,16]{3,2,1,0:T(8,128)(2,1)S(1)}, bf16[4,1,16,16]{3,2,1,0:T(8,128)(2,1)S(1)}, u32[]{:S(2)}, u32[]{:S(2)}) collective-permute-start(bf16[4,1,16,16]{3,2,1,0:T(8,128)(2,1)S(1)} %get-tuple-element.66), channel_id=1, source_target_pairs={{0,4},{4,8},{8,12},{12,16},{16,20},{20,24},{24,28},{1,5},{5,9},{9,... | collective-permute-start | bytes 6152 | tf_op jit(solution)/shard_map/ppermute | solution.py:39
  311.9 29.8 %collective-permute-start.36 = (bf16[4,8,1,16]{3,2,1,0:T(2,128)(2,1)S(1)}, bf16[4,8,1,16]{3,2,1,0:T(2,128)(2,1)S(1)}, u32[]{:S(2)}, u32[]{:S(2)}) collective-permute-start(bf16[4,8,1,16]{3,2,1,0:T(2,128)(2,1)S(1)} %get-tuple-element.68), channel_id=1, source_target_pairs={{0,1},{1,2},{2,3},{4,5},{5,6},{6,7},{8,9},{9,10},{10,11},{12,13},{... | collective-permute-start | bytes 3080 | tf_op jit(solution)/shard_map/ppermute | solution.py:39
  318.1 23.5 %collective-permute-start.37 = (bf16[4,8,1,16]{3,2,1,0:T(2,128)(2,1)S(1)}, bf16[4,8,1,16]{3,2,1,0:T(2,128)(2,1)S(1)}, u32[]{:S(2)}, u32[]{:S(2)}) collective-permute-start(bf16[4,8,1,16]{3,2,1,0:T(2,128)(2,1)S(1)} %get-tuple-element.69), channel_id=1, source_target_pairs={{1,0},{2,1},{3,2},{5,4},{6,5},{7,6},{9,8},{10,9},{11,10},{13,12},{... | collective-permute-start | bytes 3080 | tf_op jit(solution)/shard_map/ppermute | solution.py:39
  (63 other events, 910.6 us)
